TPU v7x, 32 devices: a whole 2x2x4 slice. The times are simulated.
32 devices in a mesh: region: 8 (over z, y), route: 4 (over x, core).
Axes of the slice: x: 2, y: 2, z: 4, core: 2. Of those that a mesh axis runs over, the one named last changes fastest.
Arguments:
- fill: float32 [4, 98304], P(None, ('region', 'route')), may hold values from 0 to 1
- capacity: float32 [98304], P(('region', 'route')), may hold values from 0.2 to 1
- free_time: float32 [98304], P(('region', 'route')), may hold values from 0.5 to 3
- split_share: float32 [2, 98304], P(None, ('region', 'route')), may hold values from 0.05 to 0.45
- upstream_offset: int32 [2, 98304], P(None, ('region', 'route')), may hold values from -32 to 32
- path_flow: float32 [262144], P(('region', 'route')), may hold values from 0.01 to 0.1
- anchor: int32 [262144], P(('region', 'route')), may hold values from 0 to 12287
- depart: int32 [262144], P(('region', 'route')), may hold values from 0 to 11
- od_pair: int32 [32, 8192], P(('region', 'route')), may hold values from 0 to 2047, never falling along the last dimension, each value on 1 to 8 neighbouring positions
- swap_rate: int32 [32, 2048], P(('region', 'route')), may hold values from 1 to 8
- tile_index: int32 [2048, 4], P(('region', 'route')), may hold values from 0 to 767, as said below
- incidence: bfloat16 [2048, 4, 128, 128], P(('region', 'route')), may hold values from 0 to 1, as said below
Outputs:
- density: float32 [4, 98304], P(None, ('region', 'route'))
- path_cost: float32 [262144], P(('region', 'route'))
- new_flow: float32 [262144], P(('region', 'route'))
Inputs may be any that keep to these rules, and one draw needn't show every extreme that they name: `tile_index`: each device's path tiles name, with repeats, at most 16 link tiles held by any one device, and in every draw each device names exactly 16 tiles of some device. `incidence`: the first touched tile of every path tile gives each of its paths a share of at least 0.2 on one link; all shares are 0 or at least 0.2.
All inputs are finite; a program needn't handle non-finite values.
Results may differ from a plain program's by a relative error of at most 0.00034.
Values may be sent and summed in bfloat16 or wider, within the bound.
No kernel may reach another device: no remote copies, remote signals or barrier semaphores. Data moves between devices by JAX's collectives and lax.ppermute only.
A program may use at most 128 MiB of HBM per device.

v0:
```python
import jax
import jax.numpy as jnp
from jax import lax
from jax.sharding import PartitionSpec as P

NC = 4
BND = 32
ISTEPS = 5
NI = 12
OD_MOST = 8


def padded_2(cells, sides, width):
    for axis, dim in sides:
        count = lax.axis_size(axis)
        head = lax.slice_in_dim(cells, 0, width, axis=dim)
        tail = lax.slice_in_dim(cells, cells.shape[dim] - width, cells.shape[dim], axis=dim)
        cells = jnp.concatenate(
            [
                lax.ppermute(tail, axis, [(i, (i + 1) % count) for i in range(count)]),
                cells,
                lax.ppermute(head, axis, [((i + 1) % count, i) for i in range(count)]),
            ],
            axis=dim,
        )
    return cells


def sweep(state, capacity):
    rho = state[:NC]
    queue = state[NC]
    jam = 4.0 * capacity
    send = jnp.minimum(rho, capacity)
    recv = jnp.minimum(capacity, 0.5 * (jam - rho))
    inner = jnp.minimum(send[:-1], recv[1:])
    outflow = send[NC - 1]
    return (rho, queue, recv, inner, outflow)


def finish(rho, queue, recv, inner, outflow, arriving):
    waiting = queue + arriving
    entering = jnp.minimum(waiting, recv[0])
    queue = waiting - entering
    into = jnp.concatenate([entering[None], inner], 0)
    leaving = jnp.concatenate([inner, outflow[None]], 0)
    rho = rho + into - leaving
    return jnp.concatenate([rho, queue[None]], 0)


def occupy(state, capacity):
    return (jnp.sum(state[:NC], 0) + state[NC]) / capacity


def band_weights(split, offsets):
    reach = jnp.arange(-BND, BND + 1, dtype=jnp.int32)[:, None]
    first_hit = (offsets[0][None, :] == reach).astype(jnp.float32)
    second_hit = (offsets[1][None, :] == reach).astype(jnp.float32)
    return split[0][None, :] * first_hit + split[1][None, :] * second_hit


def band_inflow(weights, padded, count):
    total = jnp.zeros((count,), jnp.float32)
    for shift in range(2 * BND + 1):
        total = total + weights[shift] * padded[shift : shift + count]
    return total


def group_min(cost, group):
    reach = OD_MOST - 1
    count = cost.shape[0]
    padded_cost = jnp.pad(cost, reach, constant_values=1e30)
    padded_group = jnp.pad(group, reach, constant_values=-1)
    best = cost
    for shift in range(2 * reach + 1):
        near_cost = padded_cost[shift : shift + count]
        near_group = padded_group[shift : shift + count]
        best = jnp.minimum(best, jnp.where(near_group == group, near_cost, best))
    return best


def group_sum(values, group):
    reach = OD_MOST - 1
    count = values.shape[0]
    padded_values = jnp.pad(values, reach)
    padded_group = jnp.pad(group, reach, constant_values=-1)
    total = jnp.zeros_like(values)
    for shift in range(2 * reach + 1):
        near_values = padded_values[shift : shift + count]
        near_group = padded_group[shift : shift + count]
        total = total + jnp.where(near_group == group, near_values, 0.0)
    return total


def swap_flows(cost, flow, group, rate_num):
    best = group_min(cost, group)
    pairs = jnp.arange(rate_num.shape[0], dtype=jnp.int32)
    picker = (group[:, None] == pairs[None, :]).astype(jnp.bfloat16)
    rate = (
        jnp.dot(picker, rate_num.astype(jnp.bfloat16)[:, None], preferred_element_type=jnp.float32)[
            :, 0
        ]
        / 16.0
    )
    moved = rate * flow * (cost - best) / cost
    pull = (best / cost) ** 4
    return flow - moved + group_sum(moved, group) * pull / group_sum(pull, group)


def select_depart(totals, depart_tile):
    levels = jnp.arange(totals.shape[1], dtype=jnp.int32)
    chosen = jnp.where(levels[None, :, None] == depart_tile[:, None, :], totals, 0.0)
    return jnp.sum(chosen, 1)


def body(
    fill,
    capacity,
    free_time,
    split_share,
    upstream_offset,
    path_flow,
    anchor,
    depart,
    od_pair,
    swap_rate,
    tile_index,
    incidence,
):
    span = fill.shape[1]
    region_links = span * lax.axis_size("route")
    link_tiles = jnp.arange(region_links // 128, dtype=jnp.int32)
    lanes = jnp.arange(128, dtype=jnp.int32)
    tile_pick = jnp.where((anchor // 128)[None, :] == link_tiles[:, None], path_flow[None, :], 0.0)
    lane_pick = ((anchor % 128)[:, None] == lanes[None, :]).astype(jnp.float32)
    local_entry = jnp.dot(
        tile_pick, lane_pick, precision=lax.Precision.HIGHEST, preferred_element_type=jnp.float32
    ).reshape(-1)
    entry = lax.psum_scatter(local_entry, "route", scatter_dimension=0, tiled=True)
    state = jnp.concatenate([fill * (4.0 * capacity), jnp.zeros((1, span), jnp.float32)], 0)
    costs = jnp.zeros((NI, span), jnp.float32)
    width = ISTEPS * BND
    extent = span + 2 * width
    constants = jnp.concatenate(
        [capacity[None], split_share, entry[None], upstream_offset.astype(jnp.float32)], 0
    )
    wide_consts = padded_2(constants, ((("region", "route"), 1),), width)
    wide_capacity = wide_consts[0]
    wide_entry = wide_consts[3]
    wide_weights = band_weights(wide_consts[1:3], wide_consts[4:6].astype(jnp.int32))

    def one_interval(index, carry):
        current, table = carry
        wide_state = padded_2(current, ((("region", "route"), 1),), width)

        def one_step(step, inner_carry):
            wide_now, occupancy = inner_carry
            rho, queue, recv, inner, outflow = sweep(wide_now, wide_capacity)
            padded = jnp.pad(outflow, (BND, BND))
            arriving = wide_entry + band_inflow(wide_weights, padded, extent)
            wide_now = finish(rho, queue, recv, inner, outflow, arriving)
            return (wide_now, occupancy + occupy(wide_now[:, width : width + span], capacity))

        wide_state, occupancy = lax.fori_loop(
            0, ISTEPS, one_step, (wide_state, jnp.zeros((span,), jnp.float32))
        )
        table = lax.dynamic_update_slice_in_dim(
            table, (free_time + occupancy / ISTEPS)[None], index, 0
        )
        return (wide_state[:, width : width + span], table)

    state, costs = lax.fori_loop(0, NI, one_interval, (state, costs))
    link_cost = costs.astype(jnp.bfloat16)
    tiles = link_cost.reshape(NI, span // 128, 128).transpose(1, 0, 2)
    wanted_tiles = tile_index.reshape(-1)
    every_tile = lax.all_gather(tiles, ("region", "route"), axis=0, tiled=True)
    fetched = every_tile[wanted_tiles]
    fetched = fetched.reshape(tile_index.shape[0], tile_index.shape[1], NI, 128)
    totals = jnp.einsum("ptil,ptlq->piq", fetched, incidence, preferred_element_type=jnp.float32)
    path_cost = select_depart(totals, depart.reshape(-1, 128)).reshape(-1) / 256.0
    new_flow = swap_flows(path_cost, path_flow, od_pair[0], swap_rate[0])
    return (state[:NC], path_cost, new_flow)


def solution(mesh):
    return jax.shard_map(
        body,
        mesh=mesh,
        in_specs=(
            P(None, ("region", "route")),
            P(("region", "route")),
            P(("region", "route")),
            P(None, ("region", "route")),
            P(None, ("region", "route")),
            P(("region", "route")),
            P(("region", "route")),
            P(("region", "route")),
            P(("region", "route"), None),
            P(("region", "route"), None),
            P(("region", "route"), None),
            P(("region", "route"), None, None, None),
        ),
        out_specs=(P(None, ("region", "route")), P(("region", "route")), P(("region", "route"))),
        check_vma=False,
    )
```

profile of v0, /device:TPU:0, one launch (start us, length us, event | category | flops | bytes accessed | tf_op | source)
XLA Modules:
  0.0 403.9 jit_solution(23618724560000549)
XLA Ops:
  8.0 0.8 add_select_fusion.1
  8.8 3.3 fusion.22
  12.1 13.2 %all-reduce.6 = f32[12288]{0:T(1024)S(1)} all-reduce(f32[12288]{0:T(1024)S(1)} %fusion.22), channel_id=2, replica_groups=mesh['region'=8,'route'=4] {'route'}, use_global_device_ids=true, to_apply=%region_0.1.clone | all-reduce | flops 12288 | bytes 98304
  26.8 5.3 %collective-permute-start.3 = (f32[6,160]{1,0:T(8,128)S(1)}, f32[6,160]{1,0:T(8,128)S(1)}, u32[]{:S(2)}, u32[]{:S(2)}) collective-permute-start(f32[6,160]{1,0:T(8,128)S(1)} %get-tuple-element.553), channel_id=1, source_target_pairs={{1,0},{2,1},{3,2},{4,3},{5,4},{6,5},{7,6},{8,7},{9,8},{10,9},{11,1... | collective-permute-start | bytes 11528 | tf_op jit(solution)/shard_map/ppermute | solution.py:22
  32.2 1.3 collective-permute-done.2
  33.9 292.1 %while.61 = (s32[]{:T(128)}, f32[5,3072]{1,0:T(8,128)S(1)}, bf16[12,3072]{1,0:T(8,128)(2,1)S(1)}, f32[1,3392]{1,0:T(1,128)S(1)}, f32[3392]{0:T(1024)S(1)}, /*ind...) while((s32[]{:T(128)}, f32[5,3072]{1,0:T(8,128)S(1)}, ...), condition=%wide.region_5.6_spmd.clone, body=%wide.region_1.5_spmd.clone.sunk | while | flops 1720261 | bytes 4997616 | solution.py:171
  34.0 5.4 %collective-permute-start.1 = (f32[5,160]{1,0:T(8,128)S(1)}, f32[5,160]{1,0:T(8,128)S(1)}, u32[]{:S(2)}, u32[]{:S(2)}) collective-permute-start(f32[5,160]{1,0:T(8,128)S(1)} %get-tuple-element.771), channel_id=1, source_target_pairs={{1,0},{2,1},{3,2},{4,3},{5,4},{6,5},{7,6},{8,7},{9,8},{10,9},{11,1... | collective-permute-start | bytes 9608 | tf_op jit(solution)/shard_map/while/body/eval_jaxpr/ppermute | solution.py:22
  39.6 1.1 collective-permute-done
  40.8 17.1 %while.62 = (s32[]{:T(128)}, f32[5,3392]{1,0:T(8,128)S(1)}, f32[3072]{0:T(1024)S(1)}, f32[65,3392]{1,0:T(8,128)S(1)}, f32[1,3392]{1,0:T(1,128)S(1)}, /*index=5*/...) while((s32[]{:T(128)}, f32[5,3392]{1,0:T(8,128)S(1)}, ...), condition=%wide.region_4.4_spmd.clone, body=%wide.region_2.3_spmd.clone.sunk | while | flops 611715 | bytes 3702403 | solution.py:163
  58.3 5.4 %collective-permute-start.1 = (f32[5,160]{1,0:T(8,128)S(1)}, f32[5,160]{1,0:T(8,128)S(1)}, u32[]{:S(2)}, u32[]{:S(2)}) collective-permute-start(f32[5,160]{1,0:T(8,128)S(1)} %get-tuple-element.771), channel_id=1, source_target_pairs={{1,0},{2,1},{3,2},{4,3},{5,4},{6,5},{7,6},{8,7},{9,8},{10,9},{11,1... | collective-permute-start | bytes 9608 | tf_op jit(solution)/shard_map/while/body/eval_jaxpr/ppermute | solution.py:22
  63.9 1.1 collective-permute-done
  65.2 17.1 %while.62 = (s32[]{:T(128)}, f32[5,3392]{1,0:T(8,128)S(1)}, f32[3072]{0:T(1024)S(1)}, f32[65,3392]{1,0:T(8,128)S(1)}, f32[1,3392]{1,0:T(1,128)S(1)}, /*index=5*/...) while((s32[]{:T(128)}, f32[5,3392]{1,0:T(8,128)S(1)}, ...), condition=%wide.region_4.4_spmd.clone, body=%wide.region_2.3_spmd.clone.sunk | while | flops 611715 | bytes 3702403 | solution.py:163
  82.7 5.4 %collective-permute-start.1 = (f32[5,160]{1,0:T(8,128)S(1)}, f32[5,160]{1,0:T(8,128)S(1)}, u32[]{:S(2)}, u32[]{:S(2)}) collective-permute-start(f32[5,160]{1,0:T(8,128)S(1)} %get-tuple-element.771), channel_id=1, source_target_pairs={{1,0},{2,1},{3,2},{4,3},{5,4},{6,5},{7,6},{8,7},{9,8},{10,9},{11,1... | collective-permute-start | bytes 9608 | tf_op jit(solution)/shard_map/while/body/eval_jaxpr/ppermute | solution.py:22
  88.3 1.1 collective-permute-done
  89.5 17.1 %while.62 = (s32[]{:T(128)}, f32[5,3392]{1,0:T(8,128)S(1)}, f32[3072]{0:T(1024)S(1)}, f32[65,3392]{1,0:T(8,128)S(1)}, f32[1,3392]{1,0:T(1,128)S(1)}, /*index=5*/...) while((s32[]{:T(128)}, f32[5,3392]{1,0:T(8,128)S(1)}, ...), condition=%wide.region_4.4_spmd.clone, body=%wide.region_2.3_spmd.clone.sunk | while | flops 611715 | bytes 3702403 | solution.py:163
  107.0 5.4 %collective-permute-start.1 = (f32[5,160]{1,0:T(8,128)S(1)}, f32[5,160]{1,0:T(8,128)S(1)}, u32[]{:S(2)}, u32[]{:S(2)}) collective-permute-start(f32[5,160]{1,0:T(8,128)S(1)} %get-tuple-element.771), channel_id=1, source_target_pairs={{1,0},{2,1},{3,2},{4,3},{5,4},{6,5},{7,6},{8,7},{9,8},{10,9},{11,1... | collective-permute-start | bytes 9608 | tf_op jit(solution)/shard_map/while/body/eval_jaxpr/ppermute | solution.py:22
  112.6 1.1 collective-permute-done
  113.9 17.1 %while.62 = (s32[]{:T(128)}, f32[5,3392]{1,0:T(8,128)S(1)}, f32[3072]{0:T(1024)S(1)}, f32[65,3392]{1,0:T(8,128)S(1)}, f32[1,3392]{1,0:T(1,128)S(1)}, /*index=5*/...) while((s32[]{:T(128)}, f32[5,3392]{1,0:T(8,128)S(1)}, ...), condition=%wide.region_4.4_spmd.clone, body=%wide.region_2.3_spmd.clone.sunk | while | flops 611715 | bytes 3702403 | solution.py:163
  131.4 5.4 %collective-permute-start.1 = (f32[5,160]{1,0:T(8,128)S(1)}, f32[5,160]{1,0:T(8,128)S(1)}, u32[]{:S(2)}, u32[]{:S(2)}) collective-permute-start(f32[5,160]{1,0:T(8,128)S(1)} %get-tuple-element.771), channel_id=1, source_target_pairs={{1,0},{2,1},{3,2},{4,3},{5,4},{6,5},{7,6},{8,7},{9,8},{10,9},{11,1... | collective-permute-start | bytes 9608 | tf_op jit(solution)/shard_map/while/body/eval_jaxpr/ppermute | solution.py:22
  137.0 1.1 collective-permute-done
  138.2 17.1 %while.62 = (s32[]{:T(128)}, f32[5,3392]{1,0:T(8,128)S(1)}, f32[3072]{0:T(1024)S(1)}, f32[65,3392]{1,0:T(8,128)S(1)}, f32[1,3392]{1,0:T(1,128)S(1)}, /*index=5*/...) while((s32[]{:T(128)}, f32[5,3392]{1,0:T(8,128)S(1)}, ...), condition=%wide.region_4.4_spmd.clone, body=%wide.region_2.3_spmd.clone.sunk | while | flops 611715 | bytes 3702403 | solution.py:163
  155.7 5.4 %collective-permute-start.1 = (f32[5,160]{1,0:T(8,128)S(1)}, f32[5,160]{1,0:T(8,128)S(1)}, u32[]{:S(2)}, u32[]{:S(2)}) collective-permute-start(f32[5,160]{1,0:T(8,128)S(1)} %get-tuple-element.771), channel_id=1, source_target_pairs={{1,0},{2,1},{3,2},{4,3},{5,4},{6,5},{7,6},{8,7},{9,8},{10,9},{11,1... | collective-permute-start | bytes 9608 | tf_op jit(solution)/shard_map/while/body/eval_jaxpr/ppermute | solution.py:22
  161.3 1.1 collective-permute-done
  162.5 17.1 %while.62 = (s32[]{:T(128)}, f32[5,3392]{1,0:T(8,128)S(1)}, f32[3072]{0:T(1024)S(1)}, f32[65,3392]{1,0:T(8,128)S(1)}, f32[1,3392]{1,0:T(1,128)S(1)}, /*index=5*/...) while((s32[]{:T(128)}, f32[5,3392]{1,0:T(8,128)S(1)}, ...), condition=%wide.region_4.4_spmd.clone, body=%wide.region_2.3_spmd.clone.sunk | while | flops 611715 | bytes 3702403 | solution.py:163
  180.0 5.4 %collective-permute-start.1 = (f32[5,160]{1,0:T(8,128)S(1)}, f32[5,160]{1,0:T(8,128)S(1)}, u32[]{:S(2)}, u32[]{:S(2)}) collective-permute-start(f32[5,160]{1,0:T(8,128)S(1)} %get-tuple-element.771), channel_id=1, source_target_pairs={{1,0},{2,1},{3,2},{4,3},{5,4},{6,5},{7,6},{8,7},{9,8},{10,9},{11,1... | collective-permute-start | bytes 9608 | tf_op jit(solution)/shard_map/while/body/eval_jaxpr/ppermute | solution.py:22
  185.7 1.1 collective-permute-done
  186.9 17.1 %while.62 = (s32[]{:T(128)}, f32[5,3392]{1,0:T(8,128)S(1)}, f32[3072]{0:T(1024)S(1)}, f32[65,3392]{1,0:T(8,128)S(1)}, f32[1,3392]{1,0:T(1,128)S(1)}, /*index=5*/...) while((s32[]{:T(128)}, f32[5,3392]{1,0:T(8,128)S(1)}, ...), condition=%wide.region_4.4_spmd.clone, body=%wide.region_2.3_spmd.clone.sunk | while | flops 611715 | bytes 3702403 | solution.py:163
  204.4 5.4 %collective-permute-start.1 = (f32[5,160]{1,0:T(8,128)S(1)}, f32[5,160]{1,0:T(8,128)S(1)}, u32[]{:S(2)}, u32[]{:S(2)}) collective-permute-start(f32[5,160]{1,0:T(8,128)S(1)} %get-tuple-element.771), channel_id=1, source_target_pairs={{1,0},{2,1},{3,2},{4,3},{5,4},{6,5},{7,6},{8,7},{9,8},{10,9},{11,1... | collective-permute-start | bytes 9608 | tf_op jit(solution)/shard_map/while/body/eval_jaxpr/ppermute | solution.py:22
  210.0 1.1 collective-permute-done
  211.2 17.1 %while.62 = (s32[]{:T(128)}, f32[5,3392]{1,0:T(8,128)S(1)}, f32[3072]{0:T(1024)S(1)}, f32[65,3392]{1,0:T(8,128)S(1)}, f32[1,3392]{1,0:T(1,128)S(1)}, /*index=5*/...) while((s32[]{:T(128)}, f32[5,3392]{1,0:T(8,128)S(1)}, ...), condition=%wide.region_4.4_spmd.clone, body=%wide.region_2.3_spmd.clone.sunk | while | flops 611715 | bytes 3702403 | solution.py:163
  228.7 5.4 %collective-permute-start.1 = (f32[5,160]{1,0:T(8,128)S(1)}, f32[5,160]{1,0:T(8,128)S(1)}, u32[]{:S(2)}, u32[]{:S(2)}) collective-permute-start(f32[5,160]{1,0:T(8,128)S(1)} %get-tuple-element.771), channel_id=1, source_target_pairs={{1,0},{2,1},{3,2},{4,3},{5,4},{6,5},{7,6},{8,7},{9,8},{10,9},{11,1... | collective-permute-start | bytes 9608 | tf_op jit(solution)/shard_map/while/body/eval_jaxpr/ppermute | solution.py:22
  234.3 1.1 collective-permute-done
  235.6 17.1 %while.62 = (s32[]{:T(128)}, f32[5,3392]{1,0:T(8,128)S(1)}, f32[3072]{0:T(1024)S(1)}, f32[65,3392]{1,0:T(8,128)S(1)}, f32[1,3392]{1,0:T(1,128)S(1)}, /*index=5*/...) while((s32[]{:T(128)}, f32[5,3392]{1,0:T(8,128)S(1)}, ...), condition=%wide.region_4.4_spmd.clone, body=%wide.region_2.3_spmd.clone.sunk | while | flops 611715 | bytes 3702403 | solution.py:163
  253.1 5.4 %collective-permute-start.1 = (f32[5,160]{1,0:T(8,128)S(1)}, f32[5,160]{1,0:T(8,128)S(1)}, u32[]{:S(2)}, u32[]{:S(2)}) collective-permute-start(f32[5,160]{1,0:T(8,128)S(1)} %get-tuple-element.771), channel_id=1, source_target_pairs={{1,0},{2,1},{3,2},{4,3},{5,4},{6,5},{7,6},{8,7},{9,8},{10,9},{11,1... | collective-permute-start | bytes 9608 | tf_op jit(solution)/shard_map/while/body/eval_jaxpr/ppermute | solution.py:22
  258.7 1.1 collective-permute-done
  259.9 17.1 %while.62 = (s32[]{:T(128)}, f32[5,3392]{1,0:T(8,128)S(1)}, f32[3072]{0:T(1024)S(1)}, f32[65,3392]{1,0:T(8,128)S(1)}, f32[1,3392]{1,0:T(1,128)S(1)}, /*index=5*/...) while((s32[]{:T(128)}, f32[5,3392]{1,0:T(8,128)S(1)}, ...), condition=%wide.region_4.4_spmd.clone, body=%wide.region_2.3_spmd.clone.sunk | while | flops 611715 | bytes 3702403 | solution.py:163
  277.4 5.4 %collective-permute-start.1 = (f32[5,160]{1,0:T(8,128)S(1)}, f32[5,160]{1,0:T(8,128)S(1)}, u32[]{:S(2)}, u32[]{:S(2)}) collective-permute-start(f32[5,160]{1,0:T(8,128)S(1)} %get-tuple-element.771), channel_id=1, source_target_pairs={{1,0},{2,1},{3,2},{4,3},{5,4},{6,5},{7,6},{8,7},{9,8},{10,9},{11,1... | collective-permute-start | bytes 9608 | tf_op jit(solution)/shard_map/while/body/eval_jaxpr/ppermute | solution.py:22
  283.0 1.1 collective-permute-done
  284.3 17.1 %while.62 = (s32[]{:T(128)}, f32[5,3392]{1,0:T(8,128)S(1)}, f32[3072]{0:T(1024)S(1)}, f32[65,3392]{1,0:T(8,128)S(1)}, f32[1,3392]{1,0:T(1,128)S(1)}, /*index=5*/...) while((s32[]{:T(128)}, f32[5,3392]{1,0:T(8,128)S(1)}, ...), condition=%wide.region_4.4_spmd.clone, body=%wide.region_2.3_spmd.clone.sunk | while | flops 611715 | bytes 3702403 | solution.py:163
  301.8 5.4 %collective-permute-start.1 = (f32[5,160]{1,0:T(8,128)S(1)}, f32[5,160]{1,0:T(8,128)S(1)}, u32[]{:S(2)}, u32[]{:S(2)}) collective-permute-start(f32[5,160]{1,0:T(8,128)S(1)} %get-tuple-element.771), channel_id=1, source_target_pairs={{1,0},{2,1},{3,2},{4,3},{5,4},{6,5},{7,6},{8,7},{9,8},{10,9},{11,1... | collective-permute-start | bytes 9608 | tf_op jit(solution)/shard_map/while/body/eval_jaxpr/ppermute | solution.py:22
  307.4 1.1 collective-permute-done
  308.6 17.1 %while.62 = (s32[]{:T(128)}, f32[5,3392]{1,0:T(8,128)S(1)}, f32[3072]{0:T(1024)S(1)}, f32[65,3392]{1,0:T(8,128)S(1)}, f32[1,3392]{1,0:T(1,128)S(1)}, /*index=5*/...) while((s32[]{:T(128)}, f32[5,3392]{1,0:T(8,128)S(1)}, ...), condition=%wide.region_4.4_spmd.clone, body=%wide.region_2.3_spmd.clone.sunk | while | flops 611715 | bytes 3702403 | solution.py:163
  326.9 13.1 %fusion.18 = f32[1,8192]{1,0:T(1,128)S(1)} fusion(s32[8192]{0:T(1024)S(1)} %bitcast.44, s32[1,2048]{1,0:T(1,128)S(1)} %copy-done.9), kind=kOutput, calls=%fused_computation.106 | convolution fusion | flops 50333696 | bytes 73728 | tf_op jit(solution)/shard_map/dot_general | solution.py:99
  340.7 42.5 %all-gather.2.cloned.1.call-done = bf16[768,12,128]{2,0,1:T(8,128)(2,1)} async-done(((bf16[24,12,128]{2,0,1:T(8,128)(2,1)}), bf16[768,12,128]{2,0,1:T(8,128)(2,1)}) %all-gather.2.cloned.1.call-update) | async-done | bytes 2359312 | tf_op jit(solution)/shard_map/all_gather | solution.py:175
  383.2 4.9 %copy.20 = bf16[768,12,128]{2,1,0:T(8,128)(2,1)} copy(bf16[768,12,128]{2,0,1:T(8,128)(2,1)} %all-gather.2.cloned.1.call-done) | data formatting | bytes 4718592 | tf_op jit(solution)/shard_map/all_gather | solution.py:175
  388.2 2.7 gather_fusion
  390.9 4.6 %fusion.30 = f32[64,128]{1,0:T(8,128)S(1)} fusion(bf16[64,4,12,128]{3,2,1,0:T(8,128)(2,1)S(1)} %bitcast.37, bf16[64,4,128,128]{3,2,1,0:T(8,128)(2,1)} %param.27, s32[64,128]{1,0:T(8,128)S(1)} %bitcast.40), kind=kOutput, calls=%fused_computation.119 | convolution fusion | flops 100950016 | bytes 9240576 | tf_op jit(solution)/shard_map/ptil,ptlq->piq/dot_general | solution.py:178
  396.1 0.9 subtract_add_fusion
  (1178 shorter events, 210.8 us)
Async XLA Ops:
  7.2 18.2 %copy-start.10 = (u32[32]{0:T(128)S(1)}, u32[32]{0:T(128)}, u32[]{:S(2)}) copy-start(u32[32]{0:T(128)} %constant.153) | copy-start | bytes 388
  7.2 19.4 %copy-start.7 = (f32[2,3072]{1,0:T(2,128)S(1)}, f32[2,3072]{1,0:T(2,128)}, u32[]{:S(2)}) copy-start(f32[2,3072]{1,0:T(2,128)} %param.19) | copy-start | bytes 73732
  7.2 19.4 %copy-start = (f32[3072]{0:T(1024)S(1)}, f32[3072]{0:T(1024)}, u32[]{:S(2)}) copy-start(f32[3072]{0:T(1024)} %param.17) | copy-start | bytes 36868
  7.2 24.9 %copy-start.5 = (f32[4,3072]{1,0:T(4,128)S(1)}, f32[4,3072]{1,0:T(4,128)}, u32[]{:S(2)}) copy-start(f32[4,3072]{1,0:T(4,128)} %param.16) | copy-start | bytes 147460
  7.2 26.7 %copy-start.1 = (f32[3072]{0:T(1024)S(1)}, f32[3072]{0:T(1024)}, u32[]{:S(2)}) copy-start(f32[3072]{0:T(1024)} %param.18) | copy-start | bytes 36868
  7.2 376.0 %all-gather.2.cloned.1.call-start = ((), (), s32[]{:S(2)}) async-start(), calls=%async_computation | async-start | bytes 2433024 | tf_op jit(solution)/shard_map/all_gather | solution.py:175
  26.8 6.7 %collective-permute-start.2 = (f32[6,160]{1,0:T(8,128)S(1)}, f32[6,160]{1,0:T(8,128)S(1)}, u32[]{:S(2)}, u32[]{:S(2)}) collective-permute-start(f32[6,160]{1,0:T(8,128)S(1)} %get-tuple-element.554), channel_id=1, source_target_pairs={{0,1},{1,2},{2,3},{3,4},{4,5},{5,6},{6,7},{7,8},{8,9},{9,10},{10,1... | collective-permute-start | bytes 11528 | tf_op jit(solution)/shard_map/ppermute | solution.py:20
  26.8 6.7 %collective-permute-start.3 = (f32[6,160]{1,0:T(8,128)S(1)}, f32[6,160]{1,0:T(8,128)S(1)}, u32[]{:S(2)}, u32[]{:S(2)}) collective-permute-start(f32[6,160]{1,0:T(8,128)S(1)} %get-tuple-element.553), channel_id=1, source_target_pairs={{1,0},{2,1},{3,2},{4,3},{5,4},{6,5},{7,6},{8,7},{9,8},{10,9},{11,1... | collective-permute-start | bytes 11528 | tf_op jit(solution)/shard_map/ppermute | solution.py:22
  33.9 292.8 %copy-start.8 = (s32[64,4]{0,1:T(4,128)S(1)}, s32[64,4]{0,1:T(4,128)}, u32[]{:S(2)}) copy-start(s32[64,4]{0,1:T(4,128)} %param.26) | copy-start | bytes 3076
  33.9 293.0 %copy-start.6 = (s32[1,8192]{1,0:T(1,128)S(1)}, s32[1,8192]{1,0:T(1,128)}, u32[]{:S(2)}) copy-start(s32[1,8192]{1,0:T(1,128)} %param.24) | copy-start | bytes 98308
  33.9 293.0 %copy-start.9 = (s32[1,2048]{1,0:T(1,128)S(1)}, s32[1,2048]{1,0:T(1,128)}, u32[]{:S(2)}) copy-start(s32[1,2048]{1,0:T(1,128)} %param.25) | copy-start | bytes 24580
  34.0 6.7 %collective-permute-start = (f32[5,160]{1,0:T(8,128)S(1)}, f32[5,160]{1,0:T(8,128)S(1)}, u32[]{:S(2)}, u32[]{:S(2)}) collective-permute-start(f32[5,160]{1,0:T(8,128)S(1)} %get-tuple-element.770), channel_id=1, source_target_pairs={{0,1},{1,2},{2,3},{3,4},{4,5},{5,6},{6,7},{7,8},{8,9},{9,10},{10,1... | collective-permute-start | bytes 9608 | tf_op jit(solution)/shard_map/while/body/eval_jaxpr/ppermute | solution.py:20
  34.0 6.7 %collective-permute-start.1 = (f32[5,160]{1,0:T(8,128)S(1)}, f32[5,160]{1,0:T(8,128)S(1)}, u32[]{:S(2)}, u32[]{:S(2)}) collective-permute-start(f32[5,160]{1,0:T(8,128)S(1)} %get-tuple-element.771), channel_id=1, source_target_pairs={{1,0},{2,1},{3,2},{4,3},{5,4},{6,5},{7,6},{8,7},{9,8},{10,9},{11,1... | collective-permute-start | bytes 9608 | tf_op jit(solution)/shard_map/while/body/eval_jaxpr/ppermute | solution.py:22
  58.3 6.7 %collective-permute-start = (f32[5,160]{1,0:T(8,128)S(1)}, f32[5,160]{1,0:T(8,128)S(1)}, u32[]{:S(2)}, u32[]{:S(2)}) collective-permute-start(f32[5,160]{1,0:T(8,128)S(1)} %get-tuple-element.770), channel_id=1, source_target_pairs={{0,1},{1,2},{2,3},{3,4},{4,5},{5,6},{6,7},{7,8},{8,9},{9,10},{10,1... | collective-permute-start | bytes 9608 | tf_op jit(solution)/shard_map/while/body/eval_jaxpr/ppermute | solution.py:20
  58.3 6.7 %collective-permute-start.1 = (f32[5,160]{1,0:T(8,128)S(1)}, f32[5,160]{1,0:T(8,128)S(1)}, u32[]{:S(2)}, u32[]{:S(2)}) collective-permute-start(f32[5,160]{1,0:T(8,128)S(1)} %get-tuple-element.771), channel_id=1, source_target_pairs={{1,0},{2,1},{3,2},{4,3},{5,4},{6,5},{7,6},{8,7},{9,8},{10,9},{11,1... | collective-permute-start | bytes 9608 | tf_op jit(solution)/shard_map/while/body/eval_jaxpr/ppermute | solution.py:22
  82.7 6.7 %collective-permute-start = (f32[5,160]{1,0:T(8,128)S(1)}, f32[5,160]{1,0:T(8,128)S(1)}, u32[]{:S(2)}, u32[]{:S(2)}) collective-permute-start(f32[5,160]{1,0:T(8,128)S(1)} %get-tuple-element.770), channel_id=1, source_target_pairs={{0,1},{1,2},{2,3},{3,4},{4,5},{5,6},{6,7},{7,8},{8,9},{9,10},{10,1... | collective-permute-start | bytes 9608 | tf_op jit(solution)/shard_map/while/body/eval_jaxpr/ppermute | solution.py:20
  82.7 6.7 %collective-permute-start.1 = (f32[5,160]{1,0:T(8,128)S(1)}, f32[5,160]{1,0:T(8,128)S(1)}, u32[]{:S(2)}, u32[]{:S(2)}) collective-permute-start(f32[5,160]{1,0:T(8,128)S(1)} %get-tuple-element.771), channel_id=1, source_target_pairs={{1,0},{2,1},{3,2},{4,3},{5,4},{6,5},{7,6},{8,7},{9,8},{10,9},{11,1... | collective-permute-start | bytes 9608 | tf_op jit(solution)/shard_map/while/body/eval_jaxpr/ppermute | solution.py:22
  107.0 6.7 %collective-permute-start = (f32[5,160]{1,0:T(8,128)S(1)}, f32[5,160]{1,0:T(8,128)S(1)}, u32[]{:S(2)}, u32[]{:S(2)}) collective-permute-start(f32[5,160]{1,0:T(8,128)S(1)} %get-tuple-element.770), channel_id=1, source_target_pairs={{0,1},{1,2},{2,3},{3,4},{4,5},{5,6},{6,7},{7,8},{8,9},{9,10},{10,1... | collective-permute-start | bytes 9608 | tf_op jit(solution)/shard_map/while/body/eval_jaxpr/ppermute | solution.py:20
  107.0 6.7 %collective-permute-start.1 = (f32[5,160]{1,0:T(8,128)S(1)}, f32[5,160]{1,0:T(8,128)S(1)}, u32[]{:S(2)}, u32[]{:S(2)}) collective-permute-start(f32[5,160]{1,0:T(8,128)S(1)} %get-tuple-element.771), channel_id=1, source_target_pairs={{1,0},{2,1},{3,2},{4,3},{5,4},{6,5},{7,6},{8,7},{9,8},{10,9},{11,1... | collective-permute-start | bytes 9608 | tf_op jit(solution)/shard_map/while/body/eval_jaxpr/ppermute | solution.py:22
  131.4 6.7 %collective-permute-start = (f32[5,160]{1,0:T(8,128)S(1)}, f32[5,160]{1,0:T(8,128)S(1)}, u32[]{:S(2)}, u32[]{:S(2)}) collective-permute-start(f32[5,160]{1,0:T(8,128)S(1)} %get-tuple-element.770), channel_id=1, source_target_pairs={{0,1},{1,2},{2,3},{3,4},{4,5},{5,6},{6,7},{7,8},{8,9},{9,10},{10,1... | collective-permute-start | bytes 9608 | tf_op jit(solution)/shard_map/while/body/eval_jaxpr/ppermute | solution.py:20
  131.4 6.7 %collective-permute-start.1 = (f32[5,160]{1,0:T(8,128)S(1)}, f32[5,160]{1,0:T(8,128)S(1)}, u32[]{:S(2)}, u32[]{:S(2)}) collective-permute-start(f32[5,160]{1,0:T(8,128)S(1)} %get-tuple-element.771), channel_id=1, source_target_pairs={{1,0},{2,1},{3,2},{4,3},{5,4},{6,5},{7,6},{8,7},{9,8},{10,9},{11,1... | collective-permute-start | bytes 9608 | tf_op jit(solution)/shard_map/while/body/eval_jaxpr/ppermute | solution.py:22
  155.7 6.7 %collective-permute-start = (f32[5,160]{1,0:T(8,128)S(1)}, f32[5,160]{1,0:T(8,128)S(1)}, u32[]{:S(2)}, u32[]{:S(2)}) collective-permute-start(f32[5,160]{1,0:T(8,128)S(1)} %get-tuple-element.770), channel_id=1, source_target_pairs={{0,1},{1,2},{2,3},{3,4},{4,5},{5,6},{6,7},{7,8},{8,9},{9,10},{10,1... | collective-permute-start | bytes 9608 | tf_op jit(solution)/shard_map/while/body/eval_jaxpr/ppermute | solution.py:20
  155.7 6.7 %collective-permute-start.1 = (f32[5,160]{1,0:T(8,128)S(1)}, f32[5,160]{1,0:T(8,128)S(1)}, u32[]{:S(2)}, u32[]{:S(2)}) collective-permute-start(f32[5,160]{1,0:T(8,128)S(1)} %get-tuple-element.771), channel_id=1, source_target_pairs={{1,0},{2,1},{3,2},{4,3},{5,4},{6,5},{7,6},{8,7},{9,8},{10,9},{11,1... | collective-permute-start | bytes 9608 | tf_op jit(solution)/shard_map/while/body/eval_jaxpr/ppermute | solution.py:22
  180.0 6.7 %collective-permute-start = (f32[5,160]{1,0:T(8,128)S(1)}, f32[5,160]{1,0:T(8,128)S(1)}, u32[]{:S(2)}, u32[]{:S(2)}) collective-permute-start(f32[5,160]{1,0:T(8,128)S(1)} %get-tuple-element.770), channel_id=1, source_target_pairs={{0,1},{1,2},{2,3},{3,4},{4,5},{5,6},{6,7},{7,8},{8,9},{9,10},{10,1... | collective-permute-start | bytes 9608 | tf_op jit(solution)/shard_map/while/body/eval_jaxpr/ppermute | solution.py:20
  180.0 6.7 %collective-permute-start.1 = (f32[5,160]{1,0:T(8,128)S(1)}, f32[5,160]{1,0:T(8,128)S(1)}, u32[]{:S(2)}, u32[]{:S(2)}) collective-permute-start(f32[5,160]{1,0:T(8,128)S(1)} %get-tuple-element.771), channel_id=1, source_target_pairs={{1,0},{2,1},{3,2},{4,3},{5,4},{6,5},{7,6},{8,7},{9,8},{10,9},{11,1... | collective-permute-start | bytes 9608 | tf_op jit(solution)/shard_map/while/body/eval_jaxpr/ppermute | solution.py:22
  204.4 6.7 %collective-permute-start = (f32[5,160]{1,0:T(8,128)S(1)}, f32[5,160]{1,0:T(8,128)S(1)}, u32[]{:S(2)}, u32[]{:S(2)}) collective-permute-start(f32[5,160]{1,0:T(8,128)S(1)} %get-tuple-element.770), channel_id=1, source_target_pairs={{0,1},{1,2},{2,3},{3,4},{4,5},{5,6},{6,7},{7,8},{8,9},{9,10},{10,1... | collective-permute-start | bytes 9608 | tf_op jit(solution)/shard_map/while/body/eval_jaxpr/ppermute | solution.py:20
  204.4 6.7 %collective-permute-start.1 = (f32[5,160]{1,0:T(8,128)S(1)}, f32[5,160]{1,0:T(8,128)S(1)}, u32[]{:S(2)}, u32[]{:S(2)}) collective-permute-start(f32[5,160]{1,0:T(8,128)S(1)} %get-tuple-element.771), channel_id=1, source_target_pairs={{1,0},{2,1},{3,2},{4,3},{5,4},{6,5},{7,6},{8,7},{9,8},{10,9},{11,1... | collective-permute-start | bytes 9608 | tf_op jit(solution)/shard_map/while/body/eval_jaxpr/ppermute | solution.py:22
  228.7 6.7 %collective-permute-start = (f32[5,160]{1,0:T(8,128)S(1)}, f32[5,160]{1,0:T(8,128)S(1)}, u32[]{:S(2)}, u32[]{:S(2)}) collective-permute-start(f32[5,160]{1,0:T(8,128)S(1)} %get-tuple-element.770), channel_id=1, source_target_pairs={{0,1},{1,2},{2,3},{3,4},{4,5},{5,6},{6,7},{7,8},{8,9},{9,10},{10,1... | collective-permute-start | bytes 9608 | tf_op jit(solution)/shard_map/while/body/eval_jaxpr/ppermute | solution.py:20
  228.7 6.7 %collective-permute-start.1 = (f32[5,160]{1,0:T(8,128)S(1)}, f32[5,160]{1,0:T(8,128)S(1)}, u32[]{:S(2)}, u32[]{:S(2)}) collective-permute-start(f32[5,160]{1,0:T(8,128)S(1)} %get-tuple-element.771), channel_id=1, source_target_pairs={{1,0},{2,1},{3,2},{4,3},{5,4},{6,5},{7,6},{8,7},{9,8},{10,9},{11,1... | collective-permute-start | bytes 9608 | tf_op jit(solution)/shard_map/while/body/eval_jaxpr/ppermute | solution.py:22
  253.1 6.7 %collective-permute-start = (f32[5,160]{1,0:T(8,128)S(1)}, f32[5,160]{1,0:T(8,128)S(1)}, u32[]{:S(2)}, u32[]{:S(2)}) collective-permute-start(f32[5,160]{1,0:T(8,128)S(1)} %get-tuple-element.770), channel_id=1, source_target_pairs={{0,1},{1,2},{2,3},{3,4},{4,5},{5,6},{6,7},{7,8},{8,9},{9,10},{10,1... | collective-permute-start | bytes 9608 | tf_op jit(solution)/shard_map/while/body/eval_jaxpr/ppermute | solution.py:20
  253.1 6.7 %collective-permute-start.1 = (f32[5,160]{1,0:T(8,128)S(1)}, f32[5,160]{1,0:T(8,128)S(1)}, u32[]{:S(2)}, u32[]{:S(2)}) collective-permute-start(f32[5,160]{1,0:T(8,128)S(1)} %get-tuple-element.771), channel_id=1, source_target_pairs={{1,0},{2,1},{3,2},{4,3},{5,4},{6,5},{7,6},{8,7},{9,8},{10,9},{11,1... | collective-permute-start | bytes 9608 | tf_op jit(solution)/shard_map/while/body/eval_jaxpr/ppermute | solution.py:22
  277.4 6.7 %collective-permute-start = (f32[5,160]{1,0:T(8,128)S(1)}, f32[5,160]{1,0:T(8,128)S(1)}, u32[]{:S(2)}, u32[]{:S(2)}) collective-permute-start(f32[5,160]{1,0:T(8,128)S(1)} %get-tuple-element.770), channel_id=1, source_target_pairs={{0,1},{1,2},{2,3},{3,4},{4,5},{5,6},{6,7},{7,8},{8,9},{9,10},{10,1... | collective-permute-start | bytes 9608 | tf_op jit(solution)/shard_map/while/body/eval_jaxpr/ppermute | solution.py:20
  277.4 6.7 %collective-permute-start.1 = (f32[5,160]{1,0:T(8,128)S(1)}, f32[5,160]{1,0:T(8,128)S(1)}, u32[]{:S(2)}, u32[]{:S(2)}) collective-permute-start(f32[5,160]{1,0:T(8,128)S(1)} %get-tuple-element.771), channel_id=1, source_target_pairs={{1,0},{2,1},{3,2},{4,3},{5,4},{6,5},{7,6},{8,7},{9,8},{10,9},{11,1... | collective-permute-start | bytes 9608 | tf_op jit(solution)/shard_map/while/body/eval_jaxpr/ppermute | solution.py:22
  301.7 6.7 %collective-permute-start = (f32[5,160]{1,0:T(8,128)S(1)}, f32[5,160]{1,0:T(8,128)S(1)}, u32[]{:S(2)}, u32[]{:S(2)}) collective-permute-start(f32[5,160]{1,0:T(8,128)S(1)} %get-tuple-element.770), channel_id=1, source_target_pairs={{0,1},{1,2},{2,3},{3,4},{4,5},{5,6},{6,7},{7,8},{8,9},{9,10},{10,1... | collective-permute-start | bytes 9608 | tf_op jit(solution)/shard_map/while/body/eval_jaxpr/ppermute | solution.py:20
  301.8 6.7 %collective-permute-start.1 = (f32[5,160]{1,0:T(8,128)S(1)}, f32[5,160]{1,0:T(8,128)S(1)}, u32[]{:S(2)}, u32[]{:S(2)}) collective-permute-start(f32[5,160]{1,0:T(8,128)S(1)} %get-tuple-element.771), channel_id=1, source_target_pairs={{1,0},{2,1},{3,2},{4,3},{5,4},{6,5},{7,6},{8,7},{9,8},{10,9},{11,1... | collective-permute-start | bytes 9608 | tf_op jit(solution)/shard_map/while/body/eval_jaxpr/ppermute | solution.py:22
  340.1 50.8 %copy-start.3 = (s32[8192]{0:T(1024)S(1)}, s32[8192]{0:T(1024)}, u32[]{:S(2)}) copy-start(s32[8192]{0:T(1024)} %param.23) | copy-start | bytes 98308
  390.9 5.0 %copy-start.4 = (f32[8192]{0:T(1024)S(1)}, f32[8192]{0:T(1024)}, u32[]{:S(2)}) copy-start(f32[8192]{0:T(1024)} %param.21) | copy-start | bytes 98308
  395.5 1.5 copy-start.2
Sparse Core Ops, SparseCore 0:
  326.8 56.3 all-gather.1
where the time goes:
time: 404 us
  local copies, waits for them, and re-layouts  173 us (43%)
  starting transfers between devices  69.7 us (17%)
  waiting for transfers between devices  57.3 us (14%)
  other arithmetic  46.5 us (12%)
  matrix products  21 us (5%)
  between operations  15 us (4%)
  blocking collectives  13.2 us (3%)
  loops' own time  8.2 us (2%)
    slice x240, local copies, waits for them, and re-layouts, band_inflow(): total = total + weights[shift] * padded[shift:shift + count]  146 us
    ppermute x13, starting transfers between devices, padded_2(): lax.ppermute(head, axis, [((i + 1) % count, i) for i in range(count)])  69.6 us
    all_gather x1, waiting for transfers between devices, body(): every_tile = lax.all_gather(tiles, ('region', 'route'), axis=0, tiled=True)  42.5 us
    sub x60, other arithmetic, finish(): queue = waiting - entering  23 us
    ppermute x13, waiting for transfers between devices, padded_2(): lax.ppermute(tail, axis, [(i, (i + 1) % count) for i in range(count)])  14 us
    unnamed x1, blocking collectives  13.2 us
    dot_general x1, matrix products, swap_flows(): jnp.dot(picker, rate_num.astype(jnp.bfloat16)[:, None], preferred_element...  13.1 us
  transfers between devices with their start and end apart: 27, of which 26 were waited for; matrix products, arithmetic and copies ran while one was open for 4% of the time, Pallas kernels for 0%

commit v1 on v0

v1 whole, which is shorter than its diff:
```python
import jax
import jax.numpy as jnp
from jax import lax
from jax.experimental import pallas as pl
from jax.experimental.pallas import tpu as pltpu
from jax.sharding import PartitionSpec as P

NC = 4
BND = 32
ISTEPS = 5
NI = 12
OD_MOST = 8
LINE = ("region", "route")


def halo_width(span):
    width = NI * ISTEPS * BND
    while (span + 2 * width) % 1024:
        width += 1
    return width


def padded(cells, width):
    count = lax.axis_size(LINE)
    head = cells[:, :width]
    tail = cells[:, cells.shape[1] - width :]
    return jnp.concatenate(
        [
            lax.ppermute(tail, LINE, [(i, (i + 1) % count) for i in range(count)]),
            cells,
            lax.ppermute(head, LINE, [((i + 1) % count, i) for i in range(count)]),
        ],
        axis=1,
    )


def to_cols(rows):
    extent = rows.shape[-1]
    lead = rows.shape[:-1]
    return jnp.swapaxes(rows.reshape(lead + (128, extent // 128)), -1, -2)


def from_cols(cols):
    lead = cols.shape[:-2]
    return jnp.swapaxes(cols, -1, -2).reshape(lead + (-1,))


def sim_kernel(st0_ref, cons_ref, occ_ref, st_ref, w_ref, p_ref):
    rows = st0_ref.shape[1]
    st_ref[...] = st0_ref[...]
    s0 = cons_ref[1]
    s1 = cons_ref[2]
    o0 = cons_ref[3]
    o1 = cons_ref[4]
    for k in range(2 * BND + 1):
        d = float(k - BND)
        w_ref[k] = jnp.where(o0 == d, s0, 0.0) + jnp.where(o1 == d, s1, 0.0)

    def step(j, acc):
        cap = cons_ref[0]
        jam = 4.0 * cap
        rho = [st_ref[c] for c in range(NC)]
        queue = st_ref[NC]
        send = [jnp.minimum(r, cap) for r in rho]
        recv = [jnp.minimum(cap, 0.5 * (jam - r)) for r in rho]
        inner = [jnp.minimum(send[c], recv[c + 1]) for c in range(NC - 1)]
        outflow = send[NC - 1]
        p_ref[BND : BND + rows] = outflow
        p_ref[BND + rows :] = pltpu.roll(outflow[:BND], 127, 1)
        p_ref[:BND] = pltpu.roll(outflow[rows - BND :], 1, 1)
        arriving = cons_ref[5]
        for k in range(2 * BND + 1):
            arriving = arriving + w_ref[k] * p_ref[pl.ds(k, rows), :]
        waiting = queue + arriving
        entering = jnp.minimum(waiting, recv[0])
        queue = waiting - entering
        into = [entering] + inner
        leaving = inner + [outflow]
        new = [(rho[c] + into[c]) - leaving[c] for c in range(NC)]
        for c in range(NC):
            st_ref[c] = new[c]
        st_ref[NC] = queue
        occ = ((((new[0] + new[1]) + new[2]) + new[3]) + queue) / cap
        return acc + occ

    def interval(i, carry):
        acc = lax.fori_loop(0, ISTEPS, step, jnp.zeros((rows, 128), jnp.float32))
        occ_ref[i] = acc
        return carry

    lax.fori_loop(0, occ_ref.shape[0], interval, 0)


def simulate(st0, cons, count):
    rows = st0.shape[1]
    return pl.pallas_call(
        sim_kernel,
        out_shape=(
            jax.ShapeDtypeStruct((count, rows, 128), jnp.float32),
            jax.ShapeDtypeStruct(st0.shape, jnp.float32),
        ),
        scratch_shapes=[
            pltpu.VMEM((2 * BND + 1, rows, 128), jnp.float32),
            pltpu.VMEM((rows + 2 * BND, 128), jnp.float32),
        ],
    )(st0, cons)


def group_min(cost, group):
    reach = OD_MOST - 1
    count = cost.shape[0]
    padded_cost = jnp.pad(cost, reach, constant_values=1e30)
    padded_group = jnp.pad(group, reach, constant_values=-1)
    best = cost
    for shift in range(2 * reach + 1):
        near_cost = padded_cost[shift : shift + count]
        near_group = padded_group[shift : shift + count]
        best = jnp.minimum(best, jnp.where(near_group == group, near_cost, best))
    return best


def group_sum(values, group):
    reach = OD_MOST - 1
    count = values.shape[0]
    padded_values = jnp.pad(values, reach)
    padded_group = jnp.pad(group, reach, constant_values=-1)
    total = jnp.zeros_like(values)
    for shift in range(2 * reach + 1):
        near_values = padded_values[shift : shift + count]
        near_group = padded_group[shift : shift + count]
        total = total + jnp.where(near_group == group, near_values, 0.0)
    return total


def swap_flows(cost, flow, group, rate_num):
    best = group_min(cost, group)
    rate = jnp.take(rate_num, group).astype(jnp.float32) / 16.0
    moved = rate * flow * (cost - best) / cost
    pull = (best / cost) ** 4
    return flow - moved + group_sum(moved, group) * pull / group_sum(pull, group)


def select_depart(totals, depart_tile):
    levels = jnp.arange(totals.shape[1], dtype=jnp.int32)
    chosen = jnp.where(levels[None, :, None] == depart_tile[:, None, :], totals, 0.0)
    return jnp.sum(chosen, 1)


def body(
    fill,
    capacity,
    free_time,
    split_share,
    upstream_offset,
    path_flow,
    anchor,
    depart,
    od_pair,
    swap_rate,
    tile_index,
    incidence,
):
    span = fill.shape[1]
    region_links = span * lax.axis_size("route")
    link_tiles = jnp.arange(region_links // 128, dtype=jnp.int32)
    lanes = jnp.arange(128, dtype=jnp.int32)
    tile_pick = jnp.where((anchor // 128)[None, :] == link_tiles[:, None], path_flow[None, :], 0.0)
    lane_pick = ((anchor % 128)[:, None] == lanes[None, :]).astype(jnp.float32)
    local_entry = jnp.dot(
        tile_pick, lane_pick, precision=lax.Precision.HIGHEST, preferred_element_type=jnp.float32
    ).reshape(-1)
    entry = lax.psum_scatter(local_entry, "route", scatter_dimension=0, tiled=True)

    width = halo_width(span)
    rows_in = jnp.concatenate(
        [fill, capacity[None], split_share, upstream_offset.astype(jnp.float32), entry[None]], 0
    )
    wide = padded(rows_in, width)
    wide_cap = wide[NC]
    st0 = jnp.concatenate([wide[:NC] * (4.0 * wide_cap), jnp.zeros_like(wide[:1])], 0)
    cons = wide[NC:]
    occ, state = simulate(to_cols(st0), to_cols(cons), NI)
    occ = from_cols(occ)[:, width : width + span]
    state = from_cols(state)[:NC, width : width + span]
    costs = free_time + occ / ISTEPS

    link_cost = costs.astype(jnp.bfloat16)
    tiles = link_cost.reshape(NI, span // 128, 128).transpose(1, 0, 2)
    wanted_tiles = tile_index.reshape(-1)
    every_tile = lax.all_gather(tiles, LINE, axis=0, tiled=True)
    fetched = every_tile[wanted_tiles]
    fetched = fetched.reshape(tile_index.shape[0], tile_index.shape[1], NI, 128)
    totals = jnp.einsum("ptil,ptlq->piq", fetched, incidence, preferred_element_type=jnp.float32)
    path_cost = select_depart(totals, depart.reshape(-1, 128)).reshape(-1) / 256.0
    new_flow = swap_flows(path_cost, path_flow, od_pair[0], swap_rate[0])
    return (state, path_cost, new_flow)


def solution(mesh):
    return jax.shard_map(
        body,
        mesh=mesh,
        in_specs=(
            P(None, LINE),
            P(LINE),
            P(LINE),
            P(None, LINE),
            P(None, LINE),
            P(LINE),
            P(LINE),
            P(LINE),
            P(LINE, None),
            P(LINE, None),
            P(LINE, None),
            P(LINE, None, None, None),
        ),
        out_specs=(P(None, LINE), P(LINE), P(LINE)),
        check_vma=False,
    )
```

time: 404 us -> 132 us (0.33)
  local copies, waits for them, and re-layouts: 173 us -> 60 us
  starting transfers between devices: 69.7 us -> 4.23 us
  waiting for transfers between devices: 57.3 us -> 12.4 us
  other arithmetic: 46.5 us -> 3.16 us
  Pallas kernels: 0 us -> 15.2 us
  matrix products: 21 us -> 7.92 us
  loops' own time: 8.2 us -> 0 us
    slice x388 -> x2, local copies, waits for them, and re-layouts: 159 us -> 0.65 us  [the longest x1 0.63 us: body(): state = from_cols(state)[:NC, width:width + span]]
    ppermute x26 -> x2, starting transfers between devices: 69.7 us -> 4.19 us  [the longest x1 4.19 us: padded(): lax.ppermute(head, LINE, [((i + 1) % count, i) for i in range(count)])]
    gather x0 -> x1, local copies, waits for them, and re-layouts: none -> 45.5 us  [swap_flows(): rate = jnp.take(rate_num, group).astype(jnp.float32) / 16.0]
    all_gather x1, waiting for transfers between devices: 42.5 us -> 4.37 us  [body(): every_tile = lax.all_gather(tiles, LINE, axis=0, tiled=True)]
    sub x120 -> x0, other arithmetic: 26.3 us -> none  [the longest x60 23 us: finish(): queue = waiting - entering]
    pallas_call x0 -> x1, Pallas kernels: none -> 15.2 us  [simulate(): pl.pallas_call(sim_kernel, out_shape=(jax.ShapeDtypeStruct((count, rows,...]
    dot_general x1 -> x0, matrix products: 13.1 us -> none  [swap_flows(): jnp.dot(picker, rate_num.astype(jnp.bfloat16)[:, None], preferred_element...]
    another operation x13 -> x0, loops' own time: 8.2 us -> none  [the longest x12 7.28 us: one_interval(): lax.fori_loop(0, ISTEPS, one_step, (wide_state, jnp.zeros((span,), jnp.fl...]
  transfers between devices with their start and end apart: 27 -> 3, of which waited for: 26 -> 3; matrix products, arithmetic and copies ran while one was open for 4% -> 36% of each run, Pallas kernels for 0% -> 0%
where the time goes in v1:
time: 132 us; the launch traced here: 131 us
  local copies, waits for them, and re-layouts  60 us (45%)
  Pallas kernels  15.2 us (12%)
  between operations  15 us (11%)
  blocking collectives  13.2 us (10%)
  waiting for transfers between devices  12.4 us (9%)
  matrix products  7.92 us (6%)
  starting transfers between devices  4.23 us (3%)
  other arithmetic  3.16 us (2%)
    gather x1, local copies, waits for them, and re-layouts, swap_flows(): rate = jnp.take(rate_num, group).astype(jnp.float32) / 16.0  45.5 us
    pallas_call x1, Pallas kernels, simulate(): pl.pallas_call(sim_kernel, out_shape=(jax.ShapeDtypeStruct((count, rows,...  15.2 us
    unnamed x1, blocking collectives  13.2 us
    ppermute x1, waiting for transfers between devices, padded(): lax.ppermute(tail, LINE, [(i, (i + 1) % count) for i in range(count)])  5.47 us
    all_gather x1, local copies, waits for them, and re-layouts, body(): every_tile = lax.all_gather(tiles, LINE, axis=0, tiled=True)  4.93 us
    dot_general x1, matrix products, body(): jnp.einsum('ptil,ptlq->piq', fetched, incidence, preferred_element_type=j...  4.61 us
    all_gather x1, waiting for transfers between devices, body(): every_tile = lax.all_gather(tiles, LINE, axis=0, tiled=True)  4.37 us
    ppermute x1, starting transfers between devices, padded(): lax.ppermute(head, LINE, [((i + 1) % count, i) for i in range(count)])  4.19 us
  transfers between devices with their start and end apart: 3, of which 3 were waited for; matrix products, arithmetic and copies ran while one was open for 36% of the time, Pallas kernels for 0%

profile of v1, /device:TPU:0, one launch (start us, length us, event | category | flops | bytes accessed | tf_op | source)
XLA Modules:
  0.0 131.2 jit_solution(7311397140521082309)
XLA Ops:
  7.2 0.0 copy-start
  7.2 0.0 copy-start.11
  7.2 0.0 copy-start.6
  7.2 0.0 copy-start.8
  7.2 0.0 copy-start.7
  7.2 0.0 all-gather.2.cloned.1.call-start
  7.3 0.7 convert_element_type.13
  8.0 0.8 add_select_fusion.1
  8.8 3.3 %fusion.2 = f32[12288]{0:T(1024)S(1)} fusion(s32[8192]{0:T(1024)S(1)} %get-tuple-element.25, f32[8192]{0:T(1024)} %param.17, s32[8192]{0:T(1024)S(1)} %get-tuple-element.24), kind=kOutput, calls=%fused_computation.6 | convolution fusion | flops 1210580992 | bytes 147456 | tf_op jit(solution)/shard_map/dot_general | solution.py:169
  12.1 13.2 %all-reduce.5 = f32[12288]{0:T(1024)S(1)} all-reduce(f32[12288]{0:T(1024)S(1)} %fusion.2), channel_id=2, replica_groups=mesh['region'=8,'route'=4] {'route'}, use_global_device_ids=true, to_apply=%region_0.1.clone | all-reduce | flops 12288 | bytes 98304
  25.4 0.0 copy-done.11
  25.4 0.6 dynamic-slice
  26.6 0.0 copy-done.6
  26.7 0.3 concatenate.9
  27.0 4.2 %collective-permute-start.1 = (f32[10,2048]{1,0:T(8,128)S(1)}, f32[10,2048]{1,0:T(8,128)S(1)}, u32[]{:S(2)}, u32[]{:S(2)}) collective-permute-start(f32[10,2048]{1,0:T(8,128)S(1)} %get-tuple-element.23), channel_id=1, source_target_pairs={{1,0},{2,1},{3,2},{4,3},{5,4},{6,5},{7,6},{8,7},{9,8},{10,9},{11,1... | collective-permute-start | bytes 245768 | tf_op jit(solution)/shard_map/ppermute | solution.py:31
  31.2 0.0 collective-permute-start
  31.2 2.5 %collective-permute-done.1 = f32[10,2048]{1,0:T(8,128)S(1)} collective-permute-done((f32[10,2048]{1,0:T(8,128)S(1)}, f32[10,2048]{1,0:T(8,128)S(1)}, u32[]{:S(2)}, u32[]{:S(2)}) %collective-permute-start.1) | collective-permute-done | bytes 81952 | tf_op jit(solution)/shard_map/ppermute | solution.py:31
  33.7 5.5 %collective-permute-done = f32[10,2048]{1,0:T(8,128)S(1)} collective-permute-done((f32[10,2048]{1,0:T(8,128)S(1)}, f32[10,2048]{1,0:T(8,128)S(1)}, u32[]{:S(2)}, u32[]{:S(2)}) %collective-permute-start) | collective-permute-done | bytes 81952 | tf_op jit(solution)/shard_map/ppermute | solution.py:29
  39.2 0.0 copy-start.9
  39.3 0.0 copy-start.10
  39.3 0.0 copy-start.1
  39.3 0.3 reshape.101
  39.6 0.8 copy.26
  40.4 0.3 reshape.102
  40.8 0.8 copy.27
  41.6 15.2 %shard_map.139 = (f32[12,56,128]{2,1,0:T(8,128)}, f32[5,56,128]{2,1,0:T(8,128)}) custom-call(f32[5,56,128]{2,1,0:T(8,128)} %bitcast.37, f32[6,56,128]{2,1,0:T(8,128)} %bitcast.36), custom_call_target="tpu_custom_call" | custom-call | tf_op jit(solution)/shard_map/pallas_call | solution.py:96
  56.8 1.2 copy.29
  58.1 0.5 reshape.104
  58.6 0.6 slice_bitcast_fusion
  59.2 0.0 all-gather.2.cloned.1.call-update
  59.3 0.1 copy.30
  59.4 0.1 reshape.106
  59.6 45.5 %gather_fusion.1 = s32[8192]{0:T(1024)S(1)} fusion(s32[2048]{0:T(1024)S(1)} %bitcast.34, s32[8192]{0:T(1024)S(1)} %broadcast_clamp_fusion), kind=kCustom, calls=%fused_computation.1 | custom fusion | bytes 98304 | tf_op jit(solution)/shard_map/jit(_take)/gather | solution.py:137
  105.2 0.2 copy.28
  105.3 0.2 reshape.103
  105.6 0.6 slice.292
  106.2 4.4 %all-gather.2.cloned.1.call-done = bf16[768,12,128]{2,0,1:T(8,128)(2,1)} async-done(((bf16[24,12,128]{2,0,1:T(8,128)(2,1)}), bf16[768,12,128]{2,0,1:T(8,128)(2,1)}) %all-gather.2.cloned.1.call-update) | async-done | bytes 2359312 | tf_op jit(solution)/shard_map/all_gather | solution.py:190
  110.6 4.9 %copy.31 = bf16[768,12,128]{2,1,0:T(8,128)(2,1)} copy(bf16[768,12,128]{2,0,1:T(8,128)(2,1)} %all-gather.2.cloned.1.call-done) | data formatting | bytes 4718592 | tf_op jit(solution)/shard_map/all_gather | solution.py:190
  115.5 2.7 %gather_fusion = bf16[256,12,128]{2,1,0:T(8,128)(2,1)S(1)} fusion(bf16[768,12,128]{2,1,0:T(8,128)(2,1)} %copy.31, s32[1024]{0:T(1024)S(1)} %pad_clamp_fusion), kind=kCustom, calls=%fused_computation | custom fusion | bytes 1573888 | tf_op jit(solution)/shard_map/gather | solution.py:191
  118.2 0.0 copy-done.4
  118.2 0.0 copy-start.5
  118.3 4.6 %fusion.10 = f32[64,128]{1,0:T(8,128)S(1)} fusion(bf16[64,4,12,128]{3,2,1,0:T(8,128)(2,1)S(1)} %bitcast.35, bf16[64,4,128,128]{3,2,1,0:T(8,128)(2,1)} %param.23, s32[64,128]{1,0:T(8,128)S(1)} %bitcast.44), kind=kOutput, calls=%fused_computation.13 | convolution fusion | flops 100950016 | bytes 9240576 | tf_op jit(solution)/shard_map/ptil,ptlq->piq/dot_general | solution.py:193
  122.9 0.0 copy-start.2
  122.9 0.3 multiply_multiply_fusion
  123.2 0.0 copy-done.5
  123.2 0.2 multiply_divide_fusion
  123.4 0.9 subtract_add_fusion
  124.4 0.0 copy-done.2
  (22 shorter events, 0.3 us)
Async XLA Ops:
  7.2 52.4 %copy-start = (s32[1,2048]{1,0:T(1,128)S(1)}, s32[1,2048]{1,0:T(1,128)}, u32[]{:S(2)}) copy-start(s32[1,2048]{1,0:T(1,128)} %param.21) | copy-start | bytes 24580
  7.2 18.2 %copy-start.11 = (u32[32]{0:T(128)S(1)}, u32[32]{0:T(128)}, u32[]{:S(2)}) copy-start(u32[32]{0:T(128)} %constant.80) | copy-start | bytes 388
  7.2 19.4 %copy-start.6 = (f32[4,3072]{1,0:T(4,128)S(1)}, f32[4,3072]{1,0:T(4,128)}, u32[]{:S(2)}) copy-start(f32[4,3072]{1,0:T(4,128)} %param.12) | copy-start | bytes 147460
  7.2 19.4 %copy-start.8 = (f32[3072]{0:T(1024)S(1)}, f32[3072]{0:T(1024)}, u32[]{:S(2)}) copy-start(f32[3072]{0:T(1024)} %param.13) | copy-start | bytes 36868
  7.2 19.4 %copy-start.7 = (f32[2,3072]{1,0:T(2,128)S(1)}, f32[2,3072]{1,0:T(2,128)}, u32[]{:S(2)}) copy-start(f32[2,3072]{1,0:T(2,128)} %param.15) | copy-start | bytes 73732
  7.2 103.3 %all-gather.2.cloned.1.call-start = ((), (), s32[]{:S(2)}) async-start(), calls=%async_computation | async-start | bytes 2433024 | tf_op jit(solution)/shard_map/all_gather | solution.py:190
  27.0 6.7 %collective-permute-start.1 = (f32[10,2048]{1,0:T(8,128)S(1)}, f32[10,2048]{1,0:T(8,128)S(1)}, u32[]{:S(2)}, u32[]{:S(2)}) collective-permute-start(f32[10,2048]{1,0:T(8,128)S(1)} %get-tuple-element.23), channel_id=1, source_target_pairs={{1,0},{2,1},{3,2},{4,3},{5,4},{6,5},{7,6},{8,7},{9,8},{10,9},{11,1... | collective-permute-start | bytes 245768 | tf_op jit(solution)/shard_map/ppermute | solution.py:31
  31.2 8.0 %collective-permute-start = (f32[10,2048]{1,0:T(8,128)S(1)}, f32[10,2048]{1,0:T(8,128)S(1)}, u32[]{:S(2)}, u32[]{:S(2)}) collective-permute-start(f32[10,2048]{1,0:T(8,128)S(1)} %get-tuple-element.22), channel_id=1, source_target_pairs={{0,1},{1,2},{2,3},{3,4},{4,5},{5,6},{6,7},{7,8},{8,9},{9,10},{10,1... | collective-permute-start | bytes 245768 | tf_op jit(solution)/shard_map/ppermute | solution.py:29
  39.2 19.4 %copy-start.9 = (f32[3072]{0:T(1024)S(1)}, f32[3072]{0:T(1024)}, u32[]{:S(2)}) copy-start(f32[3072]{0:T(1024)} %param.14) | copy-start | bytes 36868
  39.3 20.0 %copy-start.10 = (s32[64,4]{0,1:T(4,128)S(1)}, s32[64,4]{0,1:T(4,128)}, u32[]{:S(2)}) copy-start(s32[64,4]{0,1:T(4,128)} %param.22) | copy-start | bytes 3076
  39.3 20.2 %copy-start.1 = (s32[1,8192]{1,0:T(1,128)S(1)}, s32[1,8192]{1,0:T(1,128)}, u32[]{:S(2)}) copy-start(s32[1,8192]{1,0:T(1,128)} %param.20) | copy-start | bytes 98308
  59.6 45.6 %copy-start.3 = (f32[5,56,128]{2,1,0:T(8,128)S(1)}, f32[5,56,128]{2,1,0:T(8,128)}, u32[]{:S(2)}) copy-start(f32[5,56,128]{2,1,0:T(8,128)} %get-tuple-element.5) | copy-start | bytes 430084
  106.2 12.0 %copy-start.4 = (s32[8192]{0:T(1024)S(1)}, s32[8192]{0:T(1024)}, u32[]{:S(2)}) copy-start(s32[8192]{0:T(1024)} %param.19) | copy-start | bytes 98308
  118.2 5.0 %copy-start.5 = (f32[8192]{0:T(1024)S(1)}, f32[8192]{0:T(1024)}, u32[]{:S(2)}) copy-start(f32[8192]{0:T(1024)} %param.17) | copy-start | bytes 98308
  122.9 1.5 %copy-start.2 = (f32[8192]{0:T(1024)}, f32[8192]{0:T(1024)S(1)}, u32[]{:S(2)}) copy-start(f32[8192]{0:T(1024)S(1)} %multiply_bitcast_fusion) | copy-start | bytes 98308
Sparse Core Ops, SparseCore 0:
  59.4 51.1 all-gather.1

commit v2 on v1

--- a/solution.py
+++ b/solution.py
@@ -10,7 +10,7 @@
 ISTEPS = 5
 NI = 12
 OD_MOST = 8
-LINE = ("region", "route")
+LINE = ("z", "plane", "route")
 
 
 def halo_width(span):
@@ -132,9 +132,18 @@
     return total
 
 
+def pick_rate(rate_num, group):
+    count = rate_num.shape[0]
+    table = rate_num.reshape(count // 128, 128).astype(jnp.float32)
+    row_pick = ((group // 128)[:, None] == jnp.arange(count // 128)[None, :]).astype(jnp.float32)
+    picked = jnp.dot(row_pick, table, precision=lax.Precision.HIGHEST, preferred_element_type=jnp.float32)
+    lanes = jnp.arange(128, dtype=jnp.int32)
+    return jnp.sum(jnp.where((group % 128)[:, None] == lanes[None, :], picked, 0.0), axis=1)
+
+
 def swap_flows(cost, flow, group, rate_num):
     best = group_min(cost, group)
-    rate = jnp.take(rate_num, group).astype(jnp.float32) / 16.0
+    rate = pick_rate(rate_num, group) / 16.0
     moved = rate * flow * (cost - best) / cost
     pull = (best / cost) ** 4
     return flow - moved + group_sum(moved, group) * pull / group_sum(pull, group)
@@ -187,7 +196,8 @@
     link_cost = costs.astype(jnp.bfloat16)
     tiles = link_cost.reshape(NI, span // 128, 128).transpose(1, 0, 2)
     wanted_tiles = tile_index.reshape(-1)
-    every_tile = lax.all_gather(tiles, LINE, axis=0, tiled=True)
+    every_tile = lax.all_gather(tiles, ("plane", "route"), axis=0, tiled=True)
+    every_tile = lax.all_gather(every_tile, "z", axis=0, tiled=True)
     fetched = every_tile[wanted_tiles]
     fetched = fetched.reshape(tile_index.shape[0], tile_index.shape[1], NI, 128)
     totals = jnp.einsum("ptil,ptlq->piq", fetched, incidence, preferred_element_type=jnp.float32)
@@ -196,10 +206,22 @@
     return (state, path_cost, new_flow)
 
 
+def z_count(devices):
+    try:
+        return len({d.coords[2] for d in devices.flat})
+    except (AttributeError, IndexError, TypeError):
+        return 4
+
+
 def solution(mesh):
+    devices = mesh.devices
+    count = z_count(devices)
+    split = jax.sharding.Mesh(
+        devices.reshape(count, devices.shape[0] // count, devices.shape[1]), LINE
+    )
     return jax.shard_map(
         body,
-        mesh=mesh,
+        mesh=split,
         in_specs=(
             P(None, LINE),
             P(LINE),

time: 132 us -> 139 us (1.053)
  local copies, waits for them, and re-layouts: 60 us -> 13.9 us
  waiting for transfers between devices: 12.4 us -> 52.7 us
  blocking collectives: 13.2 us -> 23.7 us
  matrix products: 7.92 us -> 10.1 us
    gather x1 -> x0, local copies, waits for them, and re-layouts: 45.5 us -> none  [swap_flows(): rate = jnp.take(rate_num, group).astype(jnp.float32) / 16.0]
    all_gather x1, waiting for transfers between devices: 4.37 us -> 44.7 us  [body(): every_tile = lax.all_gather(every_tile, 'z', axis=0, tiled=True)]
    all_gather x0 -> x1, blocking collectives: none -> 10.5 us  [body(): every_tile = lax.all_gather(tiles, ('plane', 'route'), axis=0, tiled=True)]
    dot_general x0 -> x1, matrix products: none -> 2.21 us  [pick_rate(): jnp.dot(row_pick, table, precision=lax.Precision.HIGHEST, preferred_eleme...]
  transfers between devices with their start and end apart: 3 -> 3, of which waited for: 3 -> 3; matrix products, arithmetic and copies ran while one was open for 36% -> 3% of each run, Pallas kernels for 0% -> 0%
where the time goes in v2:
time: 139 us; the launch traced here: 138 us
  waiting for transfers between devices  52.7 us (38%)
  blocking collectives  23.7 us (17%)
  Pallas kernels  15.2 us (11%)
  between operations  15.1 us (11%)
  local copies, waits for them, and re-layouts  13.9 us (10%)
  matrix products  10.1 us (7%)
  starting transfers between devices  4.24 us (3%)
  other arithmetic  3.17 us (2%)
    all_gather x1, waiting for transfers between devices, body(): every_tile = lax.all_gather(every_tile, 'z', axis=0, tiled=True)  44.7 us
    pallas_call x1, Pallas kernels, simulate(): pl.pallas_call(sim_kernel, out_shape=(jax.ShapeDtypeStruct((count, rows,...  15.2 us
    unnamed x1, blocking collectives  13.2 us
    all_gather x1, blocking collectives, body(): every_tile = lax.all_gather(tiles, ('plane', 'route'), axis=0, tiled=True)  10.5 us
    ppermute x1, waiting for transfers between devices, padded(): lax.ppermute(tail, LINE, [(i, (i + 1) % count) for i in range(count)])  5.47 us
    all_gather x1, local copies, waits for them, and re-layouts, body(): every_tile = lax.all_gather(every_tile, 'z', axis=0, tiled=True)  4.92 us
    dot_general x1, matrix products, body(): jnp.einsum('ptil,ptlq->piq', fetched, incidence, preferred_element_type=j...  4.6 us
    ppermute x1, starting transfers between devices, padded(): lax.ppermute(head, LINE, [((i + 1) % count, i) for i in range(count)])  4.2 us
  transfers between devices with their start and end apart: 3, of which 3 were waited for; matrix products, arithmetic and copies ran while one was open for 3% of the time, Pallas kernels for 0%

profile of v2, /device:TPU:0, one launch (start us, length us, event | category | flops | bytes accessed | tf_op | source)
XLA Modules:
  0.0 138.1 jit_solution(2305806845312829249)
XLA Ops:
  7.2 0.0 copy-start.11
  7.2 0.0 copy-start.5
  7.2 0.0 copy-start.7
  7.2 0.0 copy-start.6
  7.2 0.0 all-gather.2.cloned.1.call-start
  7.3 0.7 convert_element_type.17
  8.0 0.8 add_select_fusion.3
  8.8 3.3 %fusion.2 = f32[12288]{0:T(1024)S(1)} fusion(s32[8192]{0:T(1024)S(1)} %get-tuple-element.27, f32[8192]{0:T(1024)} %param.17, s32[8192]{0:T(1024)S(1)} %get-tuple-element.26), kind=kOutput, calls=%fused_computation.7 | convolution fusion | flops 1210580992 | bytes 147456 | tf_op jit(solution)/shard_map/dot_general | solution.py:178
  12.1 0.0 copy-start.8
  12.1 13.2 %all-reduce.5 = f32[12288]{0:T(1024)S(1)} all-reduce(f32[12288]{0:T(1024)S(1)} %fusion.2), channel_id=2, replica_groups=mesh['z'=4,'plane'=2,'route'=4] {'route'}, use_global_device_ids=true, to_apply=%region_0.1.clone | all-reduce | flops 12288 | bytes 98304
  25.3 0.0 copy-done.11
  25.4 0.6 dynamic-slice
  26.6 0.3 concatenate.9
  27.0 4.2 %collective-permute-start.1 = (f32[10,2048]{1,0:T(8,128)S(1)}, f32[10,2048]{1,0:T(8,128)S(1)}, u32[]{:S(2)}, u32[]{:S(2)}) collective-permute-start(f32[10,2048]{1,0:T(8,128)S(1)} %get-tuple-element.23), channel_id=1, source_target_pairs={{1,0},{2,1},{3,2},{4,3},{5,4},{6,5},{7,6},{8,7},{9,8},{10,9},{11,1... | collective-permute-start | bytes 245768 | tf_op jit(solution)/shard_map/ppermute | solution.py:31
  31.1 0.0 collective-permute-start
  31.2 2.5 %collective-permute-done.1 = f32[10,2048]{1,0:T(8,128)S(1)} collective-permute-done((f32[10,2048]{1,0:T(8,128)S(1)}, f32[10,2048]{1,0:T(8,128)S(1)}, u32[]{:S(2)}, u32[]{:S(2)}) %collective-permute-start.1) | collective-permute-done | bytes 81952 | tf_op jit(solution)/shard_map/ppermute | solution.py:31
  33.7 5.5 %collective-permute-done = f32[10,2048]{1,0:T(8,128)S(1)} collective-permute-done((f32[10,2048]{1,0:T(8,128)S(1)}, f32[10,2048]{1,0:T(8,128)S(1)}, u32[]{:S(2)}, u32[]{:S(2)}) %collective-permute-start) | collective-permute-done | bytes 81952 | tf_op jit(solution)/shard_map/ppermute | solution.py:29
  39.2 0.0 copy-start.10
  39.2 0.0 copy-start.9
  39.2 0.0 copy-start.4
  39.3 0.3 reshape.117
  39.6 0.8 copy.32
  40.4 0.3 reshape.118
  40.8 0.8 copy.33
  41.6 15.2 %shard_map.139 = (f32[12,56,128]{2,1,0:T(8,128)}, f32[5,56,128]{2,1,0:T(8,128)}) custom-call(f32[5,56,128]{2,1,0:T(8,128)} %bitcast.34, f32[6,56,128]{2,1,0:T(8,128)} %bitcast.33), custom_call_target="tpu_custom_call" | custom-call | tf_op jit(solution)/shard_map/pallas_call | solution.py:96
  56.8 1.3 copy.35
  58.1 0.5 reshape.120
  58.6 10.5 %all_gather.6 = bf16[192,12,128]{2,0,1:T(8,128)(2,1)} all-gather(bf16[24,12,128]{2,0,1:T(8,128)(2,1)S(1)} %slice_bitcast_fusion), channel_id=1, replica_groups=mesh['z'=4,'plane'=2,'route'=4] {'plane','route'}, dimensions={0}, use_global_device_ids=true | all-gather | bytes 663552 | tf_op jit(solution)/shard_map/all_gather | solution.py:199
  69.2 0.0 all-gather.2.cloned.1.call-update
  69.2 0.0 copy-done.10
  69.2 0.1 copy.36
  69.3 0.1 reshape.122
  69.4 0.0 copy-done.9
  69.5 2.2 %fusion.6 = f32[8192]{0:T(1024)S(1)} fusion(f32[16,128]{1,0:T(8,128)S(1)} %bitcast.45, s32[8192]{0:T(1024)S(1)} %get-tuple-element.25, s32[8192]{0:T(1024)S(1)} %get-tuple-element.24), kind=kOutput, calls=%fused_computation.9 | convolution fusion | flops 204595200 | bytes 106496 | tf_op jit(solution)/shard_map/dot_general | solution.py:139
  71.7 0.0 copy-done.1
  71.7 0.2 copy.34
  71.9 0.0 copy-start.2
  71.9 0.2 reshape.119
  72.1 0.6 slice.290
  72.8 44.7 %all-gather.2.cloned.1.call-done = bf16[768,12,128]{2,0,1:T(8,128)(2,1)} async-done(((bf16[192,12,128]{2,0,1:T(8,128)(2,1)}), bf16[768,12,128]{2,0,1:T(8,128)(2,1)}) %all-gather.2.cloned.1.call-update) | async-done | bytes 2359312 | tf_op jit(solution)/shard_map/all_gather | solution.py:200
  117.5 4.9 %copy.37 = bf16[768,12,128]{2,1,0:T(8,128)(2,1)} copy(bf16[768,12,128]{2,0,1:T(8,128)(2,1)} %all-gather.2.cloned.1.call-done) | data formatting | bytes 4718592 | tf_op jit(solution)/shard_map/all_gather | solution.py:200
  122.4 2.7 %gather_fusion = bf16[256,12,128]{2,1,0:T(8,128)(2,1)S(1)} fusion(bf16[768,12,128]{2,1,0:T(8,128)(2,1)} %copy.37, s32[1024]{0:T(1024)S(1)} %pad_clamp_fusion), kind=kCustom, calls=%fused_computation | custom fusion | bytes 1573888 | tf_op jit(solution)/shard_map/gather | solution.py:201
  125.1 0.0 copy-start.3
  125.1 4.6 %fusion.11 = f32[64,128]{1,0:T(8,128)S(1)} fusion(bf16[64,4,12,128]{3,2,1,0:T(8,128)(2,1)S(1)} %bitcast.32, bf16[64,4,128,128]{3,2,1,0:T(8,128)(2,1)} %param.23, s32[64,128]{1,0:T(8,128)S(1)} %bitcast.39), kind=kOutput, calls=%fused_computation.15 | convolution fusion | flops 100950016 | bytes 9240576 | tf_op jit(solution)/shard_map/ptil,ptlq->piq/dot_general | solution.py:203
  129.8 0.0 copy-start
  129.8 0.3 multiply_multiply_fusion
  130.1 0.2 multiply_divide_fusion
  130.3 0.9 subtract_add_fusion
  (23 shorter events, 0.3 us)
Async XLA Ops:
  7.2 18.2 %copy-start.11 = (u32[32]{0:T(128)S(1)}, u32[32]{0:T(128)}, u32[]{:S(2)}) copy-start(u32[32]{0:T(128)} %constant.77) | copy-start | bytes 388
  7.2 19.4 %copy-start.5 = (f32[4,3072]{1,0:T(4,128)S(1)}, f32[4,3072]{1,0:T(4,128)}, u32[]{:S(2)}) copy-start(f32[4,3072]{1,0:T(4,128)} %param.12) | copy-start | bytes 147460
  7.2 19.4 %copy-start.7 = (f32[3072]{0:T(1024)S(1)}, f32[3072]{0:T(1024)}, u32[]{:S(2)}) copy-start(f32[3072]{0:T(1024)} %param.13) | copy-start | bytes 36868
  7.2 19.4 %copy-start.6 = (f32[2,3072]{1,0:T(2,128)S(1)}, f32[2,3072]{1,0:T(2,128)}, u32[]{:S(2)}) copy-start(f32[2,3072]{1,0:T(2,128)} %param.15) | copy-start | bytes 73732
  7.2 110.3 %all-gather.2.cloned.1.call-start = ((), (), s32[]{:S(2)}) async-start(), calls=%async_computation | async-start | bytes 2949120 | tf_op jit(solution)/shard_map/all_gather | solution.py:200
  12.1 46.5 %copy-start.8 = (f32[3072]{0:T(1024)S(1)}, f32[3072]{0:T(1024)}, u32[]{:S(2)}) copy-start(f32[3072]{0:T(1024)} %param.14) | copy-start | bytes 36868
  27.0 6.7 %collective-permute-start.1 = (f32[10,2048]{1,0:T(8,128)S(1)}, f32[10,2048]{1,0:T(8,128)S(1)}, u32[]{:S(2)}, u32[]{:S(2)}) collective-permute-start(f32[10,2048]{1,0:T(8,128)S(1)} %get-tuple-element.23), channel_id=1, source_target_pairs={{1,0},{2,1},{3,2},{4,3},{5,4},{6,5},{7,6},{8,7},{9,8},{10,9},{11,1... | collective-permute-start | bytes 245768 | tf_op jit(solution)/shard_map/ppermute | solution.py:31
  31.1 8.0 %collective-permute-start = (f32[10,2048]{1,0:T(8,128)S(1)}, f32[10,2048]{1,0:T(8,128)S(1)}, u32[]{:S(2)}, u32[]{:S(2)}) collective-permute-start(f32[10,2048]{1,0:T(8,128)S(1)} %get-tuple-element.22), channel_id=1, source_target_pairs={{0,1},{1,2},{2,3},{3,4},{4,5},{5,6},{6,7},{7,8},{8,9},{9,10},{10,1... | collective-permute-start | bytes 245768 | tf_op jit(solution)/shard_map/ppermute | solution.py:29
  39.2 30.0 %copy-start.10 = (s32[64,4]{0,1:T(4,128)S(1)}, s32[64,4]{0,1:T(4,128)}, u32[]{:S(2)}) copy-start(s32[64,4]{0,1:T(4,128)} %param.22) | copy-start | bytes 3076
  39.2 30.2 %copy-start.9 = (s32[1,2048]{1,0:T(1,128)S(1)}, s32[1,2048]{1,0:T(1,128)}, u32[]{:S(2)}) copy-start(s32[1,2048]{1,0:T(1,128)} %param.21) | copy-start | bytes 24580
  39.2 30.2 %copy-start.4 = (s32[1,8192]{1,0:T(1,128)S(1)}, s32[1,8192]{1,0:T(1,128)}, u32[]{:S(2)}) copy-start(s32[1,8192]{1,0:T(1,128)} %param.20) | copy-start | bytes 98308
  56.8 14.9 %copy-start.1 = (f32[5,56,128]{2,1,0:T(8,128)S(1)}, f32[5,56,128]{2,1,0:T(8,128)}, u32[]{:S(2)}) copy-start(f32[5,56,128]{2,1,0:T(8,128)} %get-tuple-element.5) | copy-start | bytes 430084
  71.9 53.2 %copy-start.2 = (s32[8192]{0:T(1024)S(1)}, s32[8192]{0:T(1024)}, u32[]{:S(2)}) copy-start(s32[8192]{0:T(1024)} %param.19) | copy-start | bytes 98308
  125.1 5.0 %copy-start.3 = (f32[8192]{0:T(1024)S(1)}, f32[8192]{0:T(1024)}, u32[]{:S(2)}) copy-start(f32[8192]{0:T(1024)} %param.17) | copy-start | bytes 98308
  129.8 1.5 %copy-start = (f32[8192]{0:T(1024)}, f32[8192]{0:T(1024)S(1)}, u32[]{:S(2)}) copy-start(f32[8192]{0:T(1024)S(1)} %multiply_bitcast_fusion) | copy-start | bytes 98308
Sparse Core Ops, SparseCore 0:
  69.3 48.1 all-gather.1

commit v3 on v2

--- a/solution.py
+++ b/solution.py
@@ -141,9 +141,8 @@
     return jnp.sum(jnp.where((group % 128)[:, None] == lanes[None, :], picked, 0.0), axis=1)
 
 
-def swap_flows(cost, flow, group, rate_num):
+def swap_flows(cost, flow, group, rate):
     best = group_min(cost, group)
-    rate = pick_rate(rate_num, group) / 16.0
     moved = rate * flow * (cost - best) / cost
     pull = (best / cost) ** 4
     return flow - moved + group_sum(moved, group) * pull / group_sum(pull, group)
@@ -194,15 +193,15 @@
     costs = free_time + occ / ISTEPS
 
     link_cost = costs.astype(jnp.bfloat16)
-    tiles = link_cost.reshape(NI, span // 128, 128).transpose(1, 0, 2)
+    tiles = link_cost.reshape(NI, span // 128, 128).transpose(1, 0, 2).reshape(span // 128, NI * 128)
     wanted_tiles = tile_index.reshape(-1)
-    every_tile = lax.all_gather(tiles, ("plane", "route"), axis=0, tiled=True)
-    every_tile = lax.all_gather(every_tile, "z", axis=0, tiled=True)
+    rate = pick_rate(swap_rate[0], od_pair[0]) / 16.0
+    every_tile = lax.all_gather(tiles, LINE, axis=0, tiled=True)
     fetched = every_tile[wanted_tiles]
     fetched = fetched.reshape(tile_index.shape[0], tile_index.shape[1], NI, 128)
     totals = jnp.einsum("ptil,ptlq->piq", fetched, incidence, preferred_element_type=jnp.float32)
     path_cost = select_depart(totals, depart.reshape(-1, 128)).reshape(-1) / 256.0
-    new_flow = swap_flows(path_cost, path_flow, od_pair[0], swap_rate[0])
+    new_flow = swap_flows(path_cost, path_flow, od_pair[0], rate)
     return (state, path_cost, new_flow)
 
 

time: 139 us -> 130 us (0.935)
  blocking collectives: 23.7 us -> 13.2 us
  waiting for transfers between devices: 52.7 us -> 57.7 us
  local copies, waits for them, and re-layouts: 13.9 us -> 11.4 us
    all_gather x1 -> x0, blocking collectives: 10.5 us -> none  [body(): every_tile = lax.all_gather(tiles, ('plane', 'route'), axis=0, tiled=True)]
    all_gather x1, waiting for transfers between devices: 44.7 us -> 49.7 us  [body(): every_tile = lax.all_gather(tiles, LINE, axis=0, tiled=True)]
    all_gather x1 -> x0, local copies, waits for them, and re-layouts: 4.92 us -> none  [body(): every_tile = lax.all_gather(every_tile, 'z', axis=0, tiled=True)]
where the time goes in v3:
time: 130 us
  waiting for transfers between devices  57.7 us (44%)
  Pallas kernels  15.2 us (12%)
  between operations  15 us (12%)
  blocking collectives  13.2 us (10%)
  local copies, waits for them, and re-layouts  11.4 us (9%)
  matrix products  10.1 us (8%)
  starting transfers between devices  4.24 us (3%)
  other arithmetic  3.16 us (2%)
    all_gather x1, waiting for transfers between devices, body(): every_tile = lax.all_gather(tiles, LINE, axis=0, tiled=True)  49.7 us
    pallas_call x1, Pallas kernels, simulate(): pl.pallas_call(sim_kernel, out_shape=(jax.ShapeDtypeStruct((count, rows,...  15.2 us
    unnamed x1, blocking collectives  13.2 us
    ppermute x1, waiting for transfers between devices, padded(): lax.ppermute(tail, LINE, [(i, (i + 1) % count) for i in range(count)])  5.47 us
    dot_general x1, matrix products, body(): jnp.einsum('ptil,ptlq->piq', fetched, incidence, preferred_element_type=j...  4.6 us
    ppermute x1, starting transfers between devices, padded(): lax.ppermute(head, LINE, [((i + 1) % count, i) for i in range(count)])  4.2 us
    gather x1, local copies, waits for them, and re-layouts, body(): fetched = every_tile[wanted_tiles]  3.96 us
    dot_general x1, matrix products, body(): jnp.dot(tile_pick, lane_pick, precision=lax.Precision.HIGHEST, preferred_...  3.3 us
  transfers between devices with their start and end apart: 3, of which 3 were waited for; matrix products, arithmetic and copies ran while one was open for 3% of the time, Pallas kernels for 0%

profile of v3, /device:TPU:0, one launch (start us, length us, event | category | flops | bytes accessed | tf_op | source)
XLA Modules:
  0.0 130.0 jit_solution(12047705342325761976)
XLA Ops:
  7.2 0.0 copy-start.11
  7.2 0.0 copy-start.5
  7.2 0.0 copy-start.7
  7.2 0.0 copy-start.6
  7.2 0.0 all-gather.2.cloned.1.call-start
  7.3 0.7 convert_element_type.17
  8.0 0.8 add_select_fusion.3
  8.8 3.3 %fusion.2 = f32[12288]{0:T(1024)S(1)} fusion(s32[8192]{0:T(1024)S(1)} %get-tuple-element.27, f32[8192]{0:T(1024)} %param.17, s32[8192]{0:T(1024)S(1)} %get-tuple-element.26), kind=kOutput, calls=%fused_computation.7 | convolution fusion | flops 1210580992 | bytes 147456 | tf_op jit(solution)/shard_map/dot_general | solution.py:177
  12.1 0.0 copy-start.8
  12.1 13.2 %all-reduce.5 = f32[12288]{0:T(1024)S(1)} all-reduce(f32[12288]{0:T(1024)S(1)} %fusion.2), channel_id=2, replica_groups=mesh['z'=4,'plane'=2,'route'=4] {'route'}, use_global_device_ids=true, to_apply=%region_0.1.clone | all-reduce | flops 12288 | bytes 98304
  25.3 0.0 copy-done.11
  25.4 0.6 dynamic-slice
  26.6 0.0 copy-done.5
  26.6 0.0 copy-done.7
  26.6 0.0 copy-done.6
  26.6 0.3 concatenate.9
  26.9 0.0 copy-start.10
  26.9 0.0 copy-start.9
  26.9 0.0 copy-start.4
  27.0 4.2 %collective-permute-start.1 = (f32[10,2048]{1,0:T(8,128)S(1)}, f32[10,2048]{1,0:T(8,128)S(1)}, u32[]{:S(2)}, u32[]{:S(2)}) collective-permute-start(f32[10,2048]{1,0:T(8,128)S(1)} %get-tuple-element.23), channel_id=1, source_target_pairs={{1,0},{2,1},{3,2},{4,3},{5,4},{6,5},{7,6},{8,7},{9,8},{10,9},{11,1... | collective-permute-start | bytes 245768 | tf_op jit(solution)/shard_map/ppermute | solution.py:31
  31.2 0.0 collective-permute-start
  31.2 2.5 %collective-permute-done.1 = f32[10,2048]{1,0:T(8,128)S(1)} collective-permute-done((f32[10,2048]{1,0:T(8,128)S(1)}, f32[10,2048]{1,0:T(8,128)S(1)}, u32[]{:S(2)}, u32[]{:S(2)}) %collective-permute-start.1) | collective-permute-done | bytes 81952 | tf_op jit(solution)/shard_map/ppermute | solution.py:31
  33.7 5.5 %collective-permute-done = f32[10,2048]{1,0:T(8,128)S(1)} collective-permute-done((f32[10,2048]{1,0:T(8,128)S(1)}, f32[10,2048]{1,0:T(8,128)S(1)}, u32[]{:S(2)}, u32[]{:S(2)}) %collective-permute-start) | collective-permute-done | bytes 81952 | tf_op jit(solution)/shard_map/ppermute | solution.py:29
  39.3 0.3 reshape.120
  39.6 0.8 copy.27
  40.4 0.3 reshape.121
  40.8 0.8 copy.28
  41.6 15.2 %shard_map.139 = (f32[12,56,128]{2,1,0:T(8,128)}, f32[5,56,128]{2,1,0:T(8,128)}) custom-call(f32[5,56,128]{2,1,0:T(8,128)} %bitcast.36, f32[6,56,128]{2,1,0:T(8,128)} %bitcast.35), custom_call_target="tpu_custom_call" | custom-call | tf_op jit(solution)/shard_map/pallas_call | solution.py:96
  56.8 1.3 copy.30
  58.1 0.5 reshape.123
  58.6 0.0 copy-done.8
  58.6 0.6 copy_bitcast_fusion
  59.2 0.0 all-gather.2.cloned.1.call-update
  59.3 0.1 copy.32
  59.4 0.1 reshape.126
  59.6 2.2 %fusion.6 = f32[8192]{0:T(1024)S(1)} fusion(f32[16,128]{1,0:T(8,128)S(1)} %bitcast.47, s32[8192]{0:T(1024)S(1)} %get-tuple-element.25, s32[8192]{0:T(1024)S(1)} %get-tuple-element.24), kind=kOutput, calls=%fused_computation.9 | convolution fusion | flops 204595200 | bytes 106496 | tf_op jit(solution)/shard_map/dot_general | solution.py:139
  61.8 0.2 copy.29
  62.0 0.2 reshape.122
  62.2 0.6 slice.290
  62.9 49.7 %all-gather.2.cloned.1.call-done = bf16[768,1536]{1,0:T(8,128)(2,1)} async-done(((bf16[24,1536]{1,0:T(8,128)(2,1)}), bf16[768,1536]{1,0:T(8,128)(2,1)}) %all-gather.2.cloned.1.call-update) | async-done | bytes 2359312 | tf_op jit(solution)/shard_map/all_gather | solution.py:199
  112.5 4.0 %gather_fusion = bf16[256,1536]{1,0:T(8,128)(2,1)S(1)} fusion(bf16[768,1536]{1,0:T(8,128)(2,1)} %all-gather.2.cloned.1.call-done, s32[1024]{0:T(1024)S(1)} %pad_clamp_fusion), kind=kCustom, calls=%fused_computation | custom fusion | bytes 1573888 | tf_op jit(solution)/shard_map/gather | solution.py:200
  116.5 0.5 reshape.127
  117.1 0.0 copy-start.3
  117.1 4.6 %fusion.11 = f32[64,128]{1,0:T(8,128)S(1)} fusion(bf16[64,4,12,128]{3,2,1,0:T(8,128)(2,1)S(1)} %reshape.127, bf16[64,4,128,128]{3,2,1,0:T(8,128)(2,1)} %param.23, s32[64,128]{1,0:T(8,128)S(1)} %bitcast.41), kind=kOutput, calls=%fused_computation.15 | convolution fusion | flops 100950016 | bytes 9240576 | tf_op jit(solution)/shard_map/ptil,ptlq->piq/dot_general | solution.py:202
  121.7 0.0 copy-start
  121.7 0.3 multiply_multiply_fusion
  122.0 0.2 multiply_divide_fusion
  122.2 0.9 subtract_add_fusion
  (22 shorter events, 0.3 us)
Async XLA Ops:
  7.2 18.2 %copy-start.11 = (u32[32]{0:T(128)S(1)}, u32[32]{0:T(128)}, u32[]{:S(2)}) copy-start(u32[32]{0:T(128)} %constant.77) | copy-start | bytes 388
  7.2 19.4 %copy-start.5 = (f32[4,3072]{1,0:T(4,128)S(1)}, f32[4,3072]{1,0:T(4,128)}, u32[]{:S(2)}) copy-start(f32[4,3072]{1,0:T(4,128)} %param.12) | copy-start | bytes 147460
  7.2 19.4 %copy-start.7 = (f32[3072]{0:T(1024)S(1)}, f32[3072]{0:T(1024)}, u32[]{:S(2)}) copy-start(f32[3072]{0:T(1024)} %param.13) | copy-start | bytes 36868
  7.2 19.4 %copy-start.6 = (f32[2,3072]{1,0:T(2,128)S(1)}, f32[2,3072]{1,0:T(2,128)}, u32[]{:S(2)}) copy-start(f32[2,3072]{1,0:T(2,128)} %param.15) | copy-start | bytes 73732
  7.2 105.3 %all-gather.2.cloned.1.call-start = ((), (), s32[]{:S(2)}) async-start(), calls=%async_computation | async-start | bytes 2433024 | tf_op jit(solution)/shard_map/all_gather | solution.py:199
  12.1 46.4 %copy-start.8 = (f32[3072]{0:T(1024)S(1)}, f32[3072]{0:T(1024)}, u32[]{:S(2)}) copy-start(f32[3072]{0:T(1024)} %param.14) | copy-start | bytes 36868
  26.9 32.3 %copy-start.10 = (s32[64,4]{0,1:T(4,128)S(1)}, s32[64,4]{0,1:T(4,128)}, u32[]{:S(2)}) copy-start(s32[64,4]{0,1:T(4,128)} %param.22) | copy-start | bytes 3076
  26.9 32.5 %copy-start.9 = (s32[1,2048]{1,0:T(1,128)S(1)}, s32[1,2048]{1,0:T(1,128)}, u32[]{:S(2)}) copy-start(s32[1,2048]{1,0:T(1,128)} %param.21) | copy-start | bytes 24580
  26.9 32.6 %copy-start.4 = (s32[1,8192]{1,0:T(1,128)S(1)}, s32[1,8192]{1,0:T(1,128)}, u32[]{:S(2)}) copy-start(s32[1,8192]{1,0:T(1,128)} %param.20) | copy-start | bytes 98308
  27.0 6.7 %collective-permute-start.1 = (f32[10,2048]{1,0:T(8,128)S(1)}, f32[10,2048]{1,0:T(8,128)S(1)}, u32[]{:S(2)}, u32[]{:S(2)}) collective-permute-start(f32[10,2048]{1,0:T(8,128)S(1)} %get-tuple-element.23), channel_id=1, source_target_pairs={{1,0},{2,1},{3,2},{4,3},{5,4},{6,5},{7,6},{8,7},{9,8},{10,9},{11,1... | collective-permute-start | bytes 245768 | tf_op jit(solution)/shard_map/ppermute | solution.py:31
  31.2 8.0 %collective-permute-start = (f32[10,2048]{1,0:T(8,128)S(1)}, f32[10,2048]{1,0:T(8,128)S(1)}, u32[]{:S(2)}, u32[]{:S(2)}) collective-permute-start(f32[10,2048]{1,0:T(8,128)S(1)} %get-tuple-element.22), channel_id=1, source_target_pairs={{0,1},{1,2},{2,3},{3,4},{4,5},{5,6},{6,7},{7,8},{8,9},{9,10},{10,1... | collective-permute-start | bytes 245768 | tf_op jit(solution)/shard_map/ppermute | solution.py:29
  56.8 5.0 %copy-start.1 = (f32[5,56,128]{2,1,0:T(8,128)S(1)}, f32[5,56,128]{2,1,0:T(8,128)}, u32[]{:S(2)}) copy-start(f32[5,56,128]{2,1,0:T(8,128)} %get-tuple-element.5) | copy-start | bytes 430084
  62.9 54.2 %copy-start.2 = (s32[8192]{0:T(1024)S(1)}, s32[8192]{0:T(1024)}, u32[]{:S(2)}) copy-start(s32[8192]{0:T(1024)} %param.19) | copy-start | bytes 98308
  117.1 5.0 %copy-start.3 = (f32[8192]{0:T(1024)S(1)}, f32[8192]{0:T(1024)}, u32[]{:S(2)}) copy-start(f32[8192]{0:T(1024)} %param.17) | copy-start | bytes 98308
  121.7 1.5 %copy-start = (f32[8192]{0:T(1024)}, f32[8192]{0:T(1024)S(1)}, u32[]{:S(2)}) copy-start(f32[8192]{0:T(1024)S(1)} %multiply_bitcast_fusion) | copy-start | bytes 98308
Sparse Core Ops, SparseCore 0:
  59.4 53.0 all-gather.1

commit v4 on v3

--- a/solution.py
+++ b/solution.py
@@ -196,7 +196,19 @@
     tiles = link_cost.reshape(NI, span // 128, 128).transpose(1, 0, 2).reshape(span // 128, NI * 128)
     wanted_tiles = tile_index.reshape(-1)
     rate = pick_rate(swap_rate[0], od_pair[0]) / 16.0
-    every_tile = lax.all_gather(tiles, LINE, axis=0, tiled=True)
+    every_tile = lax.all_gather(tiles, "z", axis=0, tiled=True)
+    piece = every_tile.shape[1] // 3
+    every_tile = jnp.concatenate(
+        [
+            lax.all_gather(every_tile[:, c * piece : (c + 1) * piece], ("plane", "route"), axis=0, tiled=True)
+            for c in range(3)
+        ],
+        1,
+    )
+    own = tiles.shape[0]
+    planes = lax.axis_size(("plane", "route"))
+    device = wanted_tiles // own
+    wanted_tiles = (device % planes) * (lax.axis_size("z") * own) + (device // planes) * own + wanted_tiles % own
     fetched = every_tile[wanted_tiles]
     fetched = fetched.reshape(tile_index.shape[0], tile_index.shape[1], NI, 128)
     totals = jnp.einsum("ptil,ptlq->piq", fetched, incidence, preferred_element_type=jnp.float32)

time: 130 us -> 106 us (0.82)
  waiting for transfers between devices: 57.7 us -> 4.96 us
  blocking collectives: 13.2 us -> 56.6 us
  between operations: 15 us -> 1.68 us
  local copies, waits for them, and re-layouts: 11.4 us -> 9.38 us
    all_gather x1 -> x0, waiting for transfers between devices: 49.7 us -> none  [body(): every_tile = lax.all_gather(tiles, LINE, axis=0, tiled=True)]
    all_gather x0 -> x4, blocking collectives: none -> 43.3 us  [the longest x3 29.4 us: body(): lax.all_gather(every_tile[:, c * piece:(c + 1) * piece], ('plane', 'route...]
    gather x1, local copies, waits for them, and re-layouts: 3.96 us -> 1.26 us  [body(): fetched = every_tile[wanted_tiles]]
    ppermute x1, waiting for transfers between devices: 2.52 us -> 0.01 us  [padded(): lax.ppermute(head, LINE, [((i + 1) % count, i) for i in range(count)])]
  transfers between devices with their start and end apart: 3 -> 2, of which waited for: 3 -> 1; matrix products, arithmetic and copies ran while one was open for 3% -> 3% of each run, Pallas kernels for 0% -> 0%
where the time goes in v4:
time: 106 us; the launch traced here: 105 us
  blocking collectives  56.6 us (53%)
  Pallas kernels  15.2 us (14%)
  matrix products  10.1 us (10%)
  local copies, waits for them, and re-layouts  9.38 us (9%)
  waiting for transfers between devices  4.96 us (5%)
  starting transfers between devices  4.19 us (4%)
  other arithmetic  3.39 us (3%)
  between operations  1.68 us (2%)
    all_gather x3, blocking collectives, body(): lax.all_gather(every_tile[:, c * piece:(c + 1) * piece], ('plane', 'route...  29.4 us
    pallas_call x1, Pallas kernels, simulate(): pl.pallas_call(sim_kernel, out_shape=(jax.ShapeDtypeStruct((count, rows,...  15.2 us
    all_gather x1, blocking collectives, body(): every_tile = lax.all_gather(tiles, 'z', axis=0, tiled=True)  13.9 us
    unnamed x1, blocking collectives  13.2 us
    ppermute x1, waiting for transfers between devices, padded(): lax.ppermute(tail, LINE, [(i, (i + 1) % count) for i in range(count)])  4.96 us
    dot_general x1, matrix products, body(): jnp.einsum('ptil,ptlq->piq', fetched, incidence, preferred_element_type=j...  4.6 us
    ppermute x1, starting transfers between devices, padded(): lax.ppermute(head, LINE, [((i + 1) % count, i) for i in range(count)])  4.19 us
    dot_general x1, matrix products, body(): jnp.dot(tile_pick, lane_pick, precision=lax.Precision.HIGHEST, preferred_...  3.3 us
  transfers between devices with their start and end apart: 2, of which 1 were waited for; matrix products, arithmetic and copies ran while one was open for 3% of the time, Pallas kernels for 0%

profile of v4, /device:TPU:0, one launch (start us, length us, event | category | flops | bytes accessed | tf_op | source)
XLA Modules:
  0.0 105.5 jit_solution(10751700425739895915)
XLA Ops:
  0.6 0.0 copy-start.10
  0.6 0.0 copy-start.4
  0.7 0.0 copy-start.6
  0.7 0.0 copy-start.5
  0.7 0.0 copy-start.8
  0.7 0.0 copy-start.9
  0.7 0.8 convert_element_type.17
  1.5 0.8 add_select_fusion.3
  2.3 3.3 %fusion.2 = f32[12288]{0:T(1024)S(1)} fusion(s32[8192]{0:T(1024)S(1)} %get-tuple-element.30, f32[8192]{0:T(1024)} %param.17, s32[8192]{0:T(1024)S(1)} %get-tuple-element.29), kind=kOutput, calls=%fused_computation.8 | convolution fusion | flops 1210580992 | bytes 147456 | tf_op jit(solution)/shard_map/dot_general | solution.py:177
  5.6 13.2 %all-reduce.5 = f32[12288]{0:T(1024)S(1)} all-reduce(f32[12288]{0:T(1024)S(1)} %fusion.2), channel_id=2, replica_groups=mesh['z'=4,'plane'=2,'route'=4] {'route'}, use_global_device_ids=true, to_apply=%region_0.1.clone | all-reduce | flops 12288 | bytes 98304
  18.8 0.6 dynamic-slice
  20.1 0.3 concatenate.12
  20.4 4.2 %collective-permute-start.1 = (f32[10,2048]{1,0:T(8,128)S(1)}, f32[10,2048]{1,0:T(8,128)S(1)}, u32[]{:S(2)}, u32[]{:S(2)}) collective-permute-start(f32[10,2048]{1,0:T(8,128)S(1)} %get-tuple-element.26), channel_id=1, source_target_pairs={{1,0},{2,1},{3,2},{4,3},{5,4},{6,5},{7,6},{8,7},{9,8},{10,9},{11,1... | collective-permute-start | bytes 245768 | tf_op jit(solution)/shard_map/ppermute | solution.py:31
  24.6 0.0 collective-permute-start
  24.7 0.1 copy.37
  24.8 0.1 rem.97
  24.9 0.1 copy.38
  25.0 0.1 div.82
  25.1 0.1 copy.36
  25.2 0.1 ne.136
  25.4 2.2 %fusion.6 = f32[8192]{0:T(1024)S(1)} fusion(f32[16,128]{1,0:T(8,128)S(1)} %bitcast.47, s32[8192]{0:T(1024)S(1)} %get-tuple-element.28, s32[8192]{0:T(1024)S(1)} %get-tuple-element.27), kind=kOutput, calls=%fused_computation.10 | convolution fusion | flops 204595200 | bytes 106496 | tf_op jit(solution)/shard_map/dot_general | solution.py:139
  27.6 0.0 copy-start.7
  27.6 0.0 collective-permute-done.1
  27.7 5.0 %collective-permute-done = f32[10,2048]{1,0:T(8,128)S(1)} collective-permute-done((f32[10,2048]{1,0:T(8,128)S(1)}, f32[10,2048]{1,0:T(8,128)S(1)}, u32[]{:S(2)}, u32[]{:S(2)}) %collective-permute-start) | collective-permute-done | bytes 81952 | tf_op jit(solution)/shard_map/ppermute | solution.py:29
  32.7 0.3 reshape.237
  33.0 0.8 copy.31
  33.9 0.3 reshape.238
  34.2 0.8 copy.32
  35.0 15.2 %shard_map.139 = (f32[12,56,128]{2,1,0:T(8,128)}, f32[5,56,128]{2,1,0:T(8,128)}) custom-call(f32[5,56,128]{2,1,0:T(8,128)} %bitcast.36, f32[6,56,128]{2,1,0:T(8,128)} %bitcast.35), custom_call_target="tpu_custom_call" | custom-call | tf_op jit(solution)/shard_map/pallas_call | solution.py:96
  50.2 1.1 %copy.33 = f32[5,128,56]{2,1,0:T(8,128)S(1)} copy(f32[5,128,56]{1,2,0:T(8,128)} %bitcast.40) | data formatting | bytes 286720 | tf_op jit(solution)/shard_map/transpose | solution.py:45
  51.3 0.2 reshape.239
  51.5 0.6 slice.302
  52.2 1.2 %copy.34 = f32[12,128,56]{2,1,0:T(8,128)S(1)} copy(f32[12,128,56]{1,2,0:T(8,128)} %bitcast.38) | data formatting | bytes 688128 | tf_op jit(solution)/shard_map/transpose | solution.py:45
  53.4 0.5 reshape.240
  54.0 13.9 %all_gather.12 = bf16[96,1536]{1,0:T(8,128)(2,1)S(1)} all-gather(bf16[24,1536]{1,0:T(8,128)(2,1)S(1)} %copy_bitcast_fusion), channel_id=1, replica_groups=mesh['z'=4,'plane'=2,'route'=4] {'z'}, dimensions={0}, use_global_device_ids=true | all-gather | bytes 368640 | tf_op jit(solution)/shard_map/all_gather | solution.py:199
  67.9 9.5 %all_gather.15 = bf16[768,512]{1,0:T(8,128)(2,1)S(1)} all-gather(bf16[96,512]{1,0:T(8,128)(2,1)S(1)} %get-tuple-element.23), channel_id=1, replica_groups=mesh['z'=4,'plane'=2,'route'=4] {'plane','route'}, dimensions={0}, use_global_device_ids=true | all-gather | bytes 884736 | tf_op jit(solution)/shard_map/all_gather | solution.py:203
  77.4 10.3 %all_gather.14 = bf16[768,512]{1,0:T(8,128)(2,1)S(1)} all-gather(bf16[96,512]{1,0:T(8,128)(2,1)S(1)} %get-tuple-element.24), channel_id=1, replica_groups=mesh['z'=4,'plane'=2,'route'=4] {'plane','route'}, dimensions={0}, use_global_device_ids=true | all-gather | bytes 884736 | tf_op jit(solution)/shard_map/all_gather | solution.py:203
  87.7 9.6 %all_gather.13 = bf16[768,512]{1,0:T(8,128)(2,1)S(1)} all-gather(bf16[96,512]{1,0:T(8,128)(2,1)S(1)} %get-tuple-element.22), channel_id=1, replica_groups=mesh['z'=4,'plane'=2,'route'=4] {'plane','route'}, dimensions={0}, use_global_device_ids=true | all-gather | bytes 884736 | tf_op jit(solution)/shard_map/all_gather | solution.py:203
  97.4 0.2 pad_maximum_fusion
  97.5 0.0 copy-start.1
  97.5 1.3 %gather_fusion = bf16[256,1536]{1,0:T(8,128)(2,1)S(1)} fusion(bf16[768,1536]{1,0:T(8,128)(2,1)S(1)} %pad_maximum_fusion, s32[1024]{0:T(1024)S(1)} %pad_clamp_fusion), kind=kCustom, calls=%fused_computation | custom fusion | bytes 1573888 | tf_op jit(solution)/shard_map/gather | solution.py:212
  98.8 0.5 reshape.243
  99.3 0.0 copy-start.2
  99.4 4.6 %fusion.11 = f32[64,128]{1,0:T(8,128)S(1)} fusion(bf16[64,4,12,128]{3,2,1,0:T(8,128)(2,1)S(1)} %reshape.243, bf16[64,4,128,128]{3,2,1,0:T(8,128)(2,1)} %param.23, s32[64,128]{1,0:T(8,128)S(1)} %bitcast.41), kind=kOutput, calls=%fused_computation.16 | convolution fusion | flops 100950016 | bytes 9240576 | tf_op jit(solution)/shard_map/ptil,ptlq->piq/dot_general | solution.py:214
  104.0 0.0 copy-start
  104.0 0.3 multiply_multiply_fusion
  104.3 0.2 multiply_divide_fusion
  104.5 0.9 subtract_add_fusion
  (29 shorter events, 0.3 us)
Async XLA Ops:
  0.6 18.2 %copy-start.10 = (u32[32]{0:T(128)S(1)}, u32[32]{0:T(128)}, u32[]{:S(2)}) copy-start(u32[32]{0:T(128)} %constant.116) | copy-start | bytes 388
  0.6 19.5 %copy-start.4 = (f32[4,3072]{1,0:T(4,128)S(1)}, f32[4,3072]{1,0:T(4,128)}, u32[]{:S(2)}) copy-start(f32[4,3072]{1,0:T(4,128)} %param.12) | copy-start | bytes 147460
  0.7 19.5 %copy-start.6 = (f32[3072]{0:T(1024)S(1)}, f32[3072]{0:T(1024)}, u32[]{:S(2)}) copy-start(f32[3072]{0:T(1024)} %param.13) | copy-start | bytes 36868
  0.7 19.5 %copy-start.5 = (f32[2,3072]{1,0:T(2,128)S(1)}, f32[2,3072]{1,0:T(2,128)}, u32[]{:S(2)}) copy-start(f32[2,3072]{1,0:T(2,128)} %param.15) | copy-start | bytes 73732
  0.7 24.0 %copy-start.8 = (s32[64,4]{0,1:T(4,128)S(1)}, s32[64,4]{0,1:T(4,128)}, u32[]{:S(2)}) copy-start(s32[64,4]{0,1:T(4,128)} %param.22) | copy-start | bytes 3076
  0.7 24.6 %copy-start.9 = (s32[1,2048]{1,0:T(1,128)S(1)}, s32[1,2048]{1,0:T(1,128)}, u32[]{:S(2)}) copy-start(s32[1,2048]{1,0:T(1,128)} %param.21) | copy-start | bytes 24580
  0.7 24.6 %copy-start.3 = (s32[1,8192]{1,0:T(1,128)S(1)}, s32[1,8192]{1,0:T(1,128)}, u32[]{:S(2)}) copy-start(s32[1,8192]{1,0:T(1,128)} %param.20) | copy-start | bytes 98308
  20.4 7.2 %collective-permute-start.1 = (f32[10,2048]{1,0:T(8,128)S(1)}, f32[10,2048]{1,0:T(8,128)S(1)}, u32[]{:S(2)}, u32[]{:S(2)}) collective-permute-start(f32[10,2048]{1,0:T(8,128)S(1)} %get-tuple-element.26), channel_id=1, source_target_pairs={{1,0},{2,1},{3,2},{4,3},{5,4},{6,5},{7,6},{8,7},{9,8},{10,9},{11,1... | collective-permute-start | bytes 245768 | tf_op jit(solution)/shard_map/ppermute | solution.py:31
  24.6 8.0 %collective-permute-start = (f32[10,2048]{1,0:T(8,128)S(1)}, f32[10,2048]{1,0:T(8,128)S(1)}, u32[]{:S(2)}, u32[]{:S(2)}) collective-permute-start(f32[10,2048]{1,0:T(8,128)S(1)} %get-tuple-element.25), channel_id=1, source_target_pairs={{0,1},{1,2},{2,3},{3,4},{4,5},{5,6},{6,7},{7,8},{8,9},{9,10},{10,1... | collective-permute-start | bytes 245768 | tf_op jit(solution)/shard_map/ppermute | solution.py:29
  27.6 26.3 %copy-start.7 = (f32[3072]{0:T(1024)S(1)}, f32[3072]{0:T(1024)}, u32[]{:S(2)}) copy-start(f32[3072]{0:T(1024)} %param.14) | copy-start | bytes 36868
  97.5 1.8 %copy-start.1 = (s32[8192]{0:T(1024)S(1)}, s32[8192]{0:T(1024)}, u32[]{:S(2)}) copy-start(s32[8192]{0:T(1024)} %param.19) | copy-start | bytes 98308
  99.3 5.0 %copy-start.2 = (f32[8192]{0:T(1024)S(1)}, f32[8192]{0:T(1024)}, u32[]{:S(2)}) copy-start(f32[8192]{0:T(1024)} %param.17) | copy-start | bytes 98308
  104.0 1.5 %copy-start = (f32[8192]{0:T(1024)}, f32[8192]{0:T(1024)S(1)}, u32[]{:S(2)}) copy-start(f32[8192]{0:T(1024)S(1)} %multiply_bitcast_fusion) | copy-start | bytes 98308

commit v5 on v4

--- a/solution.py
+++ b/solution.py
@@ -32,6 +32,32 @@
         ],
         axis=1,
     )
+
+
+def entry_window(local_entry, span, width):
+    count = lax.axis_size(LINE)
+    owners = lax.axis_size("route")
+    me = lax.axis_index(LINE)
+    part = local_entry.reshape(owners, span)
+
+    def chunk(device):
+        row = lax.dynamic_index_in_dim(part, device % owners, 0, keepdims=False)
+        return jnp.where(device // owners == me // owners, row, 0.0)
+
+    total = None
+    for k in range(-owners, owners + 1):
+        target = (me - k) % count
+        message = jnp.concatenate(
+            [
+                chunk((target - 1) % count)[span - width :],
+                chunk(target),
+                chunk((target + 1) % count)[:width],
+            ]
+        )
+        if k:
+            message = lax.ppermute(message, LINE, [(j, (j - k) % count) for j in range(count)])
+        total = message if total is None else total + message
+    return total
 
 
 def to_cols(rows):
@@ -177,13 +203,12 @@
     local_entry = jnp.dot(
         tile_pick, lane_pick, precision=lax.Precision.HIGHEST, preferred_element_type=jnp.float32
     ).reshape(-1)
-    entry = lax.psum_scatter(local_entry, "route", scatter_dimension=0, tiled=True)
-
     width = halo_width(span)
-    rows_in = jnp.concatenate(
-        [fill, capacity[None], split_share, upstream_offset.astype(jnp.float32), entry[None]], 0
-    )
-    wide = padded(rows_in, width)
+    wide = jnp.concatenate(
+        [padded(jnp.concatenate([fill, capacity[None], split_share, upstream_offset.astype(jnp.float32)], 0), width),
+         entry_window(local_entry, span, width)[None]],
+        0,
+    )
     wide_cap = wide[NC]
     st0 = jnp.concatenate([wide[:NC] * (4.0 * wide_cap), jnp.zeros_like(wide[:1])], 0)
     cons = wide[NC:]

time: 106 us -> 110 us (1.038)
  starting transfers between devices: 4.19 us -> 18.3 us
  blocking collectives: 56.6 us -> 43.5 us
  waiting for transfers between devices: 4.96 us -> 7.95 us
    ppermute x0 -> x8, starting transfers between devices: none -> 13.9 us  [entry_window(): lax.ppermute(message, LINE, [(j, (j - k) % count) for j in range(count)])]
    unnamed x1 -> x0, blocking collectives: 13.2 us -> none
    ppermute x1, waiting for transfers between devices: 0.01 us -> 2.46 us  [padded(): lax.ppermute(head, LINE, [((i + 1) % count, i) for i in range(count)])]
  transfers between devices with their start and end apart: 2 -> 10, of which waited for: 1 -> 2; matrix products, arithmetic and copies ran while one was open for 3% -> 3% of each run, Pallas kernels for 0% -> 0%
where the time goes in v5:
time: 110 us; the launch traced here: 109 us
  blocking collectives  43.5 us (40%)
  starting transfers between devices  18.3 us (17%)
  Pallas kernels  15.2 us (14%)
  matrix products  10.1 us (9%)
  local copies, waits for them, and re-layouts  8.53 us (8%)
  waiting for transfers between devices  7.95 us (7%)
  other arithmetic  3.42 us (3%)
  between operations  2.37 us (2%)
    all_gather x3, blocking collectives, body(): lax.all_gather(every_tile[:, c * piece:(c + 1) * piece], ('plane', 'route...  29.4 us
    pallas_call x1, Pallas kernels, simulate(): pl.pallas_call(sim_kernel, out_shape=(jax.ShapeDtypeStruct((count, rows,...  15.2 us
    all_gather x1, blocking collectives, body(): every_tile = lax.all_gather(tiles, 'z', axis=0, tiled=True)  14 us
    ppermute x8, starting transfers between devices, entry_window(): lax.ppermute(message, LINE, [(j, (j - k) % count) for j in range(count)])  13.9 us
    ppermute x1, waiting for transfers between devices, padded(): lax.ppermute(tail, LINE, [(i, (i + 1) % count) for i in range(count)])  5.47 us
    dot_general x1, matrix products, body(): jnp.einsum('ptil,ptlq->piq', fetched, incidence, preferred_element_type=j...  4.6 us
    ppermute x1, starting transfers between devices, padded(): lax.ppermute(head, LINE, [((i + 1) % count, i) for i in range(count)])  4.42 us
    dot_general x1, matrix products, body(): jnp.dot(tile_pick, lane_pick, precision=lax.Precision.HIGHEST, preferred_...  3.3 us
  transfers between devices with their start and end apart: 10, of which 2 were waited for; matrix products, arithmetic and copies ran while one was open for 3% of the time, Pallas kernels for 0%

profile of v5, /device:TPU:0, one launch (start us, length us, event | category | flops | bytes accessed | tf_op | source)
XLA Modules:
  0.0 109.4 jit_solution(1576490805606219693)
XLA Ops:
  1.4 0.8 add_select_fusion.3
  2.2 3.3 %fusion = f32[96,128]{1,0:T(8,128)S(1)} fusion(s32[8192]{0:T(1024)S(1)} %get-tuple-element.57, f32[8192]{0:T(1024)} %param.17, s32[8192]{0:T(1024)S(1)} %get-tuple-element.56), kind=kOutput, calls=%fused_computation.4 | convolution fusion | flops 1210580992 | bytes 147456 | tf_op jit(solution)/shard_map/dot_general | solution.py:203
  6.0 0.2 broadcast_select_fusion.24
  6.2 0.1 broadcast_select_fusion.7
  6.3 6.1 %collective-permute-start.9 = (f32[7168]{0:T(1024)S(1)}, f32[7168]{0:T(1024)S(1)}, u32[]{:S(2)}, u32[]{:S(2)}) collective-permute-start(f32[7168]{0:T(1024)S(1)} %pad_maximum_fusion.20), channel_id=1, source_target_pairs={{0,28},{1,29},{2,30},{3,31},{4,0},{5,1},{6,2},{7,3},{8,4},{9,5},{1... | collective-permute-start | bytes 86024 | tf_op jit(solution)/shard_map/ppermute | solution.py:58
  12.4 2.0 %collective-permute-start.7 = (f32[7168]{0:T(1024)S(1)}, f32[7168]{0:T(1024)S(1)}, u32[]{:S(2)}, u32[]{:S(2)}) collective-permute-start(f32[7168]{0:T(1024)S(1)} %pad_maximum_fusion.18), channel_id=1, source_target_pairs={{0,30},{1,31},{2,0},{3,1},{4,2},{5,3},{6,4},{7,5},{8,6},{9,7},{10,... | collective-permute-start | bytes 86024 | tf_op jit(solution)/shard_map/ppermute | solution.py:58
  14.4 0.1 broadcast_select_fusion.23
  14.6 1.8 %collective-permute-start.6 = (f32[7168]{0:T(1024)S(1)}, f32[7168]{0:T(1024)S(1)}, u32[]{:S(2)}, u32[]{:S(2)}) collective-permute-start(f32[7168]{0:T(1024)S(1)} %pad_maximum_fusion.17), channel_id=1, source_target_pairs={{0,31},{1,0},{2,1},{3,2},{4,3},{5,4},{6,5},{7,6},{8,7},{9,8},{10,9... | collective-permute-start | bytes 86024 | tf_op jit(solution)/shard_map/ppermute | solution.py:58
  16.5 0.1 pad_maximum_fusion.7
  16.6 0.1 copy.29
  16.7 0.1 rem.1188
  16.8 0.1 copy.30
  16.9 0.1 div.389
  17.0 0.1 copy.28
  17.1 0.1 ne.605
  17.4 0.1 broadcast_select_fusion.26
  17.5 2.2 %fusion.3 = f32[8192]{0:T(1024)S(1)} fusion(f32[16,128]{1,0:T(8,128)S(1)} %bitcast.101, s32[8192]{0:T(1024)S(1)} %get-tuple-element.55, s32[8192]{0:T(1024)S(1)} %get-tuple-element.54), kind=kOutput, calls=%fused_computation.9 | convolution fusion | flops 204595200 | bytes 106496 | tf_op jit(solution)/shard_map/dot_general | solution.py:165
  19.8 0.1 collective-permute-start.4
  19.8 1.2 %collective-permute-start.2 = (f32[7168]{0:T(1024)S(1)}, f32[7168]{0:T(1024)S(1)}, u32[]{:S(2)}, u32[]{:S(2)}) collective-permute-start(f32[7168]{0:T(1024)S(1)} %pad_maximum_fusion.13), channel_id=1, source_target_pairs={{0,4},{1,5},{2,6},{3,7},{4,8},{5,9},{6,10},{7,11},{8,12},{9,13},{1... | collective-permute-start | bytes 86024 | tf_op jit(solution)/shard_map/ppermute | solution.py:58
  21.0 2.8 %collective-permute-start.3 = (f32[7168]{0:T(1024)S(1)}, f32[7168]{0:T(1024)S(1)}, u32[]{:S(2)}, u32[]{:S(2)}) collective-permute-start(f32[7168]{0:T(1024)S(1)} %pad_maximum_fusion.14), channel_id=1, source_target_pairs={{0,3},{1,4},{2,5},{3,6},{4,7},{5,8},{6,9},{7,10},{8,11},{9,12},{10... | collective-permute-start | bytes 86024 | tf_op jit(solution)/shard_map/ppermute | solution.py:58
  23.8 4.4 %collective-permute-start.1 = (f32[9,2048]{1,0:T(8,128)S(1)}, f32[9,2048]{1,0:T(8,128)S(1)}, u32[]{:S(2)}, u32[]{:S(2)}) collective-permute-start(f32[9,2048]{1,0:T(8,128)S(1)} %get-tuple-element.26), channel_id=1, source_target_pairs={{1,0},{2,1},{3,2},{4,3},{5,4},{6,5},{7,6},{8,7},{9,8},{10,9},{11,1... | collective-permute-start | bytes 221192 | tf_op jit(solution)/shard_map/ppermute | solution.py:31
  28.3 2.5 %collective-permute-done.1 = f32[9,2048]{1,0:T(8,128)S(1)} collective-permute-done((f32[9,2048]{1,0:T(8,128)S(1)}, f32[9,2048]{1,0:T(8,128)S(1)}, u32[]{:S(2)}, u32[]{:S(2)}) %collective-permute-start.1) | collective-permute-done | bytes 73760 | tf_op jit(solution)/shard_map/ppermute | solution.py:31
  30.8 5.5 %collective-permute-done = f32[9,2048]{1,0:T(8,128)S(1)} collective-permute-done((f32[9,2048]{1,0:T(8,128)S(1)}, f32[9,2048]{1,0:T(8,128)S(1)}, u32[]{:S(2)}, u32[]{:S(2)}) %collective-permute-start) | collective-permute-done | bytes 73760 | tf_op jit(solution)/shard_map/ppermute | solution.py:29
  36.2 0.1 fusion.89
  36.3 0.1 maximum_multiply_fusion
  36.4 0.3 reshape.332
  36.7 0.8 copy.23
  37.5 0.1 pad_maximum_fusion.1
  37.6 0.3 reshape.333
  38.0 0.8 copy.24
  38.8 15.2 %shard_map.139 = (f32[12,56,128]{2,1,0:T(8,128)}, f32[5,56,128]{2,1,0:T(8,128)}) custom-call(f32[5,56,128]{2,1,0:T(8,128)} %bitcast.60, f32[6,56,128]{2,1,0:T(8,128)} %bitcast.59), custom_call_target="tpu_custom_call" | custom-call | tf_op jit(solution)/shard_map/pallas_call | solution.py:122
  54.0 1.1 copy.25
  55.1 0.2 reshape.334
  55.3 0.6 slice.446
  56.0 1.2 %copy.26 = f32[12,128,56]{2,1,0:T(8,128)S(1)} copy(f32[12,128,56]{1,2,0:T(8,128)} %bitcast.62) | data formatting | bytes 688128 | tf_op jit(solution)/shard_map/transpose | solution.py:71
  57.2 0.5 reshape.335
  57.8 14.0 %all_gather.12 = bf16[96,1536]{1,0:T(8,128)(2,1)S(1)} all-gather(bf16[24,1536]{1,0:T(8,128)(2,1)S(1)} %copy_bitcast_fusion), channel_id=1, replica_groups=mesh['z'=4,'plane'=2,'route'=4] {'z'}, dimensions={0}, use_global_device_ids=true | all-gather | bytes 368640 | tf_op jit(solution)/shard_map/all_gather | solution.py:224
  71.8 9.5 %all_gather.15 = bf16[768,512]{1,0:T(8,128)(2,1)S(1)} all-gather(bf16[96,512]{1,0:T(8,128)(2,1)S(1)} %get-tuple-element.23), channel_id=1, replica_groups=mesh['z'=4,'plane'=2,'route'=4] {'plane','route'}, dimensions={0}, use_global_device_ids=true | all-gather | bytes 884736 | tf_op jit(solution)/shard_map/all_gather | solution.py:228
  81.3 10.5 %all_gather.14 = bf16[768,512]{1,0:T(8,128)(2,1)S(1)} all-gather(bf16[96,512]{1,0:T(8,128)(2,1)S(1)} %get-tuple-element.24), channel_id=1, replica_groups=mesh['z'=4,'plane'=2,'route'=4] {'plane','route'}, dimensions={0}, use_global_device_ids=true | all-gather | bytes 884736 | tf_op jit(solution)/shard_map/all_gather | solution.py:228
  91.8 9.5 %all_gather.13 = bf16[768,512]{1,0:T(8,128)(2,1)S(1)} all-gather(bf16[96,512]{1,0:T(8,128)(2,1)S(1)} %get-tuple-element.22), channel_id=1, replica_groups=mesh['z'=4,'plane'=2,'route'=4] {'plane','route'}, dimensions={0}, use_global_device_ids=true | all-gather | bytes 884736 | tf_op jit(solution)/shard_map/all_gather | solution.py:228
  101.3 0.2 pad_maximum_fusion
  101.5 1.3 %gather_fusion = bf16[256,1536]{1,0:T(8,128)(2,1)S(1)} fusion(bf16[768,1536]{1,0:T(8,128)(2,1)S(1)} %pad_maximum_fusion, s32[1024]{0:T(1024)S(1)} %pad_clamp_fusion), kind=kCustom, calls=%fused_computation | custom fusion | bytes 1573888 | tf_op jit(solution)/shard_map/gather | solution.py:237
  102.7 0.5 reshape.338
  103.3 4.6 %fusion.8 = f32[64,128]{1,0:T(8,128)S(1)} fusion(bf16[64,4,12,128]{3,2,1,0:T(8,128)(2,1)S(1)} %reshape.338, bf16[64,4,128,128]{3,2,1,0:T(8,128)(2,1)} %param.23, s32[64,128]{1,0:T(8,128)S(1)} %bitcast.69), kind=kOutput, calls=%fused_computation.15 | convolution fusion | flops 100950016 | bytes 9240576 | tf_op jit(solution)/shard_map/ptil,ptlq->piq/dot_general | solution.py:239
  107.9 0.0 copy-start.2
  107.9 0.3 multiply_multiply_fusion
  108.3 0.2 multiply_divide_fusion
  108.5 0.9 subtract_add_fusion
  (56 shorter events, 0.4 us)
Async XLA Ops:
  0.6 15.7 %copy-start.9 = (s32[64,4]{0,1:T(4,128)S(1)}, s32[64,4]{0,1:T(4,128)}, u32[]{:S(2)}) copy-start(s32[64,4]{0,1:T(4,128)} %param.22) | copy-start | bytes 3076
  0.6 15.8 %copy-start.7 = (s32[2,3072]{1,0:T(2,128)S(1)}, s32[2,3072]{1,0:T(2,128)}, u32[]{:S(2)}) copy-start(s32[2,3072]{1,0:T(2,128)} %param.16) | copy-start | bytes 73732
  0.7 15.8 %copy-start.1 = (f32[2,3072]{1,0:T(2,128)S(1)}, f32[2,3072]{1,0:T(2,128)}, u32[]{:S(2)}) copy-start(f32[2,3072]{1,0:T(2,128)} %param.15) | copy-start | bytes 73732
  0.7 15.8 %copy-start.3 = (f32[3072]{0:T(1024)S(1)}, f32[3072]{0:T(1024)}, u32[]{:S(2)}) copy-start(f32[3072]{0:T(1024)} %param.13) | copy-start | bytes 36868
  0.7 15.8 %copy-start = (f32[4,3072]{1,0:T(4,128)S(1)}, f32[4,3072]{1,0:T(4,128)}, u32[]{:S(2)}) copy-start(f32[4,3072]{1,0:T(4,128)} %param.12) | copy-start | bytes 147460
  0.7 16.6 %copy-start.10 = (s32[1,2048]{1,0:T(1,128)S(1)}, s32[1,2048]{1,0:T(1,128)}, u32[]{:S(2)}) copy-start(s32[1,2048]{1,0:T(1,128)} %param.21) | copy-start | bytes 24580
  0.7 16.6 %copy-start.6 = (s32[1,8192]{1,0:T(1,128)S(1)}, s32[1,8192]{1,0:T(1,128)}, u32[]{:S(2)}) copy-start(s32[1,8192]{1,0:T(1,128)} %param.20) | copy-start | bytes 98308
  6.3 13.4 %collective-permute-start.9 = (f32[7168]{0:T(1024)S(1)}, f32[7168]{0:T(1024)S(1)}, u32[]{:S(2)}, u32[]{:S(2)}) collective-permute-start(f32[7168]{0:T(1024)S(1)} %pad_maximum_fusion.20), channel_id=1, source_target_pairs={{0,28},{1,29},{2,30},{3,31},{4,0},{5,1},{6,2},{7,3},{8,4},{9,5},{1... | collective-permute-start | bytes 86024 | tf_op jit(solution)/shard_map/ppermute | solution.py:58
  12.4 7.4 %collective-permute-start.8 = (f32[7168]{0:T(1024)S(1)}, f32[7168]{0:T(1024)S(1)}, u32[]{:S(2)}, u32[]{:S(2)}) collective-permute-start(f32[7168]{0:T(1024)S(1)} %pad_maximum_fusion.19), channel_id=1, source_target_pairs={{0,29},{1,30},{2,31},{3,0},{4,1},{5,2},{6,3},{7,4},{8,5},{9,6},{10... | collective-permute-start | bytes 86024 | tf_op jit(solution)/shard_map/ppermute | solution.py:58
  12.4 8.6 %collective-permute-start.7 = (f32[7168]{0:T(1024)S(1)}, f32[7168]{0:T(1024)S(1)}, u32[]{:S(2)}, u32[]{:S(2)}) collective-permute-start(f32[7168]{0:T(1024)S(1)} %pad_maximum_fusion.18), channel_id=1, source_target_pairs={{0,30},{1,31},{2,0},{3,1},{4,2},{5,3},{6,4},{7,5},{8,6},{9,7},{10,... | collective-permute-start | bytes 86024 | tf_op jit(solution)/shard_map/ppermute | solution.py:58
  14.6 9.3 %collective-permute-start.6 = (f32[7168]{0:T(1024)S(1)}, f32[7168]{0:T(1024)S(1)}, u32[]{:S(2)}, u32[]{:S(2)}) collective-permute-start(f32[7168]{0:T(1024)S(1)} %pad_maximum_fusion.17), channel_id=1, source_target_pairs={{0,31},{1,0},{2,1},{3,2},{4,3},{5,4},{6,5},{7,6},{8,7},{9,8},{10,9... | collective-permute-start | bytes 86024 | tf_op jit(solution)/shard_map/ppermute | solution.py:58
  16.4 11.9 %collective-permute-start.5 = (f32[7168]{0:T(1024)S(1)}, f32[7168]{0:T(1024)S(1)}, u32[]{:S(2)}, u32[]{:S(2)}) collective-permute-start(f32[7168]{0:T(1024)S(1)} %pad_maximum_fusion.16), channel_id=1, source_target_pairs={{0,1},{1,2},{2,3},{3,4},{4,5},{5,6},{6,7},{7,8},{8,9},{9,10},{10,1... | collective-permute-start | bytes 86024 | tf_op jit(solution)/shard_map/ppermute | solution.py:58
  19.7 38.0 %copy-start.8 = (f32[3072]{0:T(1024)S(1)}, f32[3072]{0:T(1024)}, u32[]{:S(2)}) copy-start(f32[3072]{0:T(1024)} %param.14) | copy-start | bytes 36868
  19.8 8.5 %collective-permute-start.4 = (f32[7168]{0:T(1024)S(1)}, f32[7168]{0:T(1024)S(1)}, u32[]{:S(2)}, u32[]{:S(2)}) collective-permute-start(f32[7168]{0:T(1024)S(1)} %pad_maximum_fusion.15), channel_id=1, source_target_pairs={{0,2},{1,3},{2,4},{3,5},{4,6},{5,7},{6,8},{7,9},{8,10},{9,11},{10,... | collective-permute-start | bytes 86024 | tf_op jit(solution)/shard_map/ppermute | solution.py:58
  19.8 8.4 %collective-permute-start.2 = (f32[7168]{0:T(1024)S(1)}, f32[7168]{0:T(1024)S(1)}, u32[]{:S(2)}, u32[]{:S(2)}) collective-permute-start(f32[7168]{0:T(1024)S(1)} %pad_maximum_fusion.13), channel_id=1, source_target_pairs={{0,4},{1,5},{2,6},{3,7},{4,8},{5,9},{6,10},{7,11},{8,12},{9,13},{1... | collective-permute-start | bytes 86024 | tf_op jit(solution)/shard_map/ppermute | solution.py:58
  21.0 7.3 %collective-permute-start.3 = (f32[7168]{0:T(1024)S(1)}, f32[7168]{0:T(1024)S(1)}, u32[]{:S(2)}, u32[]{:S(2)}) collective-permute-start(f32[7168]{0:T(1024)S(1)} %pad_maximum_fusion.14), channel_id=1, source_target_pairs={{0,3},{1,4},{2,5},{3,6},{4,7},{5,8},{6,9},{7,10},{8,11},{9,12},{10... | collective-permute-start | bytes 86024 | tf_op jit(solution)/shard_map/ppermute | solution.py:58
  23.8 6.9 %collective-permute-start.1 = (f32[9,2048]{1,0:T(8,128)S(1)}, f32[9,2048]{1,0:T(8,128)S(1)}, u32[]{:S(2)}, u32[]{:S(2)}) collective-permute-start(f32[9,2048]{1,0:T(8,128)S(1)} %get-tuple-element.26), channel_id=1, source_target_pairs={{1,0},{2,1},{3,2},{4,3},{5,4},{6,5},{7,6},{8,7},{9,8},{10,9},{11,1... | collective-permute-start | bytes 221192 | tf_op jit(solution)/shard_map/ppermute | solution.py:31
  28.3 8.0 %collective-permute-start = (f32[9,2048]{1,0:T(8,128)S(1)}, f32[9,2048]{1,0:T(8,128)S(1)}, u32[]{:S(2)}, u32[]{:S(2)}) collective-permute-start(f32[9,2048]{1,0:T(8,128)S(1)} %get-tuple-element.25), channel_id=1, source_target_pairs={{0,1},{1,2},{2,3},{3,4},{4,5},{5,6},{6,7},{7,8},{8,9},{9,10},{10,1... | collective-permute-start | bytes 221192 | tf_op jit(solution)/shard_map/ppermute | solution.py:29
  101.4 1.8 %copy-start.4 = (s32[8192]{0:T(1024)S(1)}, s32[8192]{0:T(1024)}, u32[]{:S(2)}) copy-start(s32[8192]{0:T(1024)} %param.19) | copy-start | bytes 98308
  103.3 5.0 %copy-start.5 = (f32[8192]{0:T(1024)S(1)}, f32[8192]{0:T(1024)}, u32[]{:S(2)}) copy-start(f32[8192]{0:T(1024)} %param.17) | copy-start | bytes 98308
  107.9 1.5 %copy-start.2 = (f32[8192]{0:T(1024)}, f32[8192]{0:T(1024)S(1)}, u32[]{:S(2)}) copy-start(f32[8192]{0:T(1024)S(1)} %multiply_bitcast_fusion) | copy-start | bytes 98308

commit v6 on v4

--- a/solution.py
+++ b/solution.py
@@ -169,16 +169,17 @@
     incidence,
 ):
     span = fill.shape[1]
-    region_links = span * lax.axis_size("route")
-    link_tiles = jnp.arange(region_links // 128, dtype=jnp.int32)
+    paths = lax.all_gather(
+        jnp.stack([path_flow, anchor.astype(jnp.float32)]), "route", axis=1, tiled=True
+    )
+    near = paths[1].astype(jnp.int32)
+    own_tiles = jnp.arange(span // 128, dtype=jnp.int32) + lax.axis_index("route") * (span // 128)
     lanes = jnp.arange(128, dtype=jnp.int32)
-    tile_pick = jnp.where((anchor // 128)[None, :] == link_tiles[:, None], path_flow[None, :], 0.0)
-    lane_pick = ((anchor % 128)[:, None] == lanes[None, :]).astype(jnp.float32)
-    local_entry = jnp.dot(
+    tile_pick = jnp.where((near // 128)[None, :] == own_tiles[:, None], paths[0][None, :], 0.0)
+    lane_pick = ((near % 128)[:, None] == lanes[None, :]).astype(jnp.float32)
+    entry = jnp.dot(
         tile_pick, lane_pick, precision=lax.Precision.HIGHEST, preferred_element_type=jnp.float32
     ).reshape(-1)
-    entry = lax.psum_scatter(local_entry, "route", scatter_dimension=0, tiled=True)
-
     width = halo_width(span)
     rows_in = jnp.concatenate(
         [fill, capacity[None], split_share, upstream_offset.astype(jnp.float32), entry[None]], 0

time: 106 us -> 105 us (level)
  blocking collectives: 56.6 us -> 50.4 us
  matrix products: 10.1 us -> 13.5 us
  other arithmetic: 3.39 us -> 5.41 us
  starting transfers between devices: 4.19 us -> 5.53 us
    unnamed x1 -> x0, blocking collectives: 13.2 us -> none
    all_gather x0 -> x1, blocking collectives: none -> 7.19 us  [body(): lax.all_gather(jnp.stack([path_flow, anchor.astype(jnp.float32)]), 'route...]
    dot_general x1, matrix products: 3.3 us -> 6.68 us  [body(): jnp.dot(tile_pick, lane_pick, precision=lax.Precision.HIGHEST, preferred_...]
    ppermute x1, starting transfers between devices: 4.19 us -> 5.53 us  [padded(): lax.ppermute(head, LINE, [((i + 1) % count, i) for i in range(count)])]
where the time goes in v6:
time: 105 us
  blocking collectives  50.4 us (48%)
  Pallas kernels  15.2 us (14%)
  matrix products  13.5 us (13%)
  local copies, waits for them, and re-layouts  8.79 us (8%)
  starting transfers between devices  5.53 us (5%)
  other arithmetic  5.41 us (5%)
  waiting for transfers between devices  4.96 us (5%)
    all_gather x3, blocking collectives, body(): lax.all_gather(every_tile[:, c * piece:(c + 1) * piece], ('plane', 'route...  29.3 us
    pallas_call x1, Pallas kernels, simulate(): pl.pallas_call(sim_kernel, out_shape=(jax.ShapeDtypeStruct((count, rows,...  15.2 us
    all_gather x1, blocking collectives, body(): every_tile = lax.all_gather(tiles, 'z', axis=0, tiled=True)  13.9 us
    all_gather x1, blocking collectives, body(): lax.all_gather(jnp.stack([path_flow, anchor.astype(jnp.float32)]), 'route...  7.19 us
    dot_general x1, matrix products, body(): jnp.dot(tile_pick, lane_pick, precision=lax.Precision.HIGHEST, preferred_...  6.68 us
    ppermute x1, starting transfers between devices, padded(): lax.ppermute(head, LINE, [((i + 1) % count, i) for i in range(count)])  5.53 us
    ppermute x1, waiting for transfers between devices, padded(): lax.ppermute(tail, LINE, [(i, (i + 1) % count) for i in range(count)])  4.95 us
    dot_general x1, matrix products, body(): jnp.einsum('ptil,ptlq->piq', fetched, incidence, preferred_element_type=j...  4.6 us
  transfers between devices with their start and end apart: 2, of which 1 were waited for; matrix products, arithmetic and copies ran while one was open for 3% of the time, Pallas kernels for 0%

profile of v6, /device:TPU:0, one launch (start us, length us, event | category | flops | bytes accessed | tf_op | source)
XLA Modules:
  0.0 104.8 jit_solution(15726984876340392051)
XLA Ops:
  0.6 0.8 convert_element_type.32
  1.4 0.8 pad_maximum_fusion.3
  2.2 7.2 %all_gather.15 = f32[2,32768]{1,0:T(2,128)S(1)} all-gather(f32[2,8192]{1,0:T(2,128)S(1)} %pad_maximum_fusion.3), channel_id=1, replica_groups=mesh['z'=4,'plane'=2,'route'=4] {'route'}, dimensions={1}, use_global_device_ids=true | all-gather | bytes 327680 | tf_op jit(solution)/shard_map/all_gather | solution.py:172
  9.4 0.2 fusion.111
  9.6 0.7 and_select_fusion
  10.3 0.7 convert_element_type.31
  11.1 0.1 add_select_fusion
  11.2 0.0 copy-start.4
  11.2 0.0 copy-start.5
  11.2 0.0 copy-start.6
  11.2 0.0 copy-start.8
  11.2 0.0 copy-start.9
  11.2 0.0 copy-start.3
  11.2 0.3 fusion.119
  11.5 6.7 %fusion = f32[24,128]{1,0:T(8,128)S(1)} fusion(s32[32768]{0:T(1024)S(1)} %add_select_fusion, f32[24,32768]{1,0:T(8,128)S(1)} %fusion.119), kind=kOutput, calls=%fused_computation.2 | convolution fusion | flops 1212153856 | bytes 3289088 | tf_op jit(solution)/shard_map/dot_general | solution.py:180
  18.3 0.3 concatenate.12
  18.6 5.5 %collective-permute-start.1 = (f32[10,2048]{1,0:T(8,128)S(1)}, f32[10,2048]{1,0:T(8,128)S(1)}, u32[]{:S(2)}, u32[]{:S(2)}) collective-permute-start(f32[10,2048]{1,0:T(8,128)S(1)} %get-tuple-element.28), channel_id=1, source_target_pairs={{1,0},{2,1},{3,2},{4,3},{5,4},{6,5},{7,6},{8,7},{9,8},{10,9},{11,1... | collective-permute-start | bytes 245768 | tf_op jit(solution)/shard_map/ppermute | solution.py:31
  24.1 0.1 copy.29
  24.2 0.1 rem.127
  24.3 0.1 copy.30
  24.4 0.1 div.86
  24.5 0.1 copy.28
  24.7 0.1 ne.158
  24.9 2.2 %fusion.4 = f32[8192]{0:T(1024)S(1)} fusion(f32[16,128]{1,0:T(8,128)S(1)} %bitcast.55, s32[8192]{0:T(1024)S(1)} %get-tuple-element.30, s32[8192]{0:T(1024)S(1)} %get-tuple-element.29), kind=kOutput, calls=%fused_computation.9 | convolution fusion | flops 204595200 | bytes 106496 | tf_op jit(solution)/shard_map/dot_general | solution.py:139
  27.1 0.0 copy-start.7
  27.1 5.0 %collective-permute-done = f32[10,2048]{1,0:T(8,128)S(1)} collective-permute-done((f32[10,2048]{1,0:T(8,128)S(1)}, f32[10,2048]{1,0:T(8,128)S(1)}, u32[]{:S(2)}, u32[]{:S(2)}) %collective-permute-start) | collective-permute-done | bytes 81952 | tf_op jit(solution)/shard_map/ppermute | solution.py:29
  32.2 0.3 reshape.251
  32.5 0.8 copy.23
  33.3 0.3 reshape.252
  33.7 0.8 copy.24
  34.5 15.2 %shard_map.139 = (f32[12,56,128]{2,1,0:T(8,128)}, f32[5,56,128]{2,1,0:T(8,128)}) custom-call(f32[5,56,128]{2,1,0:T(8,128)} %bitcast.39, f32[6,56,128]{2,1,0:T(8,128)} %bitcast.38), custom_call_target="tpu_custom_call" | custom-call | tf_op jit(solution)/shard_map/pallas_call | solution.py:96
  49.7 1.1 %copy.25 = f32[5,128,56]{2,1,0:T(8,128)S(1)} copy(f32[5,128,56]{1,2,0:T(8,128)} %bitcast.47) | data formatting | bytes 286720 | tf_op jit(solution)/shard_map/transpose | solution.py:45
  50.8 0.2 reshape.253
  51.0 0.6 slice.312
  51.6 1.2 %copy.26 = f32[12,128,56]{2,1,0:T(8,128)S(1)} copy(f32[12,128,56]{1,2,0:T(8,128)} %bitcast.44) | data formatting | bytes 688128 | tf_op jit(solution)/shard_map/transpose | solution.py:45
  52.9 0.5 reshape.254
  53.5 13.9 %all_gather.16 = bf16[96,1536]{1,0:T(8,128)(2,1)S(1)} all-gather(bf16[24,1536]{1,0:T(8,128)(2,1)S(1)} %copy_bitcast_fusion), channel_id=1, replica_groups=mesh['z'=4,'plane'=2,'route'=4] {'z'}, dimensions={0}, use_global_device_ids=true | all-gather | bytes 368640 | tf_op jit(solution)/shard_map/all_gather | solution.py:200
  67.4 9.5 %all_gather.19 = bf16[768,512]{1,0:T(8,128)(2,1)S(1)} all-gather(bf16[96,512]{1,0:T(8,128)(2,1)S(1)} %get-tuple-element.23), channel_id=1, replica_groups=mesh['z'=4,'plane'=2,'route'=4] {'plane','route'}, dimensions={0}, use_global_device_ids=true | all-gather | bytes 884736 | tf_op jit(solution)/shard_map/all_gather | solution.py:204
  76.9 10.3 %all_gather.18 = bf16[768,512]{1,0:T(8,128)(2,1)S(1)} all-gather(bf16[96,512]{1,0:T(8,128)(2,1)S(1)} %get-tuple-element.24), channel_id=1, replica_groups=mesh['z'=4,'plane'=2,'route'=4] {'plane','route'}, dimensions={0}, use_global_device_ids=true | all-gather | bytes 884736 | tf_op jit(solution)/shard_map/all_gather | solution.py:204
  87.2 9.5 %all_gather.17 = bf16[768,512]{1,0:T(8,128)(2,1)S(1)} all-gather(bf16[96,512]{1,0:T(8,128)(2,1)S(1)} %get-tuple-element.22), channel_id=1, replica_groups=mesh['z'=4,'plane'=2,'route'=4] {'plane','route'}, dimensions={0}, use_global_device_ids=true | all-gather | bytes 884736 | tf_op jit(solution)/shard_map/all_gather | solution.py:204
  96.7 0.2 pad_maximum_fusion
  96.8 1.3 %gather_fusion = bf16[256,1536]{1,0:T(8,128)(2,1)S(1)} fusion(bf16[768,1536]{1,0:T(8,128)(2,1)S(1)} %pad_maximum_fusion, s32[1024]{0:T(1024)S(1)} %pad_clamp_fusion), kind=kCustom, calls=%fused_computation | custom fusion | bytes 1573888 | tf_op jit(solution)/shard_map/gather | solution.py:213
  98.1 0.5 reshape.257
  98.7 4.6 %fusion.10 = f32[64,128]{1,0:T(8,128)S(1)} fusion(bf16[64,4,12,128]{3,2,1,0:T(8,128)(2,1)S(1)} %reshape.257, bf16[64,4,128,128]{3,2,1,0:T(8,128)(2,1)} %param.23, s32[64,128]{1,0:T(8,128)S(1)} %bitcast.48), kind=kOutput, calls=%fused_computation.16 | convolution fusion | flops 100950016 | bytes 9240576 | tf_op jit(solution)/shard_map/ptil,ptlq->piq/dot_general | solution.py:215
  103.3 0.0 copy-start.1
  103.3 0.3 multiply_multiply_fusion
  103.6 0.2 multiply_divide_fusion
  103.8 0.9 subtract_add_fusion
  (31 shorter events, 0.3 us)
Async XLA Ops:
  11.2 7.1 %copy-start.4 = (f32[4,3072]{1,0:T(4,128)S(1)}, f32[4,3072]{1,0:T(4,128)}, u32[]{:S(2)}) copy-start(f32[4,3072]{1,0:T(4,128)} %param.12) | copy-start | bytes 147460
  11.2 7.1 %copy-start.5 = (f32[2,3072]{1,0:T(2,128)S(1)}, f32[2,3072]{1,0:T(2,128)}, u32[]{:S(2)}) copy-start(f32[2,3072]{1,0:T(2,128)} %param.15) | copy-start | bytes 73732
  11.2 7.1 %copy-start.6 = (f32[3072]{0:T(1024)S(1)}, f32[3072]{0:T(1024)}, u32[]{:S(2)}) copy-start(f32[3072]{0:T(1024)} %param.13) | copy-start | bytes 36868
  11.2 12.9 %copy-start.8 = (s32[64,4]{0,1:T(4,128)S(1)}, s32[64,4]{0,1:T(4,128)}, u32[]{:S(2)}) copy-start(s32[64,4]{0,1:T(4,128)} %param.22) | copy-start | bytes 3076
  11.2 13.6 %copy-start.9 = (s32[1,2048]{1,0:T(1,128)S(1)}, s32[1,2048]{1,0:T(1,128)}, u32[]{:S(2)}) copy-start(s32[1,2048]{1,0:T(1,128)} %param.21) | copy-start | bytes 24580
  11.2 13.6 %copy-start.3 = (s32[1,8192]{1,0:T(1,128)S(1)}, s32[1,8192]{1,0:T(1,128)}, u32[]{:S(2)}) copy-start(s32[1,8192]{1,0:T(1,128)} %param.20) | copy-start | bytes 98308
  18.6 8.6 %collective-permute-start.1 = (f32[10,2048]{1,0:T(8,128)S(1)}, f32[10,2048]{1,0:T(8,128)S(1)}, u32[]{:S(2)}, u32[]{:S(2)}) collective-permute-start(f32[10,2048]{1,0:T(8,128)S(1)} %get-tuple-element.28), channel_id=1, source_target_pairs={{1,0},{2,1},{3,2},{4,3},{5,4},{6,5},{7,6},{8,7},{9,8},{10,9},{11,1... | collective-permute-start | bytes 245768 | tf_op jit(solution)/shard_map/ppermute | solution.py:31
  24.1 8.0 %collective-permute-start = (f32[10,2048]{1,0:T(8,128)S(1)}, f32[10,2048]{1,0:T(8,128)S(1)}, u32[]{:S(2)}, u32[]{:S(2)}) collective-permute-start(f32[10,2048]{1,0:T(8,128)S(1)} %get-tuple-element.27), channel_id=1, source_target_pairs={{0,1},{1,2},{2,3},{3,4},{4,5},{5,6},{6,7},{7,8},{8,9},{9,10},{10,1... | collective-permute-start | bytes 245768 | tf_op jit(solution)/shard_map/ppermute | solution.py:29
  27.1 26.3 %copy-start.7 = (f32[3072]{0:T(1024)S(1)}, f32[3072]{0:T(1024)}, u32[]{:S(2)}) copy-start(f32[3072]{0:T(1024)} %param.14) | copy-start | bytes 36868
  96.8 1.8 %copy-start.2 = (s32[8192]{0:T(1024)S(1)}, s32[8192]{0:T(1024)}, u32[]{:S(2)}) copy-start(s32[8192]{0:T(1024)} %param.19) | copy-start | bytes 98308
  98.7 5.0 %copy-start = (f32[8192]{0:T(1024)S(1)}, f32[8192]{0:T(1024)}, u32[]{:S(2)}) copy-start(f32[8192]{0:T(1024)} %param.17) | copy-start | bytes 98308
  103.3 1.5 %copy-start.1 = (f32[8192]{0:T(1024)}, f32[8192]{0:T(1024)S(1)}, u32[]{:S(2)}) copy-start(f32[8192]{0:T(1024)S(1)} %multiply_bitcast_fusion) | copy-start | bytes 98308

commit v7 on v6

--- a/solution.py
+++ b/solution.py
@@ -197,19 +197,17 @@
     tiles = link_cost.reshape(NI, span // 128, 128).transpose(1, 0, 2).reshape(span // 128, NI * 128)
     wanted_tiles = tile_index.reshape(-1)
     rate = pick_rate(swap_rate[0], od_pair[0]) / 16.0
-    every_tile = lax.all_gather(tiles, "z", axis=0, tiled=True)
-    piece = every_tile.shape[1] // 3
-    every_tile = jnp.concatenate(
-        [
-            lax.all_gather(every_tile[:, c * piece : (c + 1) * piece], ("plane", "route"), axis=0, tiled=True)
-            for c in range(3)
-        ],
-        1,
-    )
+    zs = lax.axis_size("z")
+    plane = ("plane", "route")
+    blocks = [lax.all_gather(tiles, plane, axis=0, tiled=True)]
+    moved = [lax.ppermute(tiles, "z", [((j + d) % zs, j) for j in range(zs)]) for d in range(1, zs)]
+    blocks += [lax.all_gather(block, plane, axis=0, tiled=True) for block in moved]
+    every_tile = jnp.concatenate(blocks, 0)
     own = tiles.shape[0]
-    planes = lax.axis_size(("plane", "route"))
+    planes = lax.axis_size(plane)
     device = wanted_tiles // own
-    wanted_tiles = (device % planes) * (lax.axis_size("z") * own) + (device // planes) * own + wanted_tiles % own
+    shift = (device // planes - lax.axis_index("z")) % zs
+    wanted_tiles = shift * (planes * own) + (device % planes) * own + wanted_tiles % own
     fetched = every_tile[wanted_tiles]
     fetched = fetched.reshape(tile_index.shape[0], tile_index.shape[1], NI, 128)
     totals = jnp.einsum("ptil,ptlq->piq", fetched, incidence, preferred_element_type=jnp.float32)

time: 105 us -> 104 us (level)
  blocking collectives: 50.4 us -> 45.1 us
  starting transfers between devices: 5.53 us -> 9.4 us
    all_gather x4, blocking collectives: 43.2 us -> 37.9 us  [the longest x3 29 us: body(): lax.all_gather(block, plane, axis=0, tiled=True)]
    ppermute x0 -> x3, starting transfers between devices: none -> 3.86 us  [body(): lax.ppermute(tiles, 'z', [((j + d) % zs, j) for j in range(zs)])]
  transfers between devices with their start and end apart: 2 -> 5, of which waited for: 1 -> 1; matrix products, arithmetic and copies ran while one was open for 3% -> 5% of each run, Pallas kernels for 0% -> 0%
where the time goes in v7:
time: 104 us; the launch traced here: 103 us
  blocking collectives  45.1 us (43%)
  Pallas kernels  15.2 us (15%)
  matrix products  13.5 us (13%)
  starting transfers between devices  9.4 us (9%)
  local copies, waits for them, and re-layouts  8.78 us (8%)
  other arithmetic  5.42 us (5%)
  waiting for transfers between devices  4.96 us (5%)
  between operations  1.04 us (1%)
    all_gather x3, blocking collectives, body(): lax.all_gather(block, plane, axis=0, tiled=True)  29 us
    pallas_call x1, Pallas kernels, simulate(): pl.pallas_call(sim_kernel, out_shape=(jax.ShapeDtypeStruct((count, rows,...  15.2 us
    all_gather x1, blocking collectives, body(): blocks = [lax.all_gather(tiles, plane, axis=0, tiled=True)]  8.89 us
    all_gather x1, blocking collectives, body(): lax.all_gather(jnp.stack([path_flow, anchor.astype(jnp.float32)]), 'route...  7.19 us
    dot_general x1, matrix products, body(): jnp.dot(tile_pick, lane_pick, precision=lax.Precision.HIGHEST, preferred_...  6.68 us
    ppermute x1, starting transfers between devices, padded(): lax.ppermute(head, LINE, [((i + 1) % count, i) for i in range(count)])  5.53 us
    ppermute x1, waiting for transfers between devices, padded(): lax.ppermute(tail, LINE, [(i, (i + 1) % count) for i in range(count)])  4.95 us
    dot_general x1, matrix products, body(): jnp.einsum('ptil,ptlq->piq', fetched, incidence, preferred_element_type=j...  4.6 us
  transfers between devices with their start and end apart: 5, of which 1 were waited for; matrix products, arithmetic and copies ran while one was open for 5% of the time, Pallas kernels for 0%

profile of v7, /device:TPU:0, one launch (start us, length us, event | category | flops | bytes accessed | tf_op | source)
XLA Modules:
  0.0 103.4 jit_solution(14300440831476721510)
XLA Ops:
  0.6 0.8 convert_element_type.32
  1.4 0.8 pad_maximum_fusion.3
  2.2 7.2 %all_gather.15 = f32[2,32768]{1,0:T(2,128)S(1)} all-gather(f32[2,8192]{1,0:T(2,128)S(1)} %pad_maximum_fusion.3), channel_id=1, replica_groups=mesh['z'=4,'plane'=2,'route'=4] {'route'}, dimensions={1}, use_global_device_ids=true | all-gather | bytes 327680 | tf_op jit(solution)/shard_map/all_gather | solution.py:172
  9.4 0.2 fusion.112
  9.6 0.7 and_select_fusion
  10.3 0.7 convert_element_type.31
  11.1 0.1 add_select_fusion
  11.2 0.0 copy-start.4
  11.2 0.0 copy-start.5
  11.2 0.0 copy-start.9
  11.2 0.0 copy-start.3
  11.2 0.3 fusion.120
  11.5 6.7 %fusion = f32[24,128]{1,0:T(8,128)S(1)} fusion(s32[32768]{0:T(1024)S(1)} %add_select_fusion, f32[24,32768]{1,0:T(8,128)S(1)} %fusion.120), kind=kOutput, calls=%fused_computation.2 | convolution fusion | flops 1212153856 | bytes 3289088 | tf_op jit(solution)/shard_map/dot_general | solution.py:180
  18.3 0.3 concatenate.12
  18.6 5.5 %collective-permute-start.1 = (f32[10,2048]{1,0:T(8,128)S(1)}, f32[10,2048]{1,0:T(8,128)S(1)}, u32[]{:S(2)}, u32[]{:S(2)}) collective-permute-start(f32[10,2048]{1,0:T(8,128)S(1)} %get-tuple-element.25), channel_id=1, source_target_pairs={{1,0},{2,1},{3,2},{4,3},{5,4},{6,5},{7,6},{8,7},{9,8},{10,9},{11,1... | collective-permute-start | bytes 245768 | tf_op jit(solution)/shard_map/ppermute | solution.py:31
  24.1 0.1 copy.29
  24.2 0.1 rem.144
  24.3 0.1 copy.30
  24.4 0.1 div.86
  24.5 0.1 copy.28
  24.7 0.1 ne.177
  24.9 2.2 %fusion.4 = f32[8192]{0:T(1024)S(1)} fusion(f32[16,128]{1,0:T(8,128)S(1)} %bitcast.55, s32[8192]{0:T(1024)S(1)} %get-tuple-element.27, s32[8192]{0:T(1024)S(1)} %get-tuple-element.26), kind=kOutput, calls=%fused_computation.9 | convolution fusion | flops 204595200 | bytes 106496 | tf_op jit(solution)/shard_map/dot_general | solution.py:139
  27.1 5.0 %collective-permute-done = f32[10,2048]{1,0:T(8,128)S(1)} collective-permute-done((f32[10,2048]{1,0:T(8,128)S(1)}, f32[10,2048]{1,0:T(8,128)S(1)}, u32[]{:S(2)}, u32[]{:S(2)}) %collective-permute-start) | collective-permute-done | bytes 81952 | tf_op jit(solution)/shard_map/ppermute | solution.py:29
  32.2 0.3 reshape.287
  32.5 0.8 copy.23
  33.3 0.3 reshape.288
  33.7 0.8 copy.24
  34.5 15.2 %shard_map.139 = (f32[12,56,128]{2,1,0:T(8,128)}, f32[5,56,128]{2,1,0:T(8,128)}) custom-call(f32[5,56,128]{2,1,0:T(8,128)} %bitcast.39, f32[6,56,128]{2,1,0:T(8,128)} %bitcast.38), custom_call_target="tpu_custom_call" | custom-call | tf_op jit(solution)/shard_map/pallas_call | solution.py:96
  49.7 1.2 %copy.26 = f32[12,128,56]{2,1,0:T(8,128)S(1)} copy(f32[12,128,56]{1,2,0:T(8,128)} %bitcast.44) | data formatting | bytes 688128 | tf_op jit(solution)/shard_map/transpose | solution.py:45
  50.9 0.5 reshape.290
  51.5 0.1 collective-permute-start.4
  51.6 0.1 collective-permute-start.3
  51.7 3.7 %collective-permute-start.2 = (bf16[24,1536]{1,0:T(8,128)(2,1)S(1)}, bf16[24,1536]{1,0:T(8,128)(2,1)S(1)}, u32[]{:S(2)}, u32[]{:S(2)}) collective-permute-start(bf16[24,1536]{1,0:T(8,128)(2,1)S(1)} %copy_bitcast_fusion), channel_id=1, source_target_pairs={{8,0},{16,8},{24,16},{0,24},{9,1},{17,9},{25,17},{1,25},{10,2},{18... | collective-permute-start | bytes 221192 | tf_op jit(solution)/shard_map/ppermute | solution.py:203
  55.4 1.1 %copy.25 = f32[5,128,56]{2,1,0:T(8,128)S(1)} copy(f32[5,128,56]{1,2,0:T(8,128)} %bitcast.47) | data formatting | bytes 286720 | tf_op jit(solution)/shard_map/transpose | solution.py:45
  56.5 0.2 reshape.289
  56.7 0.6 slice.300
  57.3 8.9 %all_gather.16 = bf16[192,1536]{1,0:T(8,128)(2,1)S(1)} all-gather(bf16[24,1536]{1,0:T(8,128)(2,1)S(1)} %copy_bitcast_fusion), channel_id=1, replica_groups=mesh['z'=4,'plane'=2,'route'=4] {'plane','route'}, dimensions={0}, use_global_device_ids=true | all-gather | bytes 663552 | tf_op jit(solution)/shard_map/all_gather | solution.py:202
  66.2 10.1 %all_gather.19 = bf16[192,1536]{1,0:T(8,128)(2,1)S(1)} all-gather(bf16[24,1536]{1,0:T(8,128)(2,1)S(1)} %collective-permute-done.4), channel_id=1, replica_groups=mesh['z'=4,'plane'=2,'route'=4] {'plane','route'}, dimensions={0}, use_global_device_ids=true | all-gather | bytes 663552 | tf_op jit(solution)/shard_map/all_gather | solution.py:204
  76.3 8.9 %all_gather.18 = bf16[192,1536]{1,0:T(8,128)(2,1)S(1)} all-gather(bf16[24,1536]{1,0:T(8,128)(2,1)S(1)} %collective-permute-done.3), channel_id=1, replica_groups=mesh['z'=4,'plane'=2,'route'=4] {'plane','route'}, dimensions={0}, use_global_device_ids=true | all-gather | bytes 663552 | tf_op jit(solution)/shard_map/all_gather | solution.py:204
  85.2 10.1 %all_gather.17 = bf16[192,1536]{1,0:T(8,128)(2,1)S(1)} all-gather(bf16[24,1536]{1,0:T(8,128)(2,1)S(1)} %collective-permute-done.2), channel_id=1, replica_groups=mesh['z'=4,'plane'=2,'route'=4] {'plane','route'}, dimensions={0}, use_global_device_ids=true | all-gather | bytes 663552 | tf_op jit(solution)/shard_map/all_gather | solution.py:204
  95.3 0.2 pad_maximum_fusion
  95.5 1.3 %gather_fusion = bf16[256,1536]{1,0:T(8,128)(2,1)S(1)} fusion(bf16[768,1536]{1,0:T(8,128)(2,1)S(1)} %pad_maximum_fusion, s32[1024]{0:T(1024)S(1)} %pad_clamp_fusion), kind=kCustom, calls=%fused_computation | custom fusion | bytes 1573888 | tf_op jit(solution)/shard_map/gather | solution.py:211
  96.7 0.5 reshape.293
  97.3 4.6 %fusion.10 = f32[64,128]{1,0:T(8,128)S(1)} fusion(bf16[64,4,12,128]{3,2,1,0:T(8,128)(2,1)S(1)} %reshape.293, bf16[64,4,128,128]{3,2,1,0:T(8,128)(2,1)} %param.23, s32[64,128]{1,0:T(8,128)S(1)} %bitcast.48), kind=kOutput, calls=%fused_computation.16 | convolution fusion | flops 100950016 | bytes 9240576 | tf_op jit(solution)/shard_map/ptil,ptlq->piq/dot_general | solution.py:213
  101.9 0.0 copy-start.1
  101.9 0.3 multiply_multiply_fusion
  102.3 0.2 multiply_divide_fusion
  102.5 0.9 subtract_add_fusion
  (36 shorter events, 0.3 us)
Async XLA Ops:
  11.2 7.1 %copy-start.4 = (f32[4,3072]{1,0:T(4,128)S(1)}, f32[4,3072]{1,0:T(4,128)}, u32[]{:S(2)}) copy-start(f32[4,3072]{1,0:T(4,128)} %param.12) | copy-start | bytes 147460
  11.2 7.1 %copy-start.5 = (f32[2,3072]{1,0:T(2,128)S(1)}, f32[2,3072]{1,0:T(2,128)}, u32[]{:S(2)}) copy-start(f32[2,3072]{1,0:T(2,128)} %param.15) | copy-start | bytes 73732
  11.2 7.1 %copy-start.6 = (f32[3072]{0:T(1024)S(1)}, f32[3072]{0:T(1024)}, u32[]{:S(2)}) copy-start(f32[3072]{0:T(1024)} %param.13) | copy-start | bytes 36868
  11.2 12.9 %copy-start.8 = (s32[64,4]{0,1:T(4,128)S(1)}, s32[64,4]{0,1:T(4,128)}, u32[]{:S(2)}) copy-start(s32[64,4]{0,1:T(4,128)} %param.22) | copy-start | bytes 3076
  11.2 13.6 %copy-start.9 = (s32[1,2048]{1,0:T(1,128)S(1)}, s32[1,2048]{1,0:T(1,128)}, u32[]{:S(2)}) copy-start(s32[1,2048]{1,0:T(1,128)} %param.21) | copy-start | bytes 24580
  11.2 13.6 %copy-start.3 = (s32[1,8192]{1,0:T(1,128)S(1)}, s32[1,8192]{1,0:T(1,128)}, u32[]{:S(2)}) copy-start(s32[1,8192]{1,0:T(1,128)} %param.20) | copy-start | bytes 98308
  18.6 8.6 %collective-permute-start.1 = (f32[10,2048]{1,0:T(8,128)S(1)}, f32[10,2048]{1,0:T(8,128)S(1)}, u32[]{:S(2)}, u32[]{:S(2)}) collective-permute-start(f32[10,2048]{1,0:T(8,128)S(1)} %get-tuple-element.25), channel_id=1, source_target_pairs={{1,0},{2,1},{3,2},{4,3},{5,4},{6,5},{7,6},{8,7},{9,8},{10,9},{11,1... | collective-permute-start | bytes 245768 | tf_op jit(solution)/shard_map/ppermute | solution.py:31
  24.1 8.0 %collective-permute-start = (f32[10,2048]{1,0:T(8,128)S(1)}, f32[10,2048]{1,0:T(8,128)S(1)}, u32[]{:S(2)}, u32[]{:S(2)}) collective-permute-start(f32[10,2048]{1,0:T(8,128)S(1)} %get-tuple-element.24), channel_id=1, source_target_pairs={{0,1},{1,2},{2,3},{3,4},{4,5},{5,6},{6,7},{7,8},{8,9},{9,10},{10,1... | collective-permute-start | bytes 245768 | tf_op jit(solution)/shard_map/ppermute | solution.py:29
  27.1 24.4 %copy-start.7 = (f32[3072]{0:T(1024)S(1)}, f32[3072]{0:T(1024)}, u32[]{:S(2)}) copy-start(f32[3072]{0:T(1024)} %param.14) | copy-start | bytes 36868
  51.5 14.7 %collective-permute-start.4 = (bf16[24,1536]{1,0:T(8,128)(2,1)S(1)}, bf16[24,1536]{1,0:T(8,128)(2,1)S(1)}, u32[]{:S(2)}, u32[]{:S(2)}) collective-permute-start(bf16[24,1536]{1,0:T(8,128)(2,1)S(1)} %copy_bitcast_fusion), channel_id=1, source_target_pairs={{24,0},{0,8},{8,16},{16,24},{25,1},{1,9},{9,17},{17,25},{26,2},{2,... | collective-permute-start | bytes 221192 | tf_op jit(solution)/shard_map/ppermute | solution.py:203
  51.6 24.7 %collective-permute-start.3 = (bf16[24,1536]{1,0:T(8,128)(2,1)S(1)}, bf16[24,1536]{1,0:T(8,128)(2,1)S(1)}, u32[]{:S(2)}, u32[]{:S(2)}) collective-permute-start(bf16[24,1536]{1,0:T(8,128)(2,1)S(1)} %copy_bitcast_fusion), channel_id=1, source_target_pairs={{16,0},{24,8},{0,16},{8,24},{17,1},{25,9},{1,17},{9,25},{18,2},{26... | collective-permute-start | bytes 221192 | tf_op jit(solution)/shard_map/ppermute | solution.py:203
  51.7 33.6 %collective-permute-start.2 = (bf16[24,1536]{1,0:T(8,128)(2,1)S(1)}, bf16[24,1536]{1,0:T(8,128)(2,1)S(1)}, u32[]{:S(2)}, u32[]{:S(2)}) collective-permute-start(bf16[24,1536]{1,0:T(8,128)(2,1)S(1)} %copy_bitcast_fusion), channel_id=1, source_target_pairs={{8,0},{16,8},{24,16},{0,24},{9,1},{17,9},{25,17},{1,25},{10,2},{18... | collective-permute-start | bytes 221192 | tf_op jit(solution)/shard_map/ppermute | solution.py:203
  95.4 1.8 %copy-start.2 = (s32[8192]{0:T(1024)S(1)}, s32[8192]{0:T(1024)}, u32[]{:S(2)}) copy-start(s32[8192]{0:T(1024)} %param.19) | copy-start | bytes 98308
  97.3 5.0 %copy-start = (f32[8192]{0:T(1024)S(1)}, f32[8192]{0:T(1024)}, u32[]{:S(2)}) copy-start(f32[8192]{0:T(1024)} %param.17) | copy-start | bytes 98308
  101.9 1.5 %copy-start.1 = (f32[8192]{0:T(1024)}, f32[8192]{0:T(1024)S(1)}, u32[]{:S(2)}) copy-start(f32[8192]{0:T(1024)S(1)} %multiply_bitcast_fusion) | copy-start | bytes 98308

commit v8 on v7

--- a/solution.py
+++ b/solution.py
@@ -199,15 +199,26 @@
     rate = pick_rate(swap_rate[0], od_pair[0]) / 16.0
     zs = lax.axis_size("z")
     plane = ("plane", "route")
-    blocks = [lax.all_gather(tiles, plane, axis=0, tiled=True)]
-    moved = [lax.ppermute(tiles, "z", [((j + d) % zs, j) for j in range(zs)]) for d in range(1, zs)]
-    blocks += [lax.all_gather(block, plane, axis=0, tiled=True) for block in moved]
-    every_tile = jnp.concatenate(blocks, 0)
+    near = lax.all_gather(tiles, plane, axis=0, tiled=True)
+    moved = jnp.concatenate(
+        [lax.ppermute(tiles, "z", [((j + d) % zs, j) for j in range(zs)]) for d in range(1, zs)], 0
+    )
+    piece = moved.shape[1] // 2
+    far = jnp.concatenate(
+        [lax.all_gather(moved[:, c * piece : (c + 1) * piece], plane, axis=0, tiled=True) for c in range(2)],
+        1,
+    )
+    every_tile = jnp.concatenate([near, far], 0)
     own = tiles.shape[0]
     planes = lax.axis_size(plane)
     device = wanted_tiles // own
     shift = (device // planes - lax.axis_index("z")) % zs
-    wanted_tiles = shift * (planes * own) + (device % planes) * own + wanted_tiles % own
+    inside = (device % planes) * own + wanted_tiles % own
+    wanted_tiles = jnp.where(
+        shift == 0,
+        inside,
+        planes * own + (device % planes) * ((zs - 1) * own) + (shift - 1) * own + wanted_tiles % own,
+    )
     fetched = every_tile[wanted_tiles]
     fetched = fetched.reshape(tile_index.shape[0], tile_index.shape[1], NI, 128)
     totals = jnp.einsum("ptil,ptlq->piq", fetched, incidence, preferred_element_type=jnp.float32)

time: 104 us -> 93.5 us (0.90)
  blocking collectives: 45.1 us -> 36.4 us
  starting transfers between devices: 9.4 us -> 7.6 us
    all_gather x4 -> x3, blocking collectives: 37.9 us -> 29.2 us  [the longest x2 20.3 us: body(): lax.all_gather(moved[:, c * piece:(c + 1) * piece], plane, axis=0, tiled=...]
    ppermute x3, starting transfers between devices: 3.86 us -> 2.07 us  [body(): lax.ppermute(tiles, 'z', [((j + d) % zs, j) for j in range(zs)])]
where the time goes in v8:
time: 93.5 us; the launch traced here: 93 us
  blocking collectives  36.4 us (39%)
  Pallas kernels  15.2 us (16%)
  matrix products  13.5 us (14%)
  local copies, waits for them, and re-layouts  8.82 us (9%)
  starting transfers between devices  7.6 us (8%)
  other arithmetic  5.44 us (6%)
  waiting for transfers between devices  4.96 us (5%)
  between operations  1.08 us (1%)
    all_gather x2, blocking collectives, body(): lax.all_gather(moved[:, c * piece:(c + 1) * piece], plane, axis=0, tiled=...  20.3 us
    pallas_call x1, Pallas kernels, simulate(): pl.pallas_call(sim_kernel, out_shape=(jax.ShapeDtypeStruct((count, rows,...  15.2 us
    all_gather x1, blocking collectives, body(): near = lax.all_gather(tiles, plane, axis=0, tiled=True)  8.89 us
    all_gather x1, blocking collectives, body(): lax.all_gather(jnp.stack([path_flow, anchor.astype(jnp.float32)]), 'route...  7.19 us
    dot_general x1, matrix products, body(): jnp.dot(tile_pick, lane_pick, precision=lax.Precision.HIGHEST, preferred_...  6.68 us
    ppermute x1, starting transfers between devices, padded(): lax.ppermute(head, LINE, [((i + 1) % count, i) for i in range(count)])  5.53 us
    ppermute x1, waiting for transfers between devices, padded(): lax.ppermute(tail, LINE, [(i, (i + 1) % count) for i in range(count)])  4.95 us
    dot_general x1, matrix products, body(): jnp.einsum('ptil,ptlq->piq', fetched, incidence, preferred_element_type=j...  4.6 us
  transfers between devices with their start and end apart: 5, of which 1 were waited for; matrix products, arithmetic and copies ran while one was open for 5% of the time, Pallas kernels for 0%

profile of v8, /device:TPU:0, one launch (start us, length us, event | category | flops | bytes accessed | tf_op | source)
XLA Modules:
  0.0 93.0 jit_solution(15117068389117465424)
XLA Ops:
  0.6 0.8 convert_element_type.32
  1.4 0.8 pad_maximum_fusion.2
  2.2 7.2 %all_gather.12 = f32[2,32768]{1,0:T(2,128)S(1)} all-gather(f32[2,8192]{1,0:T(2,128)S(1)} %pad_maximum_fusion.2), channel_id=1, replica_groups=mesh['z'=4,'plane'=2,'route'=4] {'route'}, dimensions={1}, use_global_device_ids=true | all-gather | bytes 327680 | tf_op jit(solution)/shard_map/all_gather | solution.py:172
  9.4 0.2 fusion.108
  9.6 0.7 and_select_fusion
  10.3 0.7 convert_element_type.31
  11.1 0.1 add_select_fusion
  11.2 0.0 copy-start.4
  11.2 0.0 copy-start.5
  11.2 0.0 copy-start.6
  11.2 0.0 copy-start.8
  11.2 0.0 copy-start.3
  11.2 0.3 fusion.117
  11.5 6.7 %fusion = f32[24,128]{1,0:T(8,128)S(1)} fusion(s32[32768]{0:T(1024)S(1)} %add_select_fusion, f32[24,32768]{1,0:T(8,128)S(1)} %fusion.117), kind=kOutput, calls=%fused_computation.2 | convolution fusion | flops 1212153856 | bytes 3289088 | tf_op jit(solution)/shard_map/dot_general | solution.py:180
  18.3 0.3 concatenate.18
  18.6 5.5 %collective-permute-start.1 = (f32[10,2048]{1,0:T(8,128)S(1)}, f32[10,2048]{1,0:T(8,128)S(1)}, u32[]{:S(2)}, u32[]{:S(2)}) collective-permute-start(f32[10,2048]{1,0:T(8,128)S(1)} %get-tuple-element.27), channel_id=1, source_target_pairs={{1,0},{2,1},{3,2},{4,3},{5,4},{6,5},{7,6},{8,7},{9,8},{10,9},{11,1... | collective-permute-start | bytes 245768 | tf_op jit(solution)/shard_map/ppermute | solution.py:31
  24.1 0.1 copy.29
  24.2 0.1 rem.148
  24.3 0.1 copy.30
  24.4 0.1 div.86
  24.5 0.1 copy.28
  24.7 0.1 ne.183
  24.9 2.2 %fusion.4 = f32[8192]{0:T(1024)S(1)} fusion(f32[16,128]{1,0:T(8,128)S(1)} %bitcast.55, s32[8192]{0:T(1024)S(1)} %get-tuple-element.29, s32[8192]{0:T(1024)S(1)} %get-tuple-element.28), kind=kOutput, calls=%fused_computation.9 | convolution fusion | flops 204595200 | bytes 106496 | tf_op jit(solution)/shard_map/dot_general | solution.py:139
  27.1 5.0 %collective-permute-done = f32[10,2048]{1,0:T(8,128)S(1)} collective-permute-done((f32[10,2048]{1,0:T(8,128)S(1)}, f32[10,2048]{1,0:T(8,128)S(1)}, u32[]{:S(2)}, u32[]{:S(2)}) %collective-permute-start) | collective-permute-done | bytes 81952 | tf_op jit(solution)/shard_map/ppermute | solution.py:29
  32.2 0.3 reshape.305
  32.5 0.8 copy.23
  33.3 0.3 reshape.306
  33.7 0.8 copy.24
  34.5 15.2 %shard_map.139 = (f32[12,56,128]{2,1,0:T(8,128)}, f32[5,56,128]{2,1,0:T(8,128)}) custom-call(f32[5,56,128]{2,1,0:T(8,128)} %bitcast.39, f32[6,56,128]{2,1,0:T(8,128)} %bitcast.38), custom_call_target="tpu_custom_call" | custom-call | tf_op jit(solution)/shard_map/pallas_call | solution.py:96
  49.7 1.2 %copy.26 = f32[12,128,56]{2,1,0:T(8,128)S(1)} copy(f32[12,128,56]{1,2,0:T(8,128)} %bitcast.44) | data formatting | bytes 688128 | tf_op jit(solution)/shard_map/transpose | solution.py:45
  51.0 0.5 reshape.308
  51.5 0.1 collective-permute-start.2
  51.6 0.1 collective-permute-start.3
  51.7 1.9 %collective-permute-start.4 = (bf16[24,1536]{1,0:T(8,128)(2,1)S(1)}, bf16[24,1536]{1,0:T(8,128)(2,1)S(1)}, u32[]{:S(2)}, u32[]{:S(2)}) collective-permute-start(bf16[24,1536]{1,0:T(8,128)(2,1)S(1)} %copy_bitcast_fusion), channel_id=1, source_target_pairs={{24,0},{0,8},{8,16},{16,24},{25,1},{1,9},{9,17},{17,25},{26,2},{2,... | collective-permute-start | bytes 221192 | tf_op jit(solution)/shard_map/ppermute | solution.py:204
  53.6 1.1 %copy.25 = f32[5,128,56]{2,1,0:T(8,128)S(1)} copy(f32[5,128,56]{1,2,0:T(8,128)} %bitcast.47) | data formatting | bytes 286720 | tf_op jit(solution)/shard_map/transpose | solution.py:45
  54.7 0.2 reshape.307
  54.9 0.6 slice.308
  55.6 8.9 %all_gather.13 = bf16[192,1536]{1,0:T(8,128)(2,1)S(1)} all-gather(bf16[24,1536]{1,0:T(8,128)(2,1)S(1)} %copy_bitcast_fusion), channel_id=1, replica_groups=mesh['z'=4,'plane'=2,'route'=4] {'plane','route'}, dimensions={0}, use_global_device_ids=true | all-gather | bytes 663552 | tf_op jit(solution)/shard_map/all_gather | solution.py:202
  64.5 10.8 %all_gather.15 = bf16[576,768]{1,0:T(8,128)(2,1)S(1)} all-gather(bf16[72,768]{1,0:T(8,128)(2,1)S(1)} %get-tuple-element.25), channel_id=1, replica_groups=mesh['z'=4,'plane'=2,'route'=4] {'plane','route'}, dimensions={0}, use_global_device_ids=true | all-gather | bytes 995328 | tf_op jit(solution)/shard_map/all_gather | solution.py:208
  75.3 9.6 %all_gather.14 = bf16[576,768]{1,0:T(8,128)(2,1)S(1)} all-gather(bf16[72,768]{1,0:T(8,128)(2,1)S(1)} %get-tuple-element.24), channel_id=1, replica_groups=mesh['z'=4,'plane'=2,'route'=4] {'plane','route'}, dimensions={0}, use_global_device_ids=true | all-gather | bytes 995328 | tf_op jit(solution)/shard_map/all_gather | solution.py:208
  84.9 0.2 maximum_maximum_fusion
  85.1 1.3 %gather_fusion = bf16[256,1536]{1,0:T(8,128)(2,1)S(1)} fusion(bf16[768,1536]{1,0:T(8,128)(2,1)S(1)} %maximum_maximum_fusion, s32[1024]{0:T(1024)S(1)} %pad_clamp_fusion), kind=kCustom, calls=%fused_computation | custom fusion | bytes 1573888 | tf_op jit(solution)/shard_map/gather | solution.py:222
  86.3 0.5 reshape.311
  86.9 4.6 %fusion.10 = f32[64,128]{1,0:T(8,128)S(1)} fusion(bf16[64,4,12,128]{3,2,1,0:T(8,128)(2,1)S(1)} %reshape.311, bf16[64,4,128,128]{3,2,1,0:T(8,128)(2,1)} %param.23, s32[64,128]{1,0:T(8,128)S(1)} %bitcast.48), kind=kOutput, calls=%fused_computation.16 | convolution fusion | flops 100950016 | bytes 9240576 | tf_op jit(solution)/shard_map/ptil,ptlq->piq/dot_general | solution.py:224
  91.5 0.0 copy-start.1
  91.5 0.3 multiply_multiply_fusion
  91.9 0.2 multiply_divide_fusion
  92.1 0.9 %subtract_add_fusion = f32[8192]{0:T(1024)} fusion(f32[8192]{0:T(1024)S(1)} %copy-done, f32[8192]{0:T(1024)S(1)} %multiply_divide_fusion, pred[8192]{0:T(1024)(128)(4,1)S(1)} %get-tuple-element.21, f32[8192]{0:T(1024)S(1)} %get-tuple-element.7, pred[8192]{0:T(1024)(128)(4,1)S(1)} %get-tuple-element.20, pred[8192]{0:T(1024)(128)(4,1)S(1)} %get-tuple-element.19, ...), kind=kLoop, calls=%fused_computation.189 | loop fusion | flops 491520 | bytes 245760 | tf_op jit(solution)/shard_map/add | solution.py:148
  (39 shorter events, 0.4 us)
Async XLA Ops:
  11.2 7.1 %copy-start.4 = (f32[4,3072]{1,0:T(4,128)S(1)}, f32[4,3072]{1,0:T(4,128)}, u32[]{:S(2)}) copy-start(f32[4,3072]{1,0:T(4,128)} %param.12) | copy-start | bytes 147460
  11.2 7.1 %copy-start.5 = (f32[2,3072]{1,0:T(2,128)S(1)}, f32[2,3072]{1,0:T(2,128)}, u32[]{:S(2)}) copy-start(f32[2,3072]{1,0:T(2,128)} %param.15) | copy-start | bytes 73732
  11.2 7.1 %copy-start.6 = (f32[3072]{0:T(1024)S(1)}, f32[3072]{0:T(1024)}, u32[]{:S(2)}) copy-start(f32[3072]{0:T(1024)} %param.13) | copy-start | bytes 36868
  11.2 12.9 %copy-start.8 = (s32[64,4]{0,1:T(4,128)S(1)}, s32[64,4]{0,1:T(4,128)}, u32[]{:S(2)}) copy-start(s32[64,4]{0,1:T(4,128)} %param.22) | copy-start | bytes 3076
  11.2 13.6 %copy-start.9 = (s32[1,2048]{1,0:T(1,128)S(1)}, s32[1,2048]{1,0:T(1,128)}, u32[]{:S(2)}) copy-start(s32[1,2048]{1,0:T(1,128)} %param.21) | copy-start | bytes 24580
  11.2 13.6 %copy-start.3 = (s32[1,8192]{1,0:T(1,128)S(1)}, s32[1,8192]{1,0:T(1,128)}, u32[]{:S(2)}) copy-start(s32[1,8192]{1,0:T(1,128)} %param.20) | copy-start | bytes 98308
  18.6 8.6 %collective-permute-start.1 = (f32[10,2048]{1,0:T(8,128)S(1)}, f32[10,2048]{1,0:T(8,128)S(1)}, u32[]{:S(2)}, u32[]{:S(2)}) collective-permute-start(f32[10,2048]{1,0:T(8,128)S(1)} %get-tuple-element.27), channel_id=1, source_target_pairs={{1,0},{2,1},{3,2},{4,3},{5,4},{6,5},{7,6},{8,7},{9,8},{10,9},{11,1... | collective-permute-start | bytes 245768 | tf_op jit(solution)/shard_map/ppermute | solution.py:31
  24.1 8.0 %collective-permute-start = (f32[10,2048]{1,0:T(8,128)S(1)}, f32[10,2048]{1,0:T(8,128)S(1)}, u32[]{:S(2)}, u32[]{:S(2)}) collective-permute-start(f32[10,2048]{1,0:T(8,128)S(1)} %get-tuple-element.26), channel_id=1, source_target_pairs={{0,1},{1,2},{2,3},{3,4},{4,5},{5,6},{6,7},{7,8},{8,9},{9,10},{10,1... | collective-permute-start | bytes 245768 | tf_op jit(solution)/shard_map/ppermute | solution.py:29
  27.1 24.4 %copy-start.7 = (f32[3072]{0:T(1024)S(1)}, f32[3072]{0:T(1024)}, u32[]{:S(2)}) copy-start(f32[3072]{0:T(1024)} %param.14) | copy-start | bytes 36868
  51.5 12.9 %collective-permute-start.2 = (bf16[24,1536]{1,0:T(8,128)(2,1)S(1)}, bf16[24,1536]{1,0:T(8,128)(2,1)S(1)}, u32[]{:S(2)}, u32[]{:S(2)}) collective-permute-start(bf16[24,1536]{1,0:T(8,128)(2,1)S(1)} %copy_bitcast_fusion), channel_id=1, source_target_pairs={{8,0},{16,8},{24,16},{0,24},{9,1},{17,9},{25,17},{1,25},{10,2},{18... | collective-permute-start | bytes 221192 | tf_op jit(solution)/shard_map/ppermute | solution.py:204
  51.6 12.9 %collective-permute-start.3 = (bf16[24,1536]{1,0:T(8,128)(2,1)S(1)}, bf16[24,1536]{1,0:T(8,128)(2,1)S(1)}, u32[]{:S(2)}, u32[]{:S(2)}) collective-permute-start(bf16[24,1536]{1,0:T(8,128)(2,1)S(1)} %copy_bitcast_fusion), channel_id=1, source_target_pairs={{16,0},{24,8},{0,16},{8,24},{17,1},{25,9},{1,17},{9,25},{18,2},{26... | collective-permute-start | bytes 221192 | tf_op jit(solution)/shard_map/ppermute | solution.py:204
  51.7 12.8 %collective-permute-start.4 = (bf16[24,1536]{1,0:T(8,128)(2,1)S(1)}, bf16[24,1536]{1,0:T(8,128)(2,1)S(1)}, u32[]{:S(2)}, u32[]{:S(2)}) collective-permute-start(bf16[24,1536]{1,0:T(8,128)(2,1)S(1)} %copy_bitcast_fusion), channel_id=1, source_target_pairs={{24,0},{0,8},{8,16},{16,24},{25,1},{1,9},{9,17},{17,25},{26,2},{2,... | collective-permute-start | bytes 221192 | tf_op jit(solution)/shard_map/ppermute | solution.py:204
  85.1 1.8 %copy-start.2 = (s32[8192]{0:T(1024)S(1)}, s32[8192]{0:T(1024)}, u32[]{:S(2)}) copy-start(s32[8192]{0:T(1024)} %param.19) | copy-start | bytes 98308
  86.9 5.0 %copy-start = (f32[8192]{0:T(1024)S(1)}, f32[8192]{0:T(1024)}, u32[]{:S(2)}) copy-start(f32[8192]{0:T(1024)} %param.17) | copy-start | bytes 98308
  91.5 1.5 %copy-start.1 = (f32[8192]{0:T(1024)}, f32[8192]{0:T(1024)S(1)}, u32[]{:S(2)}) copy-start(f32[8192]{0:T(1024)S(1)} %multiply_bitcast_fusion) | copy-start | bytes 98308

commit v9 on v8

--- a/solution.py
+++ b/solution.py
@@ -45,9 +45,11 @@
     return jnp.swapaxes(cols, -1, -2).reshape(lead + (-1,))
 
 
-def sim_kernel(st0_ref, cons_ref, occ_ref, st_ref, w_ref, p_ref):
+def sim_kernel(st0_ref, cons_ref, occ_ref, st_ref, w_ref, p_ref, half_ref, inv_ref):
     rows = st0_ref.shape[1]
     st_ref[...] = st0_ref[...]
+    half_ref[...] = 2.0 * cons_ref[0]
+    inv_ref[...] = 1.0 / cons_ref[0]
     s0 = cons_ref[1]
     s1 = cons_ref[2]
     o0 = cons_ref[3]
@@ -58,11 +60,11 @@
 
     def step(j, acc):
         cap = cons_ref[0]
-        jam = 4.0 * cap
+        half_jam = half_ref[...]
         rho = [st_ref[c] for c in range(NC)]
         queue = st_ref[NC]
         send = [jnp.minimum(r, cap) for r in rho]
-        recv = [jnp.minimum(cap, 0.5 * (jam - r)) for r in rho]
+        recv = [jnp.minimum(cap, half_jam - 0.5 * r) for r in rho]
         inner = [jnp.minimum(send[c], recv[c + 1]) for c in range(NC - 1)]
         outflow = send[NC - 1]
         p_ref[BND : BND + rows] = outflow
@@ -80,7 +82,7 @@
         for c in range(NC):
             st_ref[c] = new[c]
         st_ref[NC] = queue
-        occ = ((((new[0] + new[1]) + new[2]) + new[3]) + queue) / cap
+        occ = ((((new[0] + new[1]) + new[2]) + new[3]) + queue) * inv_ref[...]
         return acc + occ
 
     def interval(i, carry):
@@ -102,6 +104,8 @@
         scratch_shapes=[
             pltpu.VMEM((2 * BND + 1, rows, 128), jnp.float32),
             pltpu.VMEM((rows + 2 * BND, 128), jnp.float32),
+            pltpu.VMEM((rows, 128), jnp.float32),
+            pltpu.VMEM((rows, 128), jnp.float32),
         ],
     )(st0, cons)
 

time: 93.5 us -> 93.1 us (level)
  no operation moved by 1% of the time
where the time goes in v9:
time: 93.1 us; the launch traced here: 92.6 us
  blocking collectives  36.4 us (39%)
  Pallas kernels  14.8 us (16%)
  matrix products  13.5 us (15%)
  local copies, waits for them, and re-layouts  8.82 us (9%)
  starting transfers between devices  7.6 us (8%)
  other arithmetic  5.44 us (6%)
  waiting for transfers between devices  4.96 us (5%)
  between operations  1.08 us (1%)
    all_gather x2, blocking collectives, body(): lax.all_gather(moved[:, c * piece:(c + 1) * piece], plane, axis=0, tiled=...  20.3 us
    pallas_call x1, Pallas kernels, simulate(): pl.pallas_call(sim_kernel, out_shape=(jax.ShapeDtypeStruct((count, rows,...  14.8 us
    all_gather x1, blocking collectives, body(): near = lax.all_gather(tiles, plane, axis=0, tiled=True)  8.89 us
    all_gather x1, blocking collectives, body(): lax.all_gather(jnp.stack([path_flow, anchor.astype(jnp.float32)]), 'route...  7.19 us
    dot_general x1, matrix products, body(): jnp.dot(tile_pick, lane_pick, precision=lax.Precision.HIGHEST, preferred_...  6.68 us
    ppermute x1, starting transfers between devices, padded(): lax.ppermute(head, LINE, [((i + 1) % count, i) for i in range(count)])  5.53 us
    ppermute x1, waiting for transfers between devices, padded(): lax.ppermute(tail, LINE, [(i, (i + 1) % count) for i in range(count)])  4.95 us
    dot_general x1, matrix products, body(): jnp.einsum('ptil,ptlq->piq', fetched, incidence, preferred_element_type=j...  4.6 us
  transfers between devices with their start and end apart: 5, of which 1 were waited for; matrix products, arithmetic and copies ran while one was open for 5% of the time, Pallas kernels for 0%

profile of v9, /device:TPU:0, one launch (start us, length us, event | category | flops | bytes accessed | tf_op | source)
XLA Modules:
  0.0 92.6 jit_solution(18394725735021881146)
XLA Ops:
  0.6 0.8 convert_element_type.32
  1.4 0.8 pad_maximum_fusion.2
  2.2 7.2 %all_gather.12 = f32[2,32768]{1,0:T(2,128)S(1)} all-gather(f32[2,8192]{1,0:T(2,128)S(1)} %pad_maximum_fusion.2), channel_id=1, replica_groups=mesh['z'=4,'plane'=2,'route'=4] {'route'}, dimensions={1}, use_global_device_ids=true | all-gather | bytes 327680 | tf_op jit(solution)/shard_map/all_gather | solution.py:176
  9.4 0.2 fusion.108
  9.6 0.7 and_select_fusion
  10.3 0.7 convert_element_type.31
  11.1 0.1 add_select_fusion
  11.2 0.0 copy-start.4
  11.2 0.0 copy-start.5
  11.2 0.0 copy-start.6
  11.2 0.0 copy-start.8
  11.2 0.3 fusion.117
  11.5 6.7 %fusion = f32[24,128]{1,0:T(8,128)S(1)} fusion(s32[32768]{0:T(1024)S(1)} %add_select_fusion, f32[24,32768]{1,0:T(8,128)S(1)} %fusion.117), kind=kOutput, calls=%fused_computation.2 | convolution fusion | flops 1212153856 | bytes 3289088 | tf_op jit(solution)/shard_map/dot_general | solution.py:184
  18.3 0.3 concatenate.18
  18.6 5.5 %collective-permute-start.1 = (f32[10,2048]{1,0:T(8,128)S(1)}, f32[10,2048]{1,0:T(8,128)S(1)}, u32[]{:S(2)}, u32[]{:S(2)}) collective-permute-start(f32[10,2048]{1,0:T(8,128)S(1)} %get-tuple-element.27), channel_id=1, source_target_pairs={{1,0},{2,1},{3,2},{4,3},{5,4},{6,5},{7,6},{8,7},{9,8},{10,9},{11,1... | collective-permute-start | bytes 245768 | tf_op jit(solution)/shard_map/ppermute | solution.py:31
  24.1 0.1 copy.29
  24.2 0.1 rem.148
  24.3 0.1 copy.30
  24.4 0.1 div.86
  24.5 0.1 copy.28
  24.7 0.1 ne.183
  24.9 2.2 %fusion.4 = f32[8192]{0:T(1024)S(1)} fusion(f32[16,128]{1,0:T(8,128)S(1)} %bitcast.55, s32[8192]{0:T(1024)S(1)} %get-tuple-element.29, s32[8192]{0:T(1024)S(1)} %get-tuple-element.28), kind=kOutput, calls=%fused_computation.9 | convolution fusion | flops 204595200 | bytes 106496 | tf_op jit(solution)/shard_map/dot_general | solution.py:143
  27.1 5.0 %collective-permute-done = f32[10,2048]{1,0:T(8,128)S(1)} collective-permute-done((f32[10,2048]{1,0:T(8,128)S(1)}, f32[10,2048]{1,0:T(8,128)S(1)}, u32[]{:S(2)}, u32[]{:S(2)}) %collective-permute-start) | collective-permute-done | bytes 81952 | tf_op jit(solution)/shard_map/ppermute | solution.py:29
  32.2 0.3 reshape.305
  32.5 0.8 copy.23
  33.3 0.3 reshape.306
  33.7 0.8 copy.24
  34.5 14.8 %shard_map.139 = (f32[12,56,128]{2,1,0:T(8,128)}, f32[5,56,128]{2,1,0:T(8,128)}) custom-call(f32[5,56,128]{2,1,0:T(8,128)} %bitcast.39, f32[6,56,128]{2,1,0:T(8,128)} %bitcast.38), custom_call_target="tpu_custom_call" | custom-call | tf_op jit(solution)/shard_map/pallas_call | solution.py:98
  49.3 1.2 %copy.26 = f32[12,128,56]{2,1,0:T(8,128)S(1)} copy(f32[12,128,56]{1,2,0:T(8,128)} %bitcast.44) | data formatting | bytes 688128 | tf_op jit(solution)/shard_map/transpose | solution.py:45
  50.6 0.5 reshape.308
  51.2 0.1 collective-permute-start.2
  51.2 0.1 collective-permute-start.3
  51.3 1.9 %collective-permute-start.4 = (bf16[24,1536]{1,0:T(8,128)(2,1)S(1)}, bf16[24,1536]{1,0:T(8,128)(2,1)S(1)}, u32[]{:S(2)}, u32[]{:S(2)}) collective-permute-start(bf16[24,1536]{1,0:T(8,128)(2,1)S(1)} %copy_bitcast_fusion), channel_id=1, source_target_pairs={{24,0},{0,8},{8,16},{16,24},{25,1},{1,9},{9,17},{17,25},{26,2},{2,... | collective-permute-start | bytes 221192 | tf_op jit(solution)/shard_map/ppermute | solution.py:208
  53.2 1.1 %copy.25 = f32[5,128,56]{2,1,0:T(8,128)S(1)} copy(f32[5,128,56]{1,2,0:T(8,128)} %bitcast.47) | data formatting | bytes 286720 | tf_op jit(solution)/shard_map/transpose | solution.py:45
  54.3 0.2 reshape.307
  54.6 0.6 slice.308
  55.2 8.9 %all_gather.13 = bf16[192,1536]{1,0:T(8,128)(2,1)S(1)} all-gather(bf16[24,1536]{1,0:T(8,128)(2,1)S(1)} %copy_bitcast_fusion), channel_id=1, replica_groups=mesh['z'=4,'plane'=2,'route'=4] {'plane','route'}, dimensions={0}, use_global_device_ids=true | all-gather | bytes 663552 | tf_op jit(solution)/shard_map/all_gather | solution.py:206
  64.2 10.8 %all_gather.15 = bf16[576,768]{1,0:T(8,128)(2,1)S(1)} all-gather(bf16[72,768]{1,0:T(8,128)(2,1)S(1)} %get-tuple-element.25), channel_id=1, replica_groups=mesh['z'=4,'plane'=2,'route'=4] {'plane','route'}, dimensions={0}, use_global_device_ids=true | all-gather | bytes 995328 | tf_op jit(solution)/shard_map/all_gather | solution.py:212
  74.9 9.6 %all_gather.14 = bf16[576,768]{1,0:T(8,128)(2,1)S(1)} all-gather(bf16[72,768]{1,0:T(8,128)(2,1)S(1)} %get-tuple-element.24), channel_id=1, replica_groups=mesh['z'=4,'plane'=2,'route'=4] {'plane','route'}, dimensions={0}, use_global_device_ids=true | all-gather | bytes 995328 | tf_op jit(solution)/shard_map/all_gather | solution.py:212
  84.5 0.2 maximum_maximum_fusion
  84.7 0.0 copy-start.2
  84.7 1.3 %gather_fusion = bf16[256,1536]{1,0:T(8,128)(2,1)S(1)} fusion(bf16[768,1536]{1,0:T(8,128)(2,1)S(1)} %maximum_maximum_fusion, s32[1024]{0:T(1024)S(1)} %pad_clamp_fusion), kind=kCustom, calls=%fused_computation | custom fusion | bytes 1573888 | tf_op jit(solution)/shard_map/gather | solution.py:226
  86.0 0.5 reshape.311
  86.5 4.6 %fusion.10 = f32[64,128]{1,0:T(8,128)S(1)} fusion(bf16[64,4,12,128]{3,2,1,0:T(8,128)(2,1)S(1)} %reshape.311, bf16[64,4,128,128]{3,2,1,0:T(8,128)(2,1)} %param.23, s32[64,128]{1,0:T(8,128)S(1)} %bitcast.48), kind=kOutput, calls=%fused_computation.16 | convolution fusion | flops 100950016 | bytes 9240576 | tf_op jit(solution)/shard_map/ptil,ptlq->piq/dot_general | solution.py:228
  91.2 0.0 copy-start.1
  91.2 0.3 multiply_multiply_fusion
  91.5 0.2 multiply_divide_fusion
  91.7 0.9 %subtract_add_fusion = f32[8192]{0:T(1024)} fusion(f32[8192]{0:T(1024)S(1)} %copy-done, f32[8192]{0:T(1024)S(1)} %multiply_divide_fusion, pred[8192]{0:T(1024)(128)(4,1)S(1)} %get-tuple-element.21, f32[8192]{0:T(1024)S(1)} %get-tuple-element.7, pred[8192]{0:T(1024)(128)(4,1)S(1)} %get-tuple-element.20, pred[8192]{0:T(1024)(128)(4,1)S(1)} %get-tuple-element.19, ...), kind=kLoop, calls=%fused_computation.189 | loop fusion | flops 491520 | bytes 245760 | tf_op jit(solution)/shard_map/add | solution.py:152
  (39 shorter events, 0.4 us)
Async XLA Ops:
  11.2 7.1 %copy-start.4 = (f32[4,3072]{1,0:T(4,128)S(1)}, f32[4,3072]{1,0:T(4,128)}, u32[]{:S(2)}) copy-start(f32[4,3072]{1,0:T(4,128)} %param.12) | copy-start | bytes 147460
  11.2 7.1 %copy-start.5 = (f32[2,3072]{1,0:T(2,128)S(1)}, f32[2,3072]{1,0:T(2,128)}, u32[]{:S(2)}) copy-start(f32[2,3072]{1,0:T(2,128)} %param.15) | copy-start | bytes 73732
  11.2 7.1 %copy-start.6 = (f32[3072]{0:T(1024)S(1)}, f32[3072]{0:T(1024)}, u32[]{:S(2)}) copy-start(f32[3072]{0:T(1024)} %param.13) | copy-start | bytes 36868
  11.2 12.9 %copy-start.8 = (s32[64,4]{0,1:T(4,128)S(1)}, s32[64,4]{0,1:T(4,128)}, u32[]{:S(2)}) copy-start(s32[64,4]{0,1:T(4,128)} %param.22) | copy-start | bytes 3076
  11.2 13.6 %copy-start.9 = (s32[1,2048]{1,0:T(1,128)S(1)}, s32[1,2048]{1,0:T(1,128)}, u32[]{:S(2)}) copy-start(s32[1,2048]{1,0:T(1,128)} %param.21) | copy-start | bytes 24580
  11.2 13.6 %copy-start.3 = (s32[1,8192]{1,0:T(1,128)S(1)}, s32[1,8192]{1,0:T(1,128)}, u32[]{:S(2)}) copy-start(s32[1,8192]{1,0:T(1,128)} %param.20) | copy-start | bytes 98308
  18.6 8.6 %collective-permute-start.1 = (f32[10,2048]{1,0:T(8,128)S(1)}, f32[10,2048]{1,0:T(8,128)S(1)}, u32[]{:S(2)}, u32[]{:S(2)}) collective-permute-start(f32[10,2048]{1,0:T(8,128)S(1)} %get-tuple-element.27), channel_id=1, source_target_pairs={{1,0},{2,1},{3,2},{4,3},{5,4},{6,5},{7,6},{8,7},{9,8},{10,9},{11,1... | collective-permute-start | bytes 245768 | tf_op jit(solution)/shard_map/ppermute | solution.py:31
  24.1 8.0 %collective-permute-start = (f32[10,2048]{1,0:T(8,128)S(1)}, f32[10,2048]{1,0:T(8,128)S(1)}, u32[]{:S(2)}, u32[]{:S(2)}) collective-permute-start(f32[10,2048]{1,0:T(8,128)S(1)} %get-tuple-element.26), channel_id=1, source_target_pairs={{0,1},{1,2},{2,3},{3,4},{4,5},{5,6},{6,7},{7,8},{8,9},{9,10},{10,1... | collective-permute-start | bytes 245768 | tf_op jit(solution)/shard_map/ppermute | solution.py:29
  27.1 24.0 %copy-start.7 = (f32[3072]{0:T(1024)S(1)}, f32[3072]{0:T(1024)}, u32[]{:S(2)}) copy-start(f32[3072]{0:T(1024)} %param.14) | copy-start | bytes 36868
  51.2 12.9 %collective-permute-start.2 = (bf16[24,1536]{1,0:T(8,128)(2,1)S(1)}, bf16[24,1536]{1,0:T(8,128)(2,1)S(1)}, u32[]{:S(2)}, u32[]{:S(2)}) collective-permute-start(bf16[24,1536]{1,0:T(8,128)(2,1)S(1)} %copy_bitcast_fusion), channel_id=1, source_target_pairs={{8,0},{16,8},{24,16},{0,24},{9,1},{17,9},{25,17},{1,25},{10,2},{18... | collective-permute-start | bytes 221192 | tf_op jit(solution)/shard_map/ppermute | solution.py:208
  51.2 12.9 %collective-permute-start.3 = (bf16[24,1536]{1,0:T(8,128)(2,1)S(1)}, bf16[24,1536]{1,0:T(8,128)(2,1)S(1)}, u32[]{:S(2)}, u32[]{:S(2)}) collective-permute-start(bf16[24,1536]{1,0:T(8,128)(2,1)S(1)} %copy_bitcast_fusion), channel_id=1, source_target_pairs={{16,0},{24,8},{0,16},{8,24},{17,1},{25,9},{1,17},{9,25},{18,2},{26... | collective-permute-start | bytes 221192 | tf_op jit(solution)/shard_map/ppermute | solution.py:208
  51.3 12.8 %collective-permute-start.4 = (bf16[24,1536]{1,0:T(8,128)(2,1)S(1)}, bf16[24,1536]{1,0:T(8,128)(2,1)S(1)}, u32[]{:S(2)}, u32[]{:S(2)}) collective-permute-start(bf16[24,1536]{1,0:T(8,128)(2,1)S(1)} %copy_bitcast_fusion), channel_id=1, source_target_pairs={{24,0},{0,8},{8,16},{16,24},{25,1},{1,9},{9,17},{17,25},{26,2},{2,... | collective-permute-start | bytes 221192 | tf_op jit(solution)/shard_map/ppermute | solution.py:208
  84.7 1.8 %copy-start.2 = (s32[8192]{0:T(1024)S(1)}, s32[8192]{0:T(1024)}, u32[]{:S(2)}) copy-start(s32[8192]{0:T(1024)} %param.19) | copy-start | bytes 98308
  86.5 5.0 %copy-start = (f32[8192]{0:T(1024)S(1)}, f32[8192]{0:T(1024)}, u32[]{:S(2)}) copy-start(f32[8192]{0:T(1024)} %param.17) | copy-start | bytes 98308
  91.2 1.5 %copy-start.1 = (f32[8192]{0:T(1024)}, f32[8192]{0:T(1024)S(1)}, u32[]{:S(2)}) copy-start(f32[8192]{0:T(1024)S(1)} %multiply_bitcast_fusion) | copy-start | bytes 98308
